TPU v7x, 768 devices: a whole 4x8x12 slice. The times are simulated.
768 devices in a mesh: occ: 128 (over x, z_lo, y), aux: 6 (over z_hi, core).
Axes of the slice: x: 4, y: 8, z: 12 (z_hi: 3, z_lo: 4; z = z_hi * 4 + z_lo), core: 2. Of those that a mesh axis runs over, the one named last changes fastest.
Arguments:
- b_rows: bfloat16 [12288, 16384], P('aux', 'occ'), may hold values from -0.5 to 0.5
- b_cols: bfloat16 [12288, 65536], P('aux', 'occ'), may hold values from -0.5 to 0.5
- eps_occ: float32 [256], replicated, may hold values from -1.5 to -0.3
- eps_va: float32 [64], replicated, may hold values from 0.2 to 2
- eps_vb: float32 [256], replicated, may hold values from 0.2 to 2
Outputs:
- gamma: float32 [12288, 16384], P('aux', 'occ')
All inputs are finite; a program needn't handle non-finite values.
Results may differ from a plain program's by a relative error of at most 0.0027.
Values may be sent and summed in bfloat16 or wider, within the bound.
No kernel may reach another device: no remote copies, remote signals or barrier semaphores. Data moves between devices by JAX's collectives and lax.ppermute only.
A program may use at most 32 MiB of HBM per device.

v0:
```python
import jax
import jax.numpy as jnp
from jax import lax
from jax.sharding import PartitionSpec as P

spin_scale = 1.3


def passed_along(value, axis, by):
    size = lax.axis_size(axis)
    return lax.ppermute(value, axis, [(i, (i + by) % size) for i in range(size)])


def partial_integrals(left_block, right_block):
    return lax.dot_general(
        left_block, right_block, (((0,), (0,)), ((), ())), preferred_element_type=jnp.float32
    )


def amplitudes(summed, row_energy, col_energy):
    return (spin_scale * summed / (row_energy[:, None] + col_energy[None, :])).astype(jnp.bfloat16)


def contribution(right_block, amplitude):
    return lax.dot_general(
        right_block, amplitude, (((1,), (1,)), ((), ())), preferred_element_type=jnp.float32
    )


def per_device(b_rows, b_cols, eps_occ, eps_va, eps_vb):
    per_block = b_rows.shape[1] // eps_va.shape[0]
    cycle_size = lax.axis_size("occ")
    position = lax.axis_index("occ")

    def energy(offset, virt_energy):
        which = (position + offset) % cycle_size
        occ_energy = lax.dynamic_slice_in_dim(eps_occ, which * per_block, per_block)
        return (virt_energy[None, :] - occ_energy[:, None]).reshape(-1)

    right_list = [b_cols]
    moving = b_cols
    for hop_index in range(2):
        moving = passed_along(moving, "occ", 1)
        right_list.append(moving)
    left_list = [b_rows, b_rows, b_rows]
    own_rows = energy(0, eps_va)
    row_list = [own_rows, own_rows, own_rows]
    col_list = [energy(0, eps_vb), energy(-1, eps_vb), energy(-2, eps_vb)]
    partials = []
    for index in range(3):
        partials.append(partial_integrals(left_list[index], right_list[index]))
    summed_list = []
    for index in range(3):
        summed_list.append(lax.psum(partials[index], "aux"))
    pieces = []
    for index in range(3):
        amplitude = amplitudes(summed_list[index], row_list[index], col_list[index])
        pieces.append(contribution(right_list[index], amplitude))
    gamma = pieces[0] + pieces[1] + pieces[2]
    return gamma


def solution(mesh):
    return jax.shard_map(
        per_device,
        mesh=mesh,
        in_specs=(P("aux", "occ"), P("aux", "occ"), P(), P(), P()),
        out_specs=P("aux", "occ"),
        check_vma=False,
    )
```

profile of v0, /device:TPU:1, one launch (start us, length us, event | category | flops | bytes accessed | tf_op | source)
XLA Modules:
  0.0 220.6 jit_solution(12508030139969332789)
XLA Ops:
  6.5 0.0 copy-start
  6.5 0.0 all-reduce.3.cloned.1.call-start
  6.5 4.1 %collective-permute-start = (bf16[2048,512]{1,0:T(8,128)(2,1)}, bf16[2048,512]{1,0:T(8,128)(2,1)S(1)}, u32[]{:S(2)}, u32[]{:S(2)}) collective-permute-start(bf16[2048,512]{1,0:T(8,128)(2,1)} %param.6), channel_id=1, source_target_pairs={{0,6},{6,12},{12,18},{18,24},{24,30},{30,36},{36,42},{42,48},{48,5... | collective-permute-start | bytes 6291464 | tf_op jit(solution)/shard_map/ppermute | solution.py:11
  10.7 49.1 %collective-permute-done = bf16[2048,512]{1,0:T(8,128)(2,1)S(1)} collective-permute-done((bf16[2048,512]{1,0:T(8,128)(2,1)}, bf16[2048,512]{1,0:T(8,128)(2,1)S(1)}, u32[]{:S(2)}, u32[]{:S(2)}) %collective-permute-start) | collective-permute-done | bytes 2097184 | tf_op jit(solution)/shard_map/ppermute | solution.py:11
  59.8 0.0 copy-start.2
  59.8 1.9 collective-permute-start.1
  61.7 0.0 copy-done
  61.7 2.8 %fusion.15 = f32[128,512]{1,0:T(8,128)} fusion(bf16[2048,128]{1,0:T(8,128)(2,1)S(1)} %copy-done, bf16[2048,512]{1,0:T(8,128)(2,1)} %param.6), kind=kOutput, calls=%fused_computation.24 | convolution fusion | flops 268435456 | bytes 2883584 | tf_op jit(solution)/shard_map/dot_general | solution.py:15
  64.5 1.2 fusion.16
  65.7 0.0 copy-done.2
  65.7 0.0 copy-start.8
  65.7 0.0 copy-start.10
  65.7 0.0 copy-start.9
  65.7 0.0 copy-start.1
  65.7 42.0 %collective-permute-done.1 = bf16[2048,512]{1,0:T(8,128)(2,1)S(1)} collective-permute-done((bf16[2048,512]{1,0:T(8,128)(2,1)S(1)}, bf16[2048,512]{1,0:T(8,128)(2,1)S(1)}, u32[]{:S(2)}, u32[]{:S(2)}) %collective-permute-start.1) | collective-permute-done | bytes 2097184 | tf_op jit(solution)/shard_map/ppermute | solution.py:11
  107.7 0.0 copy-start.4
  107.7 1.3 copy-done.4
  109.0 1.2 fusion.17
  110.2 0.0 all-reduce.3.cloned.1.call-update
  110.3 0.0 copy-done.8
  110.3 0.1 fusion.14
  110.4 0.0 copy-done.10
  110.4 0.1 broadcast_subtract_fusion
  110.5 0.1 sub.79
  110.6 0.0 copy-done.9
  110.6 0.1 subtract_bitcast_fusion
  110.7 97.4 %all-reduce.3.cloned.1.call-done = (f32[128,512]{1,0:T(8,128)}, f32[128,512]{1,0:T(8,128)}, f32[128,512]{1,0:T(8,128)}) async-done(((f32[128,512]{1,0:T(8,128)}, f32[128,512]{1,0:T(8,128)}, f32[128,512]{1,0:T(8,128)}), (f32[128,512]{1,0:T(8,128)}, f32[128,512]{1,0:T(8,128)}, f32[128,512]{1,0:T(8,128)})) %all-reduce.3.cloned.1.call-update) | async-done | bytes 786448 | tf_op jit(solution)/shard_map/psum | solution.py:54
  208.0 0.0 copy-start.3
  208.0 0.0 copy-start.7
  208.0 0.0 copy-done.1
  208.0 1.9 fusion.1
  210.0 0.0 copy-done.3
  210.0 0.0 copy-done.7
  210.0 0.0 copy-start.5
  210.0 0.0 copy-start.6
  210.0 0.8 convolution_add_fusion.1
  210.8 0.7 copy-done.5
  211.6 0.0 copy-done.6
  211.6 0.8 fusion
  212.4 1.3 copy.6
  (3 shorter events, 0.0 us)
Async XLA Ops:
  6.5 55.2 %copy-start = (bf16[2048,128]{1,0:T(8,128)(2,1)S(1)}, bf16[2048,128]{1,0:T(8,128)(2,1)}, u32[]{:S(2)}) copy-start(bf16[2048,128]{1,0:T(8,128)(2,1)} %param.5) | copy-start | bytes 1572868
  6.5 201.5 %all-reduce.3.cloned.1.call-start = ((), (), s32[]{:S(2)}) async-start(), calls=%async_computation | async-start | bytes 1572864 | tf_op jit(solution)/shard_map/psum | solution.py:54
  6.5 53.3 %collective-permute-start = (bf16[2048,512]{1,0:T(8,128)(2,1)}, bf16[2048,512]{1,0:T(8,128)(2,1)S(1)}, u32[]{:S(2)}, u32[]{:S(2)}) collective-permute-start(bf16[2048,512]{1,0:T(8,128)(2,1)} %param.6), channel_id=1, source_target_pairs={{0,6},{6,12},{12,18},{18,24},{24,30},{30,36},{36,42},{42,48},{48,5... | collective-permute-start | bytes 6291464 | tf_op jit(solution)/shard_map/ppermute | solution.py:11
  59.8 5.9 %copy-start.2 = (bf16[2048,512]{1,0:T(8,128)(2,1)}, bf16[2048,512]{1,0:T(8,128)(2,1)S(1)}, u32[]{:S(2)}) copy-start(bf16[2048,512]{1,0:T(8,128)(2,1)S(1)} %collective-permute-done) | copy-start | bytes 6291460
  59.8 47.9 %collective-permute-start.1 = (bf16[2048,512]{1,0:T(8,128)(2,1)S(1)}, bf16[2048,512]{1,0:T(8,128)(2,1)S(1)}, u32[]{:S(2)}, u32[]{:S(2)}) collective-permute-start(bf16[2048,512]{1,0:T(8,128)(2,1)S(1)} %collective-permute-done), channel_id=1, source_target_pairs={{0,6},{6,12},{12,18},{18,24},{24,30},{30,36},{36,42},{42,48},{48,5... | collective-permute-start | bytes 6291464 | tf_op jit(solution)/shard_map/ppermute | solution.py:11
  65.7 44.6 %copy-start.8 = (f32[256]{0:T(256)S(1)}, f32[256]{0:T(256)}, u32[]{:S(2)}) copy-start(f32[256]{0:T(256)} %param.7) | copy-start | bytes 3076
  65.7 44.7 %copy-start.10 = (f32[64]{0:T(128)S(1)}, f32[64]{0:T(128)}, u32[]{:S(2)}) copy-start(f32[64]{0:T(128)} %param.8) | copy-start | bytes 772
  65.7 44.9 %copy-start.9 = (f32[256]{0:T(256)S(1)}, f32[256]{0:T(256)}, u32[]{:S(2)}) copy-start(f32[256]{0:T(256)} %param.9) | copy-start | bytes 3076
  65.7 142.3 %copy-start.1 = (bf16[2048,512]{1,0:T(8,128)(2,1)S(1)}, bf16[2048,512]{1,0:T(8,128)(2,1)}, u32[]{:S(2)}) copy-start(bf16[2048,512]{1,0:T(8,128)(2,1)} %param.6) | copy-start | bytes 6291460
  107.7 1.3 copy-start.4
  208.0 1.9 copy-start.3
  208.0 1.9 copy-start.7
  210.0 1.6 copy-start.5
  210.0 1.6 copy-start.6
Sparse Core Ops, SparseCore 0:
  110.4 97.5 all-reduce.2
where the time goes:
time: 221 us
  waiting for transfers between devices  189 us (86%)
  between operations  13.6 us (6%)
  matrix products  8.72 us (4%)
  starting transfers between devices  6.06 us (3%)
  local copies, waits for them, and re-layouts  3.58 us (2%)
    psum x1, waiting for transfers between devices, per_device(): summed_list.append(lax.psum(partials[index], 'aux'))  97.4 us
    ppermute x2, waiting for transfers between devices, passed_along(): lax.ppermute(value, axis, [(i, (i + by) % size) for i in range(size)])  91.1 us
    ppermute x2, starting transfers between devices, passed_along(): lax.ppermute(value, axis, [(i, (i + by) % size) for i in range(size)])  6.05 us
    dot_general x3, matrix products, partial_integrals(): lax.dot_general(left_block, right_block, (((0,), (0,)), ((), ())), prefer...  5.15 us
  transfers between devices with their start and end apart: 3, of which 3 were waited for; matrix products, arithmetic and copies ran while one was open for 2% of the time, Pallas kernels for 0%

commit v1 on v0

v1 whole, which is shorter than its diff:
```python
import jax
import jax.numpy as jnp
from jax import lax
from jax.sharding import PartitionSpec as P

spin_scale = 1.3


def shifted(value, axis, by):
    size = lax.axis_size(axis)
    return lax.ppermute(value, axis, [(i, (i + by) % size) for i in range(size)])


def aux_pairs(size, step_core, step_chip):
    pairs = []
    for i in range(size):
        chip, core = divmod(i, 2)
        chips = size // 2
        pairs.append((i, ((chip + step_chip) % chips) * 2 + (core + step_core) % 2))
    return pairs


def partial_integrals(left_block, right_block):
    return lax.dot_general(
        left_block, right_block, (((0,), (0,)), ((), ())), preferred_element_type=jnp.float32
    )


def contribution(right_block, amplitude):
    return lax.dot_general(
        right_block, amplitude, (((1,), (1,)), ((), ())), preferred_element_type=jnp.float32
    )


def per_device(b_rows, b_cols, eps_occ, eps_va, eps_vb):
    per_block = b_rows.shape[1] // eps_va.shape[0]
    cycle_size = lax.axis_size("occ")
    position = lax.axis_index("occ")
    aux_size = lax.axis_size("aux")
    aux_pos = lax.axis_index("aux")
    core = aux_pos % 2
    chips = aux_size // 2
    rows = b_rows.shape[1]
    half = rows // 2

    def energy(offset, virt_energy):
        which = (position + offset) % cycle_size
        occ_energy = lax.dynamic_slice_in_dim(eps_occ, which * per_block, per_block)
        return (virt_energy[None, :] - occ_energy[:, None]).reshape(-1)

    col_energy = energy(0, eps_vb)

    def amplitude(partial, shift):
        give = lax.dynamic_slice_in_dim(partial, (1 - core) * half, half, 0)
        keep = lax.dynamic_slice_in_dim(partial, core * half, half, 0)
        got = lax.ppermute(give, "aux", aux_pairs(aux_size, 1, 0))
        summed = keep + got
        others = [lax.ppermute(summed, "aux", aux_pairs(aux_size, 0, d)) for d in range(1, chips)]
        for other in others:
            summed = summed + other
        row_energy = lax.dynamic_slice_in_dim(energy(shift, eps_va), core * half, half, 0)
        amp_half = (spin_scale * summed / (row_energy[:, None] + col_energy[None, :])).astype(jnp.bfloat16)
        amp_other = lax.ppermute(amp_half, "aux", aux_pairs(aux_size, 1, 0))
        first = jnp.concatenate([amp_half, amp_other], axis=0)
        second = jnp.concatenate([amp_other, amp_half], axis=0)
        return jnp.where(core == 0, first, second)

    rows_1 = shifted(b_rows, "occ", -1)
    rows_2 = shifted(rows_1, "occ", -1)
    pieces = []
    for shift, left in enumerate([b_rows, rows_1, rows_2]):
        amp = amplitude(partial_integrals(left, b_cols), shift)
        pieces.append(contribution(b_cols, amp))
    carried = shifted(pieces[2], "occ", 1)
    carried = shifted(pieces[1] + carried, "occ", 1)
    return pieces[0] + carried


def solution(mesh):
    return jax.shard_map(
        per_device,
        mesh=mesh,
        in_specs=(P("aux", "occ"), P("aux", "occ"), P(), P(), P()),
        out_specs=P("aux", "occ"),
        check_vma=False,
    )
```

time: 221 us -> 174 us (0.79)
  the two profiles are of different devices: /device:TPU:1 before, /device:TPU:2 now
where the time goes in v1:
time: 174 us; the launch traced here: 173 us
  starting transfers between devices  88 us (51%)
  waiting for transfers between devices  77.5 us (45%)
  matrix products  4.87 us (3%)
  local copies, waits for them, and re-layouts  1.94 us (1%)
    ppermute x4, waiting for transfers between devices, shifted(): lax.ppermute(value, axis, [(i, (i + by) % size) for i in range(size)])  65.2 us
    ppermute x6, starting transfers between devices, amplitude(): lax.ppermute(summed, 'aux', aux_pairs(aux_size, 0, d))  52.5 us
    ppermute x4, starting transfers between devices, shifted(): lax.ppermute(value, axis, [(i, (i + by) % size) for i in range(size)])  23.8 us
    ppermute x6, waiting for transfers between devices, amplitude(): lax.ppermute(summed, 'aux', aux_pairs(aux_size, 0, d))  8.84 us
    ppermute x3, starting transfers between devices, amplitude(): amp_other = lax.ppermute(amp_half, 'aux', aux_pairs(aux_size, 1, 0))  5.91 us
    ppermute x3, starting transfers between devices, amplitude(): got = lax.ppermute(give, 'aux', aux_pairs(aux_size, 1, 0))  5.76 us
    ppermute x3, waiting for transfers between devices, amplitude(): amp_other = lax.ppermute(amp_half, 'aux', aux_pairs(aux_size, 1, 0))  3.51 us
  transfers between devices with their start and end apart: 16, of which 9 were waited for; matrix products, arithmetic and copies ran while one was open for 2% of the time, Pallas kernels for 0%

profile of v1, /device:TPU:2, one launch (start us, length us, event | category | flops | bytes accessed | tf_op | source)
XLA Modules:
  0.0 173.1 jit_solution(9916086596652997308)
XLA Ops:
  0.0 10.9 %collective-permute-start.4 = (bf16[2048,128]{1,0:T(8,128)(2,1)}, bf16[2048,128]{1,0:T(8,128)(2,1)S(1)}, u32[]{:S(2)}, u32[]{:S(2)}) collective-permute-start(bf16[2048,128]{1,0:T(8,128)(2,1)} %param.5), channel_id=1, source_target_pairs={{0,762},{6,0},{12,6},{18,12},{24,18},{30,24},{36,30},{42,36},{48,4... | collective-permute-start | bytes 1572872 | tf_op jit(solution)/shard_map/ppermute | solution.py:11
  10.9 1.5 fusion.24
  12.5 1.9 %collective-permute-start = (f32[64,512]{1,0:T(8,128)S(1)}, f32[64,512]{1,0:T(8,128)S(1)}, u32[]{:S(2)}, u32[]{:S(2)}) collective-permute-start(f32[64,512]{1,0:T(8,128)S(1)} %constant_dynamic-slice_fusion.2), channel_id=1, source_target_pairs={{0,1},{1,0},{2,3},{3,2},{4,5},{5,4},{6,7},{7,6},{8,9},{9,8},{10,11... | collective-permute-start | bytes 393224 | tf_op jit(solution)/shard_map/ppermute | solution.py:56
  14.5 0.1 fusion.23
  14.6 0.1 broadcast_subtract_fusion.2
  14.7 0.1 sub.86
  14.7 0.1 sub.83
  14.8 0.1 dynamic_slice.48
  14.9 0.1 dynamic_slice.44
  15.0 0.1 sub.76
  15.0 0.1 dynamic_slice.40
  15.1 7.3 %collective-permute-done.4 = bf16[2048,128]{1,0:T(8,128)(2,1)S(1)} collective-permute-done((bf16[2048,128]{1,0:T(8,128)(2,1)}, bf16[2048,128]{1,0:T(8,128)(2,1)S(1)}, u32[]{:S(2)}, u32[]{:S(2)}) %collective-permute-start.4) | collective-permute-done | bytes 524320 | tf_op jit(solution)/shard_map/ppermute | solution.py:11
  22.4 9.1 %collective-permute-start.9 = (bf16[2048,128]{1,0:T(8,128)(2,1)S(1)}, bf16[2048,128]{1,0:T(8,128)(2,1)S(1)}, u32[]{:S(2)}, u32[]{:S(2)}) collective-permute-start(bf16[2048,128]{1,0:T(8,128)(2,1)S(1)} %collective-permute-done.4), channel_id=1, source_target_pairs={{0,762},{6,0},{12,6},{18,12},{24,18},{30,24},{36,30},{42,36},{48,4... | collective-permute-start | bytes 1572872 | tf_op jit(solution)/shard_map/ppermute | solution.py:11
  31.5 0.0 collective-permute-done
  31.5 10.6 %collective-permute-start.1 = (f32[64,512]{1,0:T(8,128)S(1)}, f32[64,512]{1,0:T(8,128)S(1)}, u32[]{:S(2)}, u32[]{:S(2)}) collective-permute-start(f32[64,512]{1,0:T(8,128)S(1)} %dynamic-slice_add_fusion.2), channel_id=1, source_target_pairs={{0,2},{1,3},{2,4},{3,5},{4,0},{5,1},{6,8},{7,9},{8,10},{9,11},{10,... | collective-permute-start | bytes 393224 | tf_op jit(solution)/shard_map/ppermute | solution.py:58
  42.2 3.2 %collective-permute-start.2 = (f32[64,512]{1,0:T(8,128)S(1)}, f32[64,512]{1,0:T(8,128)S(1)}, u32[]{:S(2)}, u32[]{:S(2)}) collective-permute-start(f32[64,512]{1,0:T(8,128)S(1)} %dynamic-slice_add_fusion.2), channel_id=1, source_target_pairs={{0,4},{1,5},{2,0},{3,1},{4,2},{5,3},{6,10},{7,11},{8,6},{9,7},{10,... | collective-permute-start | bytes 393224 | tf_op jit(solution)/shard_map/ppermute | solution.py:58
  45.3 0.5 fusion.25
  45.8 0.0 copy-start.2
  45.8 1.9 %collective-permute-start.5 = (f32[64,512]{1,0:T(8,128)S(1)}, f32[64,512]{1,0:T(8,128)S(1)}, u32[]{:S(2)}, u32[]{:S(2)}) collective-permute-start(f32[64,512]{1,0:T(8,128)S(1)} %constant_dynamic-slice_fusion.1), channel_id=1, source_target_pairs={{0,1},{1,0},{2,3},{3,2},{4,5},{5,4},{6,7},{7,6},{8,9},{9,8},{10,11... | collective-permute-start | bytes 393224 | tf_op jit(solution)/shard_map/ppermute | solution.py:56
  47.8 3.9 %collective-permute-done.9 = bf16[2048,128]{1,0:T(8,128)(2,1)S(1)} collective-permute-done((bf16[2048,128]{1,0:T(8,128)(2,1)S(1)}, bf16[2048,128]{1,0:T(8,128)(2,1)S(1)}, u32[]{:S(2)}, u32[]{:S(2)}) %collective-permute-start.9) | collective-permute-done | bytes 524320 | tf_op jit(solution)/shard_map/ppermute | solution.py:11
  51.7 0.5 fusion.26
  52.2 1.9 %collective-permute-start.10 = (f32[64,512]{1,0:T(8,128)S(1)}, f32[64,512]{1,0:T(8,128)S(1)}, u32[]{:S(2)}, u32[]{:S(2)}) collective-permute-start(f32[64,512]{1,0:T(8,128)S(1)} %constant_dynamic-slice_fusion), channel_id=1, source_target_pairs={{0,1},{1,0},{2,3},{3,2},{4,5},{5,4},{6,7},{7,6},{8,9},{9,8},{10,11... | collective-permute-start | bytes 393224 | tf_op jit(solution)/shard_map/ppermute | solution.py:56
  54.1 0.0 collective-permute-done.5
  54.2 27.1 %collective-permute-start.6 = (f32[64,512]{1,0:T(8,128)S(1)}, f32[64,512]{1,0:T(8,128)S(1)}, u32[]{:S(2)}, u32[]{:S(2)}) collective-permute-start(f32[64,512]{1,0:T(8,128)S(1)} %dynamic-slice_add_fusion.1), channel_id=1, source_target_pairs={{0,2},{1,3},{2,4},{3,5},{4,0},{5,1},{6,8},{7,9},{8,10},{9,11},{10,... | collective-permute-start | bytes 393224 | tf_op jit(solution)/shard_map/ppermute | solution.py:58
  81.2 1.9 %collective-permute-start.7 = (f32[64,512]{1,0:T(8,128)S(1)}, f32[64,512]{1,0:T(8,128)S(1)}, u32[]{:S(2)}, u32[]{:S(2)}) collective-permute-start(f32[64,512]{1,0:T(8,128)S(1)} %dynamic-slice_add_fusion.1), channel_id=1, source_target_pairs={{0,4},{1,5},{2,0},{3,1},{4,2},{5,3},{6,10},{7,11},{8,6},{9,7},{10,... | collective-permute-start | bytes 393224 | tf_op jit(solution)/shard_map/ppermute | solution.py:58
  83.2 0.0 collective-permute-done.10
  83.2 7.8 %collective-permute-start.11 = (f32[64,512]{1,0:T(8,128)S(1)}, f32[64,512]{1,0:T(8,128)S(1)}, u32[]{:S(2)}, u32[]{:S(2)}) collective-permute-start(f32[64,512]{1,0:T(8,128)S(1)} %dynamic-slice_add_fusion), channel_id=1, source_target_pairs={{0,2},{1,3},{2,4},{3,5},{4,0},{5,1},{6,8},{7,9},{8,10},{9,11},{10,... | collective-permute-start | bytes 393224 | tf_op jit(solution)/shard_map/ppermute | solution.py:58
  91.0 0.0 collective-permute-done.1
  91.0 1.9 %collective-permute-start.12 = (f32[64,512]{1,0:T(8,128)S(1)}, f32[64,512]{1,0:T(8,128)S(1)}, u32[]{:S(2)}, u32[]{:S(2)}) collective-permute-start(f32[64,512]{1,0:T(8,128)S(1)} %dynamic-slice_add_fusion), channel_id=1, source_target_pairs={{0,4},{1,5},{2,0},{3,1},{4,2},{5,3},{6,10},{7,11},{8,6},{9,7},{10,... | collective-permute-start | bytes 393224 | tf_op jit(solution)/shard_map/ppermute | solution.py:58
  93.0 0.1 subtract_bitcast_fusion
  93.1 0.0 collective-permute-done.2
  93.1 1.5 collective-permute-done.11
  94.6 7.3 %collective-permute-done.12 = f32[64,512]{1,0:T(8,128)S(1)} collective-permute-done((f32[64,512]{1,0:T(8,128)S(1)}, f32[64,512]{1,0:T(8,128)S(1)}, u32[]{:S(2)}, u32[]{:S(2)}) %collective-permute-start.12) | collective-permute-done | bytes 131104 | tf_op jit(solution)/shard_map/ppermute | solution.py:58
  101.9 0.1 divide_convert_fusion.2
  102.0 1.9 %collective-permute-start.13 = (bf16[64,512]{1,0:T(8,128)(2,1)S(1)}, bf16[64,512]{1,0:T(8,128)(2,1)S(1)}, u32[]{:S(2)}, u32[]{:S(2)}) collective-permute-start(bf16[64,512]{1,0:T(8,128)(2,1)S(1)} %get-tuple-element.7), channel_id=1, source_target_pairs={{0,1},{1,0},{2,3},{3,2},{4,5},{5,4},{6,7},{7,6},{8,9},{9,8},{10,11... | collective-permute-start | bytes 196616 | tf_op jit(solution)/shard_map/ppermute | solution.py:63
  104.0 1.2 collective-permute-done.13
  105.2 0.8 convolution_bitcast_fusion
  106.0 1.9 %collective-permute-start.14 = (f32[2048,128]{0,1:T(8,128)S(1)}, f32[2048,128]{0,1:T(8,128)S(1)}, u32[]{:S(2)}, u32[]{:S(2)}) collective-permute-start(f32[2048,128]{0,1:T(8,128)S(1)} %convolution_bitcast_fusion), channel_id=1, source_target_pairs={{0,6},{6,12},{12,18},{18,24},{24,30},{30,36},{36,42},{42,48},{48,5... | collective-permute-start | bytes 3145736 | tf_op jit(solution)/shard_map/ppermute | solution.py:11
  107.9 2.1 %collective-permute-start.8 = (bf16[64,512]{1,0:T(8,128)(2,1)S(1)}, bf16[64,512]{1,0:T(8,128)(2,1)S(1)}, u32[]{:S(2)}, u32[]{:S(2)}) collective-permute-start(bf16[64,512]{1,0:T(8,128)(2,1)S(1)} %get-tuple-element.6), channel_id=1, source_target_pairs={{0,1},{1,0},{2,3},{3,2},{4,5},{5,4},{6,7},{7,6},{8,9},{9,8},{10,11... | collective-permute-start | bytes 196616 | tf_op jit(solution)/shard_map/ppermute | solution.py:63
  110.0 1.1 collective-permute-done.8
  111.1 27.7 %collective-permute-done.14 = f32[2048,128]{0,1:T(8,128)S(1)} collective-permute-done((f32[2048,128]{0,1:T(8,128)S(1)}, f32[2048,128]{0,1:T(8,128)S(1)}, u32[]{:S(2)}, u32[]{:S(2)}) %collective-permute-start.14) | collective-permute-done | bytes 1048608 | tf_op jit(solution)/shard_map/ppermute | solution.py:11
  138.8 0.8 fusion
  139.6 1.9 %collective-permute-start.15 = (f32[2048,128]{0,1:T(8,128)S(1)}, f32[2048,128]{0,1:T(8,128)S(1)}, u32[]{:S(2)}, u32[]{:S(2)}) collective-permute-start(f32[2048,128]{0,1:T(8,128)S(1)} %fusion), channel_id=1, source_target_pairs={{0,6},{6,12},{12,18},{18,24},{24,30},{30,36},{36,42},{42,48},{48,5... | collective-permute-start | bytes 3145736 | tf_op jit(solution)/shard_map/ppermute | solution.py:11
  141.5 1.9 %collective-permute-start.3 = (bf16[64,512]{1,0:T(8,128)(2,1)S(1)}, bf16[64,512]{1,0:T(8,128)(2,1)S(1)}, u32[]{:S(2)}, u32[]{:S(2)}) collective-permute-start(bf16[64,512]{1,0:T(8,128)(2,1)S(1)} %get-tuple-element.5), channel_id=1, source_target_pairs={{0,1},{1,0},{2,3},{3,2},{4,5},{5,4},{6,7},{7,6},{8,9},{9,8},{10,11... | collective-permute-start | bytes 196616 | tf_op jit(solution)/shard_map/ppermute | solution.py:63
  143.5 1.2 collective-permute-done.3
  144.7 26.3 %collective-permute-done.15 = f32[2048,128]{0,1:T(8,128)S(1)} collective-permute-done((f32[2048,128]{0,1:T(8,128)S(1)}, f32[2048,128]{0,1:T(8,128)S(1)}, u32[]{:S(2)}, u32[]{:S(2)}) %collective-permute-start.15) | collective-permute-done | bytes 1048608 | tf_op jit(solution)/shard_map/ppermute | solution.py:11
  171.0 0.8 fusion.1
  171.8 1.3 copy.6
  (16 shorter events, 0.1 us)
Async XLA Ops:
  0.0 10.9 %copy-start = (bf16[2048,512]{1,0:T(8,128)(2,1)S(1)}, bf16[2048,512]{1,0:T(8,128)(2,1)}, u32[]{:S(2)}) copy-start(bf16[2048,512]{1,0:T(8,128)(2,1)} %param.6) | copy-start | bytes 6291460
  0.0 14.5 %copy-start.1 = (f32[256]{0:T(256)S(1)}, f32[256]{0:T(256)}, u32[]{:S(2)}) copy-start(f32[256]{0:T(256)} %param.7) | copy-start | bytes 3076
  0.0 14.6 %copy-start.3 = (f32[64]{0:T(128)S(1)}, f32[64]{0:T(128)}, u32[]{:S(2)}) copy-start(f32[64]{0:T(128)} %param.8) | copy-start | bytes 772
  0.0 22.4 %collective-permute-start.4 = (bf16[2048,128]{1,0:T(8,128)(2,1)}, bf16[2048,128]{1,0:T(8,128)(2,1)S(1)}, u32[]{:S(2)}, u32[]{:S(2)}) collective-permute-start(bf16[2048,128]{1,0:T(8,128)(2,1)} %param.5), channel_id=1, source_target_pairs={{0,762},{6,0},{12,6},{18,12},{24,18},{30,24},{36,30},{42,36},{48,4... | collective-permute-start | bytes 1572872 | tf_op jit(solution)/shard_map/ppermute | solution.py:11
  12.5 19.0 %collective-permute-start = (f32[64,512]{1,0:T(8,128)S(1)}, f32[64,512]{1,0:T(8,128)S(1)}, u32[]{:S(2)}, u32[]{:S(2)}) collective-permute-start(f32[64,512]{1,0:T(8,128)S(1)} %constant_dynamic-slice_fusion.2), channel_id=1, source_target_pairs={{0,1},{1,0},{2,3},{3,2},{4,5},{5,4},{6,7},{7,6},{8,9},{9,8},{10,11... | collective-permute-start | bytes 393224 | tf_op jit(solution)/shard_map/ppermute | solution.py:56
  22.4 29.3 %collective-permute-start.9 = (bf16[2048,128]{1,0:T(8,128)(2,1)S(1)}, bf16[2048,128]{1,0:T(8,128)(2,1)S(1)}, u32[]{:S(2)}, u32[]{:S(2)}) collective-permute-start(bf16[2048,128]{1,0:T(8,128)(2,1)S(1)} %collective-permute-done.4), channel_id=1, source_target_pairs={{0,762},{6,0},{12,6},{18,12},{24,18},{30,24},{36,30},{42,36},{48,4... | collective-permute-start | bytes 1572872 | tf_op jit(solution)/shard_map/ppermute | solution.py:11
  31.5 59.5 %collective-permute-start.1 = (f32[64,512]{1,0:T(8,128)S(1)}, f32[64,512]{1,0:T(8,128)S(1)}, u32[]{:S(2)}, u32[]{:S(2)}) collective-permute-start(f32[64,512]{1,0:T(8,128)S(1)} %dynamic-slice_add_fusion.2), channel_id=1, source_target_pairs={{0,2},{1,3},{2,4},{3,5},{4,0},{5,1},{6,8},{7,9},{8,10},{9,11},{10,... | collective-permute-start | bytes 393224 | tf_op jit(solution)/shard_map/ppermute | solution.py:58
  42.2 50.9 %collective-permute-start.2 = (f32[64,512]{1,0:T(8,128)S(1)}, f32[64,512]{1,0:T(8,128)S(1)}, u32[]{:S(2)}, u32[]{:S(2)}) collective-permute-start(f32[64,512]{1,0:T(8,128)S(1)} %dynamic-slice_add_fusion.2), channel_id=1, source_target_pairs={{0,4},{1,5},{2,0},{3,1},{4,2},{5,3},{6,10},{7,11},{8,6},{9,7},{10,... | collective-permute-start | bytes 393224 | tf_op jit(solution)/shard_map/ppermute | solution.py:58
  45.8 47.2 %copy-start.2 = (f32[256]{0:T(256)S(1)}, f32[256]{0:T(256)}, u32[]{:S(2)}) copy-start(f32[256]{0:T(256)} %param.9) | copy-start | bytes 3076
  45.8 8.3 %collective-permute-start.5 = (f32[64,512]{1,0:T(8,128)S(1)}, f32[64,512]{1,0:T(8,128)S(1)}, u32[]{:S(2)}, u32[]{:S(2)}) collective-permute-start(f32[64,512]{1,0:T(8,128)S(1)} %constant_dynamic-slice_fusion.1), channel_id=1, source_target_pairs={{0,1},{1,0},{2,3},{3,2},{4,5},{5,4},{6,7},{7,6},{8,9},{9,8},{10,11... | collective-permute-start | bytes 393224 | tf_op jit(solution)/shard_map/ppermute | solution.py:56
  52.2 31.0 %collective-permute-start.10 = (f32[64,512]{1,0:T(8,128)S(1)}, f32[64,512]{1,0:T(8,128)S(1)}, u32[]{:S(2)}, u32[]{:S(2)}) collective-permute-start(f32[64,512]{1,0:T(8,128)S(1)} %constant_dynamic-slice_fusion), channel_id=1, source_target_pairs={{0,1},{1,0},{2,3},{3,2},{4,5},{5,4},{6,7},{7,6},{8,9},{9,8},{10,11... | collective-permute-start | bytes 393224 | tf_op jit(solution)/shard_map/ppermute | solution.py:56
  54.2 38.9 %collective-permute-start.6 = (f32[64,512]{1,0:T(8,128)S(1)}, f32[64,512]{1,0:T(8,128)S(1)}, u32[]{:S(2)}, u32[]{:S(2)}) collective-permute-start(f32[64,512]{1,0:T(8,128)S(1)} %dynamic-slice_add_fusion.1), channel_id=1, source_target_pairs={{0,2},{1,3},{2,4},{3,5},{4,0},{5,1},{6,8},{7,9},{8,10},{9,11},{10,... | collective-permute-start | bytes 393224 | tf_op jit(solution)/shard_map/ppermute | solution.py:58
  81.2 11.8 %collective-permute-start.7 = (f32[64,512]{1,0:T(8,128)S(1)}, f32[64,512]{1,0:T(8,128)S(1)}, u32[]{:S(2)}, u32[]{:S(2)}) collective-permute-start(f32[64,512]{1,0:T(8,128)S(1)} %dynamic-slice_add_fusion.1), channel_id=1, source_target_pairs={{0,4},{1,5},{2,0},{3,1},{4,2},{5,3},{6,10},{7,11},{8,6},{9,7},{10,... | collective-permute-start | bytes 393224 | tf_op jit(solution)/shard_map/ppermute | solution.py:58
  83.2 11.4 %collective-permute-start.11 = (f32[64,512]{1,0:T(8,128)S(1)}, f32[64,512]{1,0:T(8,128)S(1)}, u32[]{:S(2)}, u32[]{:S(2)}) collective-permute-start(f32[64,512]{1,0:T(8,128)S(1)} %dynamic-slice_add_fusion), channel_id=1, source_target_pairs={{0,2},{1,3},{2,4},{3,5},{4,0},{5,1},{6,8},{7,9},{8,10},{9,11},{10,... | collective-permute-start | bytes 393224 | tf_op jit(solution)/shard_map/ppermute | solution.py:58
  91.0 10.9 %collective-permute-start.12 = (f32[64,512]{1,0:T(8,128)S(1)}, f32[64,512]{1,0:T(8,128)S(1)}, u32[]{:S(2)}, u32[]{:S(2)}) collective-permute-start(f32[64,512]{1,0:T(8,128)S(1)} %dynamic-slice_add_fusion), channel_id=1, source_target_pairs={{0,4},{1,5},{2,0},{3,1},{4,2},{5,3},{6,10},{7,11},{8,6},{9,7},{10,... | collective-permute-start | bytes 393224 | tf_op jit(solution)/shard_map/ppermute | solution.py:58
  102.0 3.1 %collective-permute-start.13 = (bf16[64,512]{1,0:T(8,128)(2,1)S(1)}, bf16[64,512]{1,0:T(8,128)(2,1)S(1)}, u32[]{:S(2)}, u32[]{:S(2)}) collective-permute-start(bf16[64,512]{1,0:T(8,128)(2,1)S(1)} %get-tuple-element.7), channel_id=1, source_target_pairs={{0,1},{1,0},{2,3},{3,2},{4,5},{5,4},{6,7},{7,6},{8,9},{9,8},{10,11... | collective-permute-start | bytes 196616 | tf_op jit(solution)/shard_map/ppermute | solution.py:63
  106.0 32.8 %collective-permute-start.14 = (f32[2048,128]{0,1:T(8,128)S(1)}, f32[2048,128]{0,1:T(8,128)S(1)}, u32[]{:S(2)}, u32[]{:S(2)}) collective-permute-start(f32[2048,128]{0,1:T(8,128)S(1)} %convolution_bitcast_fusion), channel_id=1, source_target_pairs={{0,6},{6,12},{12,18},{18,24},{24,30},{30,36},{36,42},{42,48},{48,5... | collective-permute-start | bytes 3145736 | tf_op jit(solution)/shard_map/ppermute | solution.py:11
  107.9 3.1 %collective-permute-start.8 = (bf16[64,512]{1,0:T(8,128)(2,1)S(1)}, bf16[64,512]{1,0:T(8,128)(2,1)S(1)}, u32[]{:S(2)}, u32[]{:S(2)}) collective-permute-start(bf16[64,512]{1,0:T(8,128)(2,1)S(1)} %get-tuple-element.6), channel_id=1, source_target_pairs={{0,1},{1,0},{2,3},{3,2},{4,5},{5,4},{6,7},{7,6},{8,9},{9,8},{10,11... | collective-permute-start | bytes 196616 | tf_op jit(solution)/shard_map/ppermute | solution.py:63
  139.6 31.3 %collective-permute-start.15 = (f32[2048,128]{0,1:T(8,128)S(1)}, f32[2048,128]{0,1:T(8,128)S(1)}, u32[]{:S(2)}, u32[]{:S(2)}) collective-permute-start(f32[2048,128]{0,1:T(8,128)S(1)} %fusion), channel_id=1, source_target_pairs={{0,6},{6,12},{12,18},{18,24},{24,30},{30,36},{36,42},{42,48},{48,5... | collective-permute-start | bytes 3145736 | tf_op jit(solution)/shard_map/ppermute | solution.py:11
  141.5 3.1 %collective-permute-start.3 = (bf16[64,512]{1,0:T(8,128)(2,1)S(1)}, bf16[64,512]{1,0:T(8,128)(2,1)S(1)}, u32[]{:S(2)}, u32[]{:S(2)}) collective-permute-start(bf16[64,512]{1,0:T(8,128)(2,1)S(1)} %get-tuple-element.5), channel_id=1, source_target_pairs={{0,1},{1,0},{2,3},{3,2},{4,5},{5,4},{6,7},{7,6},{8,9},{9,8},{10,11... | collective-permute-start | bytes 196616 | tf_op jit(solution)/shard_map/ppermute | solution.py:63

commit v2 on v1

--- a/solution.py
+++ b/solution.py
@@ -50,27 +50,32 @@
 
     col_energy = energy(0, eps_vb)
 
-    def amplitude(partial, shift):
-        give = lax.dynamic_slice_in_dim(partial, (1 - core) * half, half, 0)
-        keep = lax.dynamic_slice_in_dim(partial, core * half, half, 0)
-        got = lax.ppermute(give, "aux", aux_pairs(aux_size, 1, 0))
-        summed = keep + got
+    def core_reduce(partials):
+        stack = jnp.stack(partials)
+        give = lax.dynamic_slice_in_dim(stack, (1 - core) * half, half, 1)
+        keep = lax.dynamic_slice_in_dim(stack, core * half, half, 1)
+        return keep + lax.ppermute(give, "aux", aux_pairs(aux_size, 1, 0))
+
+    def chip_reduce(summed):
         others = [lax.ppermute(summed, "aux", aux_pairs(aux_size, 0, d)) for d in range(1, chips)]
         for other in others:
             summed = summed + other
+        return summed
+
+    def amplitude_half(summed, shift):
         row_energy = lax.dynamic_slice_in_dim(energy(shift, eps_va), core * half, half, 0)
-        amp_half = (spin_scale * summed / (row_energy[:, None] + col_energy[None, :])).astype(jnp.bfloat16)
-        amp_other = lax.ppermute(amp_half, "aux", aux_pairs(aux_size, 1, 0))
-        first = jnp.concatenate([amp_half, amp_other], axis=0)
-        second = jnp.concatenate([amp_other, amp_half], axis=0)
-        return jnp.where(core == 0, first, second)
+        return (spin_scale * summed / (row_energy[:, None] + col_energy[None, :])).astype(jnp.bfloat16)
 
     rows_1 = shifted(b_rows, "occ", -1)
+    early = chip_reduce(core_reduce([partial_integrals(b_rows, b_cols), partial_integrals(rows_1, b_cols)]))
     rows_2 = shifted(rows_1, "occ", -1)
-    pieces = []
-    for shift, left in enumerate([b_rows, rows_1, rows_2]):
-        amp = amplitude(partial_integrals(left, b_cols), shift)
-        pieces.append(contribution(b_cols, amp))
+    late = chip_reduce(core_reduce([partial_integrals(rows_2, b_cols)]))
+    amp_halves = jnp.stack([amplitude_half(early[0], 0), amplitude_half(early[1], 1), amplitude_half(late[0], 2)])
+    amp_other = lax.ppermute(amp_halves, "aux", aux_pairs(aux_size, 1, 0))
+    first = jnp.concatenate([amp_halves, amp_other], axis=1)
+    second = jnp.concatenate([amp_other, amp_halves], axis=1)
+    amps = jnp.where(core == 0, first, second)
+    pieces = [contribution(b_cols, amps[s]) for s in range(3)]
     carried = shifted(pieces[2], "occ", 1)
     carried = shifted(pieces[1] + carried, "occ", 1)
     return pieces[0] + carried

time: 174 us -> 167 us (0.960)
  the two profiles are of different devices: /device:TPU:2 before, /device:TPU:1 now
where the time goes in v2:
time: 167 us; the launch traced here: 166 us
  waiting for transfers between devices  88.3 us (53%)
  starting transfers between devices  66.8 us (40%)
  matrix products  5.93 us (4%)
  other arithmetic  3.02 us (2%)
  local copies, waits for them, and re-layouts  1.91 us (1%)
    ppermute x4, waiting for transfers between devices, shifted(): lax.ppermute(value, axis, [(i, (i + by) % size) for i in range(size)])  69.1 us
    ppermute x4, starting transfers between devices, shifted(): lax.ppermute(value, axis, [(i, (i + by) % size) for i in range(size)])  27.5 us
    ppermute x4, starting transfers between devices, chip_reduce(): lax.ppermute(summed, 'aux', aux_pairs(aux_size, 0, d))  27.3 us
    ppermute x4, waiting for transfers between devices, chip_reduce(): lax.ppermute(summed, 'aux', aux_pairs(aux_size, 0, d))  17.8 us
    ppermute x2, starting transfers between devices, core_reduce(): return keep + lax.ppermute(give, 'aux', aux_pairs(aux_size, 1, 0))  9.14 us
    dot_general x3, matrix products, partial_integrals(): lax.dot_general(left_block, right_block, (((0,), (0,)), ((), ())), prefer...  3.48 us
  transfers between devices with their start and end apart: 11, of which 7 were waited for; matrix products, arithmetic and copies ran while one was open for 3% of the time, Pallas kernels for 0%

profile of v2, /device:TPU:1, one launch (start us, length us, event | category | flops | bytes accessed | tf_op | source)
XLA Modules:
  0.0 166.3 jit_solution(8021347453676532555)
XLA Ops:
  0.0 0.0 copy-start
  0.0 13.7 %collective-permute-start = (bf16[2048,128]{1,0:T(8,128)(2,1)}, bf16[2048,128]{1,0:T(8,128)(2,1)S(1)}, u32[]{:S(2)}, u32[]{:S(2)}) collective-permute-start(bf16[2048,128]{1,0:T(8,128)(2,1)} %param.5), channel_id=1, source_target_pairs={{0,762},{6,0},{12,6},{18,12},{24,18},{30,24},{36,30},{42,36},{48,4... | collective-permute-start | bytes 1572872 | tf_op jit(solution)/shard_map/ppermute | solution.py:11
  13.7 0.0 copy-done
  13.7 1.5 convolution_bitcast_fusion.4
  15.3 0.0 copy-start.1
  15.3 0.0 copy-start.3
  15.3 9.3 %collective-permute-done = bf16[2048,128]{1,0:T(8,128)(2,1)S(1)} collective-permute-done((bf16[2048,128]{1,0:T(8,128)(2,1)}, bf16[2048,128]{1,0:T(8,128)(2,1)S(1)}, u32[]{:S(2)}, u32[]{:S(2)}) %collective-permute-start) | collective-permute-done | bytes 524320 | tf_op jit(solution)/shard_map/ppermute | solution.py:11
  24.6 0.5 convolution_bitcast_fusion.3
  25.0 0.7 fusion.1
  25.8 3.4 %collective-permute-start.1 = (f32[2,64,512]{2,1,0:T(8,128)}, f32[2,64,512]{2,1,0:T(8,128)S(1)}, u32[]{:S(2)}, u32[]{:S(2)}) collective-permute-start(f32[2,64,512]{2,1,0:T(8,128)} %fusion.1), channel_id=1, source_target_pairs={{0,1},{1,0},{2,3},{3,2},{4,5},{5,4},{6,7},{7,6},{8,9},{9,8},{10,11... | collective-permute-start | bytes 786440 | tf_op jit(solution)/shard_map/ppermute | solution.py:57
  29.2 10.0 %collective-permute-start.4 = (bf16[2048,128]{1,0:T(8,128)(2,1)S(1)}, bf16[2048,128]{1,0:T(8,128)(2,1)}, u32[]{:S(2)}, u32[]{:S(2)}) collective-permute-start(bf16[2048,128]{1,0:T(8,128)(2,1)S(1)} %collective-permute-done), channel_id=1, source_target_pairs={{0,762},{6,0},{12,6},{18,12},{24,18},{30,24},{36,30},{42,36},{48,4... | collective-permute-start | bytes 1572872 | tf_op jit(solution)/shard_map/ppermute | solution.py:11
  39.2 0.0 copy-done.1
  39.2 0.1 fusion.9
  39.3 0.1 broadcast_subtract_fusion.2
  39.4 0.0 collective-permute-done.1
  39.4 0.7 fusion.3
  40.1 11.6 %collective-permute-start.3 = (f32[2,64,512]{2,1,0:T(8,128)}, f32[2,64,512]{2,1,0:T(8,128)}, u32[]{:S(2)}, u32[]{:S(2)}) collective-permute-start(f32[2,64,512]{2,1,0:T(8,128)} %fusion.3), channel_id=1, source_target_pairs={{0,4},{1,5},{2,0},{3,1},{4,2},{5,3},{6,10},{7,11},{8,6},{9,7},{10,... | collective-permute-start | bytes 786440 | tf_op jit(solution)/shard_map/ppermute | solution.py:60
  51.7 1.9 %collective-permute-start.2 = (f32[2,64,512]{2,1,0:T(8,128)}, f32[2,64,512]{2,1,0:T(8,128)}, u32[]{:S(2)}, u32[]{:S(2)}) collective-permute-start(f32[2,64,512]{2,1,0:T(8,128)} %fusion.3), channel_id=1, source_target_pairs={{0,2},{1,3},{2,4},{3,5},{4,0},{5,1},{6,8},{7,9},{8,10},{9,11},{10,... | collective-permute-start | bytes 786440 | tf_op jit(solution)/shard_map/ppermute | solution.py:60
  53.7 0.0 collective-permute-done.4
  53.7 1.5 fusion.10
  55.2 5.7 %collective-permute-start.5 = (f32[1,64,512]{2,1,0:T(8,128)S(1)}, f32[1,64,512]{2,1,0:T(8,128)S(1)}, u32[]{:S(2)}, u32[]{:S(2)}) collective-permute-start(f32[1,64,512]{2,1,0:T(8,128)S(1)} %dynamic-slice_bitcast_fusion), channel_id=1, source_target_pairs={{0,1},{1,0},{2,3},{3,2},{4,5},{5,4},{6,7},{7,6},{8,9},{9,8},{10,11... | collective-permute-start | bytes 393224 | tf_op jit(solution)/shard_map/ppermute | solution.py:57
  60.9 0.1 subtract_bitcast_fusion
  61.0 0.1 sub.75
  61.1 0.1 dynamic_slice.34
  61.2 0.1 sub.82
  61.3 0.1 dynamic_slice.36
  61.3 0.1 sub.85
  61.4 0.1 dynamic_slice.40
  61.5 0.4 collective-permute-done.5
  61.9 11.9 %collective-permute-start.7 = (f32[1,64,512]{2,1,0:T(8,128)S(1)}, f32[1,64,512]{2,1,0:T(8,128)S(1)}, u32[]{:S(2)}, u32[]{:S(2)}) collective-permute-start(f32[1,64,512]{2,1,0:T(8,128)S(1)} %bitcast_add_fusion), channel_id=1, source_target_pairs={{0,4},{1,5},{2,0},{3,1},{4,2},{5,3},{6,10},{7,11},{8,6},{9,7},{10,... | collective-permute-start | bytes 393224 | tf_op jit(solution)/shard_map/ppermute | solution.py:60
  73.8 1.9 %collective-permute-start.6 = (f32[1,64,512]{2,1,0:T(8,128)S(1)}, f32[1,64,512]{2,1,0:T(8,128)S(1)}, u32[]{:S(2)}, u32[]{:S(2)}) collective-permute-start(f32[1,64,512]{2,1,0:T(8,128)S(1)} %bitcast_add_fusion), channel_id=1, source_target_pairs={{0,2},{1,3},{2,4},{3,5},{4,0},{5,1},{6,8},{7,9},{8,10},{9,11},{10,... | collective-permute-start | bytes 393224 | tf_op jit(solution)/shard_map/ppermute | solution.py:60
  75.7 0.0 collective-permute-done.3
  75.7 16.2 %collective-permute-done.2 = f32[2,64,512]{2,1,0:T(8,128)} collective-permute-done((f32[2,64,512]{2,1,0:T(8,128)}, f32[2,64,512]{2,1,0:T(8,128)}, u32[]{:S(2)}, u32[]{:S(2)}) %collective-permute-start.2) | collective-permute-done | bytes 262176 | tf_op jit(solution)/shard_map/ppermute | solution.py:60
  91.9 1.1 add_add_fusion
  93.0 0.0 collective-permute-done.7
  93.0 1.6 collective-permute-done.6
  94.6 0.1 fusion.8
  94.8 2.9 %collective-permute-start.8 = (bf16[3,64,512]{2,1,0:T(8,128)(2,1)S(1)}, bf16[3,64,512]{2,1,0:T(8,128)(2,1)S(1)}, u32[]{:S(2)}, u32[]{:S(2)}) collective-permute-start(bf16[3,64,512]{2,1,0:T(8,128)(2,1)S(1)} %pad_maximum_fusion), channel_id=1, source_target_pairs={{0,1},{1,0},{2,3},{3,2},{4,5},{5,4},{6,7},{7,6},{8,9},{9,8},{10,11... | collective-permute-start | bytes 589832 | tf_op jit(solution)/shard_map/ppermute | solution.py:74
  97.7 1.0 collective-permute-done.8
  98.7 0.1 maximum_select_fusion
  98.8 0.8 convolution_bitcast_fusion
  99.6 1.9 %collective-permute-start.9 = (f32[2048,128]{0,1:T(8,128)S(1)}, f32[2048,128]{0,1:T(8,128)S(1)}, u32[]{:S(2)}, u32[]{:S(2)}) collective-permute-start(f32[2048,128]{0,1:T(8,128)S(1)} %convolution_bitcast_fusion), channel_id=1, source_target_pairs={{0,6},{6,12},{12,18},{18,24},{24,30},{30,36},{36,42},{42,48},{48,5... | collective-permute-start | bytes 3145736 | tf_op jit(solution)/shard_map/ppermute | solution.py:11
  101.6 30.3 %collective-permute-done.9 = f32[2048,128]{0,1:T(8,128)S(1)} collective-permute-done((f32[2048,128]{0,1:T(8,128)S(1)}, f32[2048,128]{0,1:T(8,128)S(1)}, u32[]{:S(2)}, u32[]{:S(2)}) %collective-permute-start.9) | collective-permute-done | bytes 1048608 | tf_op jit(solution)/shard_map/ppermute | solution.py:11
  131.9 0.8 fusion
  132.7 1.9 %collective-permute-start.10 = (f32[2048,128]{0,1:T(8,128)S(1)}, f32[2048,128]{0,1:T(8,128)S(1)}, u32[]{:S(2)}, u32[]{:S(2)}) collective-permute-start(f32[2048,128]{0,1:T(8,128)S(1)} %fusion), channel_id=1, source_target_pairs={{0,6},{6,12},{12,18},{18,24},{24,30},{30,36},{36,42},{42,48},{48,5... | collective-permute-start | bytes 3145736 | tf_op jit(solution)/shard_map/ppermute | solution.py:11
  134.7 29.5 %collective-permute-done.10 = f32[2048,128]{0,1:T(8,128)S(1)} collective-permute-done((f32[2048,128]{0,1:T(8,128)S(1)}, f32[2048,128]{0,1:T(8,128)S(1)}, u32[]{:S(2)}, u32[]{:S(2)}) %collective-permute-start.10) | collective-permute-done | bytes 1048608 | tf_op jit(solution)/shard_map/ppermute | solution.py:11
  164.1 0.8 fusion.4
  165.0 1.3 copy.6
  (7 shorter events, 0.1 us)
Async XLA Ops:
  0.0 13.7 %copy-start = (bf16[2048,512]{1,0:T(8,128)(2,1)S(1)}, bf16[2048,512]{1,0:T(8,128)(2,1)}, u32[]{:S(2)}) copy-start(bf16[2048,512]{1,0:T(8,128)(2,1)} %param.6) | copy-start | bytes 6291460
  0.0 24.6 %collective-permute-start = (bf16[2048,128]{1,0:T(8,128)(2,1)}, bf16[2048,128]{1,0:T(8,128)(2,1)S(1)}, u32[]{:S(2)}, u32[]{:S(2)}) collective-permute-start(bf16[2048,128]{1,0:T(8,128)(2,1)} %param.5), channel_id=1, source_target_pairs={{0,762},{6,0},{12,6},{18,12},{24,18},{30,24},{36,30},{42,36},{48,4... | collective-permute-start | bytes 1572872 | tf_op jit(solution)/shard_map/ppermute | solution.py:11
  15.3 24.0 %copy-start.1 = (f32[256]{0:T(256)S(1)}, f32[256]{0:T(256)}, u32[]{:S(2)}) copy-start(f32[256]{0:T(256)} %param.7) | copy-start | bytes 3076
  15.3 24.1 %copy-start.3 = (f32[64]{0:T(128)S(1)}, f32[64]{0:T(128)}, u32[]{:S(2)}) copy-start(f32[64]{0:T(128)} %param.8) | copy-start | bytes 772
  25.8 13.6 %collective-permute-start.1 = (f32[2,64,512]{2,1,0:T(8,128)}, f32[2,64,512]{2,1,0:T(8,128)S(1)}, u32[]{:S(2)}, u32[]{:S(2)}) collective-permute-start(f32[2,64,512]{2,1,0:T(8,128)} %fusion.1), channel_id=1, source_target_pairs={{0,1},{1,0},{2,3},{3,2},{4,5},{5,4},{6,7},{7,6},{8,9},{9,8},{10,11... | collective-permute-start | bytes 786440 | tf_op jit(solution)/shard_map/ppermute | solution.py:57
  29.2 24.5 %collective-permute-start.4 = (bf16[2048,128]{1,0:T(8,128)(2,1)S(1)}, bf16[2048,128]{1,0:T(8,128)(2,1)}, u32[]{:S(2)}, u32[]{:S(2)}) collective-permute-start(bf16[2048,128]{1,0:T(8,128)(2,1)S(1)} %collective-permute-done), channel_id=1, source_target_pairs={{0,762},{6,0},{12,6},{18,12},{24,18},{30,24},{36,30},{42,36},{48,4... | collective-permute-start | bytes 1572872 | tf_op jit(solution)/shard_map/ppermute | solution.py:11
  39.4 21.5 %copy-start.2 = (f32[256]{0:T(256)S(1)}, f32[256]{0:T(256)}, u32[]{:S(2)}) copy-start(f32[256]{0:T(256)} %param.9) | copy-start | bytes 3076
  40.1 35.6 %collective-permute-start.3 = (f32[2,64,512]{2,1,0:T(8,128)}, f32[2,64,512]{2,1,0:T(8,128)}, u32[]{:S(2)}, u32[]{:S(2)}) collective-permute-start(f32[2,64,512]{2,1,0:T(8,128)} %fusion.3), channel_id=1, source_target_pairs={{0,4},{1,5},{2,0},{3,1},{4,2},{5,3},{6,10},{7,11},{8,6},{9,7},{10,... | collective-permute-start | bytes 786440 | tf_op jit(solution)/shard_map/ppermute | solution.py:60
  51.7 40.2 %collective-permute-start.2 = (f32[2,64,512]{2,1,0:T(8,128)}, f32[2,64,512]{2,1,0:T(8,128)}, u32[]{:S(2)}, u32[]{:S(2)}) collective-permute-start(f32[2,64,512]{2,1,0:T(8,128)} %fusion.3), channel_id=1, source_target_pairs={{0,2},{1,3},{2,4},{3,5},{4,0},{5,1},{6,8},{7,9},{8,10},{9,11},{10,... | collective-permute-start | bytes 786440 | tf_op jit(solution)/shard_map/ppermute | solution.py:60
  55.2 6.7 %collective-permute-start.5 = (f32[1,64,512]{2,1,0:T(8,128)S(1)}, f32[1,64,512]{2,1,0:T(8,128)S(1)}, u32[]{:S(2)}, u32[]{:S(2)}) collective-permute-start(f32[1,64,512]{2,1,0:T(8,128)S(1)} %dynamic-slice_bitcast_fusion), channel_id=1, source_target_pairs={{0,1},{1,0},{2,3},{3,2},{4,5},{5,4},{6,7},{7,6},{8,9},{9,8},{10,11... | collective-permute-start | bytes 393224 | tf_op jit(solution)/shard_map/ppermute | solution.py:57
  61.9 31.1 %collective-permute-start.7 = (f32[1,64,512]{2,1,0:T(8,128)S(1)}, f32[1,64,512]{2,1,0:T(8,128)S(1)}, u32[]{:S(2)}, u32[]{:S(2)}) collective-permute-start(f32[1,64,512]{2,1,0:T(8,128)S(1)} %bitcast_add_fusion), channel_id=1, source_target_pairs={{0,4},{1,5},{2,0},{3,1},{4,2},{5,3},{6,10},{7,11},{8,6},{9,7},{10,... | collective-permute-start | bytes 393224 | tf_op jit(solution)/shard_map/ppermute | solution.py:60
  73.8 20.8 %collective-permute-start.6 = (f32[1,64,512]{2,1,0:T(8,128)S(1)}, f32[1,64,512]{2,1,0:T(8,128)S(1)}, u32[]{:S(2)}, u32[]{:S(2)}) collective-permute-start(f32[1,64,512]{2,1,0:T(8,128)S(1)} %bitcast_add_fusion), channel_id=1, source_target_pairs={{0,2},{1,3},{2,4},{3,5},{4,0},{5,1},{6,8},{7,9},{8,10},{9,11},{10,... | collective-permute-start | bytes 393224 | tf_op jit(solution)/shard_map/ppermute | solution.py:60
  94.8 3.9 %collective-permute-start.8 = (bf16[3,64,512]{2,1,0:T(8,128)(2,1)S(1)}, bf16[3,64,512]{2,1,0:T(8,128)(2,1)S(1)}, u32[]{:S(2)}, u32[]{:S(2)}) collective-permute-start(bf16[3,64,512]{2,1,0:T(8,128)(2,1)S(1)} %pad_maximum_fusion), channel_id=1, source_target_pairs={{0,1},{1,0},{2,3},{3,2},{4,5},{5,4},{6,7},{7,6},{8,9},{9,8},{10,11... | collective-permute-start | bytes 589832 | tf_op jit(solution)/shard_map/ppermute | solution.py:74
  99.6 32.3 %collective-permute-start.9 = (f32[2048,128]{0,1:T(8,128)S(1)}, f32[2048,128]{0,1:T(8,128)S(1)}, u32[]{:S(2)}, u32[]{:S(2)}) collective-permute-start(f32[2048,128]{0,1:T(8,128)S(1)} %convolution_bitcast_fusion), channel_id=1, source_target_pairs={{0,6},{6,12},{12,18},{18,24},{24,30},{30,36},{36,42},{42,48},{48,5... | collective-permute-start | bytes 3145736 | tf_op jit(solution)/shard_map/ppermute | solution.py:11
  132.7 31.4 %collective-permute-start.10 = (f32[2048,128]{0,1:T(8,128)S(1)}, f32[2048,128]{0,1:T(8,128)S(1)}, u32[]{:S(2)}, u32[]{:S(2)}) collective-permute-start(f32[2048,128]{0,1:T(8,128)S(1)} %fusion), channel_id=1, source_target_pairs={{0,6},{6,12},{12,18},{18,24},{24,30},{30,36},{36,42},{42,48},{48,5... | collective-permute-start | bytes 3145736 | tf_op jit(solution)/shard_map/ppermute | solution.py:11

commit v3 on v2

--- a/solution.py
+++ b/solution.py
@@ -48,8 +48,6 @@
         occ_energy = lax.dynamic_slice_in_dim(eps_occ, which * per_block, per_block)
         return (virt_energy[None, :] - occ_energy[:, None]).reshape(-1)
 
-    col_energy = energy(0, eps_vb)
-
     def core_reduce(partials):
         stack = jnp.stack(partials)
         give = lax.dynamic_slice_in_dim(stack, (1 - core) * half, half, 1)
@@ -62,23 +60,25 @@
             summed = summed + other
         return summed
 
-    def amplitude_half(summed, shift):
-        row_energy = lax.dynamic_slice_in_dim(energy(shift, eps_va), core * half, half, 0)
+    def amplitude_half(summed, row_shift, col_shift):
+        row_energy = lax.dynamic_slice_in_dim(energy(row_shift, eps_va), core * half, half, 0)
+        col_energy = energy(col_shift, eps_vb)
         return (spin_scale * summed / (row_energy[:, None] + col_energy[None, :])).astype(jnp.bfloat16)
 
-    rows_1 = shifted(b_rows, "occ", -1)
-    early = chip_reduce(core_reduce([partial_integrals(b_rows, b_cols), partial_integrals(rows_1, b_cols)]))
-    rows_2 = shifted(rows_1, "occ", -1)
-    late = chip_reduce(core_reduce([partial_integrals(rows_2, b_cols)]))
-    amp_halves = jnp.stack([amplitude_half(early[0], 0), amplitude_half(early[1], 1), amplitude_half(late[0], 2)])
+    cols_prev = shifted(b_cols, "occ", 1)
+    rows_next = shifted(b_rows, "occ", -1)
+    early = chip_reduce(core_reduce([partial_integrals(b_rows, b_cols), partial_integrals(rows_next, b_cols)]))
+    late = chip_reduce(core_reduce([partial_integrals(rows_next, cols_prev)]))
+    amp_halves = jnp.stack([
+        amplitude_half(early[0], 0, 0), amplitude_half(early[1], 1, 0), amplitude_half(late[0], 1, -1)
+    ])
     amp_other = lax.ppermute(amp_halves, "aux", aux_pairs(aux_size, 1, 0))
     first = jnp.concatenate([amp_halves, amp_other], axis=1)
     second = jnp.concatenate([amp_other, amp_halves], axis=1)
     amps = jnp.where(core == 0, first, second)
-    pieces = [contribution(b_cols, amps[s]) for s in range(3)]
-    carried = shifted(pieces[2], "occ", 1)
-    carried = shifted(pieces[1] + carried, "occ", 1)
-    return pieces[0] + carried
+    own = contribution(b_cols, amps[0])
+    onward = contribution(b_cols, amps[1]) + contribution(cols_prev, amps[2])
+    return own + shifted(onward, "occ", 1)
 
 
 def solution(mesh):

time: 167 us -> 148 us (0.89)
  the two profiles are of different devices: /device:TPU:1 before, /device:TPU:4 now
where the time goes in v3:
time: 148 us; the launch traced here: 147 us
  waiting for transfers between devices  70.6 us (48%)
  starting transfers between devices  60 us (41%)
  matrix products  9.54 us (6%)
  other arithmetic  3.94 us (3%)
  local copies, waits for them, and re-layouts  2.64 us (2%)
    ppermute x3, waiting for transfers between devices, shifted(): lax.ppermute(value, axis, [(i, (i + by) % size) for i in range(size)])  58.8 us
    ppermute x4, starting transfers between devices, chip_reduce(): lax.ppermute(summed, 'aux', aux_pairs(aux_size, 0, d))  39.5 us
    ppermute x3, starting transfers between devices, shifted(): lax.ppermute(value, axis, [(i, (i + by) % size) for i in range(size)])  14.7 us
    ppermute x4, waiting for transfers between devices, chip_reduce(): lax.ppermute(summed, 'aux', aux_pairs(aux_size, 0, d))  8 us
    dot_general x3, matrix products, partial_integrals(): lax.dot_general(left_block, right_block, (((0,), (0,)), ((), ())), prefer...  5.49 us
    dot_general x3, matrix products, contribution(): lax.dot_general(right_block, amplitude, (((1,), (1,)), ((), ())), preferr...  4.05 us
    ppermute x2, starting transfers between devices, core_reduce(): return keep + lax.ppermute(give, 'aux', aux_pairs(aux_size, 1, 0))  3.83 us
  transfers between devices with their start and end apart: 10, of which 8 were waited for; matrix products, arithmetic and copies ran while one was open for 7% of the time, Pallas kernels for 0%

profile of v3, /device:TPU:4, one launch (start us, length us, event | category | flops | bytes accessed | tf_op | source)
XLA Modules:
  0.0 147.0 jit_solution(17804407873133686278)
XLA Ops:
  0.0 0.0 copy-start
  0.0 3.6 %collective-permute-start.4 = (bf16[2048,512]{1,0:T(8,128)(2,1)}, bf16[2048,512]{1,0:T(8,128)(2,1)}, u32[]{:S(2)}, u32[]{:S(2)}) collective-permute-start(bf16[2048,512]{1,0:T(8,128)(2,1)} %param.6), channel_id=1, source_target_pairs={{0,6},{6,12},{12,18},{18,24},{24,30},{30,36},{36,42},{42,48},{48,5... | collective-permute-start | bytes 6291464 | tf_op jit(solution)/shard_map/ppermute | solution.py:11
  3.6 9.2 %collective-permute-start = (bf16[2048,128]{1,0:T(8,128)(2,1)}, bf16[2048,128]{1,0:T(8,128)(2,1)S(1)}, u32[]{:S(2)}, u32[]{:S(2)}) collective-permute-start(bf16[2048,128]{1,0:T(8,128)(2,1)} %param.5), channel_id=1, source_target_pairs={{0,762},{6,0},{12,6},{18,12},{24,18},{30,24},{36,30},{42,36},{48,4... | collective-permute-start | bytes 1572872 | tf_op jit(solution)/shard_map/ppermute | solution.py:11
  12.9 2.2 %convolution_bitcast_fusion.2 = f32[1,128,512]{2,1,0:T(8,128)S(1)} fusion(bf16[2048,128]{1,0:T(8,128)(2,1)} %param.5, bf16[2048,512]{1,0:T(8,128)(2,1)} %param.6), kind=kOutput, calls=%fused_computation.4 | convolution fusion | flops 268435456 | bytes 2883584 | tf_op jit(solution)/shard_map/dot_general | solution.py:24
  15.2 0.0 copy-start.1
  15.2 0.0 copy-start.2
  15.2 9.1 %collective-permute-done = bf16[2048,128]{1,0:T(8,128)(2,1)S(1)} collective-permute-done((bf16[2048,128]{1,0:T(8,128)(2,1)}, bf16[2048,128]{1,0:T(8,128)(2,1)S(1)}, u32[]{:S(2)}, u32[]{:S(2)}) %collective-permute-start) | collective-permute-done | bytes 524320 | tf_op jit(solution)/shard_map/ppermute | solution.py:11
  24.3 0.0 copy-done
  24.3 0.5 convolution_bitcast_fusion.1
  24.8 0.7 fusion.1
  25.5 1.9 %collective-permute-start.1 = (f32[2,64,512]{2,1,0:T(8,128)}, f32[2,64,512]{2,1,0:T(8,128)S(1)}, u32[]{:S(2)}, u32[]{:S(2)}) collective-permute-start(f32[2,64,512]{2,1,0:T(8,128)} %fusion.1), channel_id=1, source_target_pairs={{0,1},{1,0},{2,3},{3,2},{4,5},{5,4},{6,7},{7,6},{8,9},{9,8},{10,11... | collective-permute-start | bytes 786440 | tf_op jit(solution)/shard_map/ppermute | solution.py:55
  27.4 0.0 copy-done.1
  27.4 0.1 fusion.10
  27.5 0.0 copy-done.2
  27.5 0.1 subtract_bitcast_fusion.1
  27.6 1.5 %collective-permute-done.1 = f32[2,64,512]{2,1,0:T(8,128)S(1)} collective-permute-done((f32[2,64,512]{2,1,0:T(8,128)}, f32[2,64,512]{2,1,0:T(8,128)S(1)}, u32[]{:S(2)}, u32[]{:S(2)}) %collective-permute-start.1) | collective-permute-done | bytes 262176 | tf_op jit(solution)/shard_map/ppermute | solution.py:55
  29.1 0.7 fusion.3
  29.9 12.2 %collective-permute-start.3 = (f32[2,64,512]{2,1,0:T(8,128)}, f32[2,64,512]{2,1,0:T(8,128)}, u32[]{:S(2)}, u32[]{:S(2)}) collective-permute-start(f32[2,64,512]{2,1,0:T(8,128)} %fusion.3), channel_id=1, source_target_pairs={{0,4},{1,5},{2,0},{3,1},{4,2},{5,3},{6,10},{7,11},{8,6},{9,7},{10,... | collective-permute-start | bytes 786440 | tf_op jit(solution)/shard_map/ppermute | solution.py:58
  42.1 1.9 %collective-permute-start.2 = (f32[2,64,512]{2,1,0:T(8,128)}, f32[2,64,512]{2,1,0:T(8,128)}, u32[]{:S(2)}, u32[]{:S(2)}) collective-permute-start(f32[2,64,512]{2,1,0:T(8,128)} %fusion.3), channel_id=1, source_target_pairs={{0,2},{1,3},{2,4},{3,5},{4,0},{5,1},{6,8},{7,9},{8,10},{9,11},{10,... | collective-permute-start | bytes 786440 | tf_op jit(solution)/shard_map/ppermute | solution.py:58
  44.0 19.7 %collective-permute-done.4 = bf16[2048,512]{1,0:T(8,128)(2,1)} collective-permute-done((bf16[2048,512]{1,0:T(8,128)(2,1)}, bf16[2048,512]{1,0:T(8,128)(2,1)}, u32[]{:S(2)}, u32[]{:S(2)}) %collective-permute-start.4) | collective-permute-done | bytes 2097184 | tf_op jit(solution)/shard_map/ppermute | solution.py:11
  63.7 2.8 %fusion.11 = f32[128,512]{1,0:T(8,128)} fusion(bf16[2048,128]{1,0:T(8,128)(2,1)S(1)} %collective-permute-done, bf16[2048,512]{1,0:T(8,128)(2,1)} %collective-permute-done.4), kind=kOutput, calls=%fused_computation.34 | convolution fusion | flops 268435456 | bytes 2883584 | tf_op jit(solution)/shard_map/dot_general | solution.py:24
  66.5 0.9 dynamic-slice_bitcast_fusion
  67.4 1.9 %collective-permute-start.5 = (f32[1,64,512]{2,1,0:T(8,128)S(1)}, f32[1,64,512]{2,1,0:T(8,128)S(1)}, u32[]{:S(2)}, u32[]{:S(2)}) collective-permute-start(f32[1,64,512]{2,1,0:T(8,128)S(1)} %dynamic-slice_bitcast_fusion), channel_id=1, source_target_pairs={{0,1},{1,0},{2,3},{3,2},{4,5},{5,4},{6,7},{7,6},{8,9},{9,8},{10,11... | collective-permute-start | bytes 393224 | tf_op jit(solution)/shard_map/ppermute | solution.py:55
  69.3 0.0 copy-done.3
  69.3 0.1 broadcast_subtract_fusion.1
  69.4 0.1 sub.92
  69.5 0.1 dynamic_slice.34
  69.6 0.1 sub.99
  69.7 0.1 dynamic_slice.36
  69.7 0.9 collective-permute-done.5
  70.7 0.9 bitcast_add_fusion
  71.6 23.4 %collective-permute-start.7 = (f32[1,64,512]{2,1,0:T(8,128)S(1)}, f32[1,64,512]{2,1,0:T(8,128)S(1)}, u32[]{:S(2)}, u32[]{:S(2)}) collective-permute-start(f32[1,64,512]{2,1,0:T(8,128)S(1)} %bitcast_add_fusion), channel_id=1, source_target_pairs={{0,4},{1,5},{2,0},{3,1},{4,2},{5,3},{6,10},{7,11},{8,6},{9,7},{10,... | collective-permute-start | bytes 393224 | tf_op jit(solution)/shard_map/ppermute | solution.py:58
  95.0 1.9 %collective-permute-start.6 = (f32[1,64,512]{2,1,0:T(8,128)S(1)}, f32[1,64,512]{2,1,0:T(8,128)S(1)}, u32[]{:S(2)}, u32[]{:S(2)}) collective-permute-start(f32[1,64,512]{2,1,0:T(8,128)S(1)} %bitcast_add_fusion), channel_id=1, source_target_pairs={{0,2},{1,3},{2,4},{3,5},{4,0},{5,1},{6,8},{7,9},{8,10},{9,11},{10,... | collective-permute-start | bytes 393224 | tf_op jit(solution)/shard_map/ppermute | solution.py:58
  96.9 0.0 collective-permute-done.3
  97.0 0.0 collective-permute-done.2
  97.0 1.1 add_add_fusion
  98.1 1.2 collective-permute-done.7
  99.3 6.8 %collective-permute-done.6 = f32[1,64,512]{2,1,0:T(8,128)S(1)} collective-permute-done((f32[1,64,512]{2,1,0:T(8,128)S(1)}, f32[1,64,512]{2,1,0:T(8,128)S(1)}, u32[]{:S(2)}, u32[]{:S(2)}) %collective-permute-start.6) | collective-permute-done | bytes 131104 | tf_op jit(solution)/shard_map/ppermute | solution.py:58
  106.1 0.1 fusion.9
  106.3 1.9 %collective-permute-start.8 = (bf16[3,64,512]{2,1,0:T(8,128)(2,1)S(1)}, bf16[3,64,512]{2,1,0:T(8,128)(2,1)S(1)}, u32[]{:S(2)}, u32[]{:S(2)}) collective-permute-start(bf16[3,64,512]{2,1,0:T(8,128)(2,1)S(1)} %pad_maximum_fusion), channel_id=1, source_target_pairs={{0,1},{1,0},{2,3},{3,2},{4,5},{5,4},{6,7},{7,6},{8,9},{9,8},{10,11... | collective-permute-start | bytes 589832 | tf_op jit(solution)/shard_map/ppermute | solution.py:75
  108.2 1.4 collective-permute-done.8
  109.6 0.1 maximum_select_fusion
  109.7 0.8 fusion.4
  110.5 2.4 %fusion = f32[2048,128]{0,1:T(8,128)S(1)} fusion(f32[128,2048]{1,0:T(8,128)S(1)} %fusion.4, bf16[2048,512]{1,0:T(8,128)(2,1)} %collective-permute-done.4, bf16[3,128,512]{2,1,0:T(8,128)(2,1)S(1)} %maximum_select_fusion), kind=kOutput, calls=%fused_computation.1 | convolution fusion | flops 268697600 | bytes 4325376 | tf_op jit(solution)/shard_map/dot_general | solution.py:30
  113.0 1.9 %collective-permute-start.9 = (f32[2048,128]{0,1:T(8,128)S(1)}, f32[2048,128]{0,1:T(8,128)S(1)}, u32[]{:S(2)}, u32[]{:S(2)}) collective-permute-start(f32[2048,128]{0,1:T(8,128)S(1)} %fusion), channel_id=1, source_target_pairs={{0,6},{6,12},{12,18},{18,24},{24,30},{30,36},{36,42},{42,48},{48,5... | collective-permute-start | bytes 3145736 | tf_op jit(solution)/shard_map/ppermute | solution.py:11
  114.9 30.0 %collective-permute-done.9 = f32[2048,128]{0,1:T(8,128)S(1)} collective-permute-done((f32[2048,128]{0,1:T(8,128)S(1)}, f32[2048,128]{0,1:T(8,128)S(1)}, u32[]{:S(2)}, u32[]{:S(2)}) %collective-permute-start.9) | collective-permute-done | bytes 1048608 | tf_op jit(solution)/shard_map/ppermute | solution.py:11
  144.9 0.8 fusion.5
  145.7 1.3 copy.6
  (4 shorter events, 0.0 us)
Async XLA Ops:
  0.0 24.3 %copy-start = (bf16[2048,512]{1,0:T(8,128)(2,1)S(1)}, bf16[2048,512]{1,0:T(8,128)(2,1)}, u32[]{:S(2)}) copy-start(bf16[2048,512]{1,0:T(8,128)(2,1)} %param.6) | copy-start | bytes 6291460
  0.0 63.7 %collective-permute-start.4 = (bf16[2048,512]{1,0:T(8,128)(2,1)}, bf16[2048,512]{1,0:T(8,128)(2,1)}, u32[]{:S(2)}, u32[]{:S(2)}) collective-permute-start(bf16[2048,512]{1,0:T(8,128)(2,1)} %param.6), channel_id=1, source_target_pairs={{0,6},{6,12},{12,18},{18,24},{24,30},{30,36},{36,42},{42,48},{48,5... | collective-permute-start | bytes 6291464 | tf_op jit(solution)/shard_map/ppermute | solution.py:11
  3.6 20.7 %collective-permute-start = (bf16[2048,128]{1,0:T(8,128)(2,1)}, bf16[2048,128]{1,0:T(8,128)(2,1)S(1)}, u32[]{:S(2)}, u32[]{:S(2)}) collective-permute-start(bf16[2048,128]{1,0:T(8,128)(2,1)} %param.5), channel_id=1, source_target_pairs={{0,762},{6,0},{12,6},{18,12},{24,18},{30,24},{36,30},{42,36},{48,4... | collective-permute-start | bytes 1572872 | tf_op jit(solution)/shard_map/ppermute | solution.py:11
  15.2 12.3 %copy-start.1 = (f32[256]{0:T(256)S(1)}, f32[256]{0:T(256)}, u32[]{:S(2)}) copy-start(f32[256]{0:T(256)} %param.7) | copy-start | bytes 3076
  15.2 12.4 %copy-start.2 = (f32[256]{0:T(256)S(1)}, f32[256]{0:T(256)}, u32[]{:S(2)}) copy-start(f32[256]{0:T(256)} %param.9) | copy-start | bytes 3076
  25.5 3.6 %collective-permute-start.1 = (f32[2,64,512]{2,1,0:T(8,128)}, f32[2,64,512]{2,1,0:T(8,128)S(1)}, u32[]{:S(2)}, u32[]{:S(2)}) collective-permute-start(f32[2,64,512]{2,1,0:T(8,128)} %fusion.1), channel_id=1, source_target_pairs={{0,1},{1,0},{2,3},{3,2},{4,5},{5,4},{6,7},{7,6},{8,9},{9,8},{10,11... | collective-permute-start | bytes 786440 | tf_op jit(solution)/shard_map/ppermute | solution.py:55
  27.6 41.7 %copy-start.3 = (f32[64]{0:T(128)S(1)}, f32[64]{0:T(128)}, u32[]{:S(2)}) copy-start(f32[64]{0:T(128)} %param.8) | copy-start | bytes 772
  29.9 67.1 %collective-permute-start.3 = (f32[2,64,512]{2,1,0:T(8,128)}, f32[2,64,512]{2,1,0:T(8,128)}, u32[]{:S(2)}, u32[]{:S(2)}) collective-permute-start(f32[2,64,512]{2,1,0:T(8,128)} %fusion.3), channel_id=1, source_target_pairs={{0,4},{1,5},{2,0},{3,1},{4,2},{5,3},{6,10},{7,11},{8,6},{9,7},{10,... | collective-permute-start | bytes 786440 | tf_op jit(solution)/shard_map/ppermute | solution.py:58
  42.1 54.9 %collective-permute-start.2 = (f32[2,64,512]{2,1,0:T(8,128)}, f32[2,64,512]{2,1,0:T(8,128)}, u32[]{:S(2)}, u32[]{:S(2)}) collective-permute-start(f32[2,64,512]{2,1,0:T(8,128)} %fusion.3), channel_id=1, source_target_pairs={{0,2},{1,3},{2,4},{3,5},{4,0},{5,1},{6,8},{7,9},{8,10},{9,11},{10,... | collective-permute-start | bytes 786440 | tf_op jit(solution)/shard_map/ppermute | solution.py:58
  67.4 3.2 %collective-permute-start.5 = (f32[1,64,512]{2,1,0:T(8,128)S(1)}, f32[1,64,512]{2,1,0:T(8,128)S(1)}, u32[]{:S(2)}, u32[]{:S(2)}) collective-permute-start(f32[1,64,512]{2,1,0:T(8,128)S(1)} %dynamic-slice_bitcast_fusion), channel_id=1, source_target_pairs={{0,1},{1,0},{2,3},{3,2},{4,5},{5,4},{6,7},{7,6},{8,9},{9,8},{10,11... | collective-permute-start | bytes 393224 | tf_op jit(solution)/shard_map/ppermute | solution.py:55
  71.6 27.8 %collective-permute-start.7 = (f32[1,64,512]{2,1,0:T(8,128)S(1)}, f32[1,64,512]{2,1,0:T(8,128)S(1)}, u32[]{:S(2)}, u32[]{:S(2)}) collective-permute-start(f32[1,64,512]{2,1,0:T(8,128)S(1)} %bitcast_add_fusion), channel_id=1, source_target_pairs={{0,4},{1,5},{2,0},{3,1},{4,2},{5,3},{6,10},{7,11},{8,6},{9,7},{10,... | collective-permute-start | bytes 393224 | tf_op jit(solution)/shard_map/ppermute | solution.py:58
  95.0 11.1 %collective-permute-start.6 = (f32[1,64,512]{2,1,0:T(8,128)S(1)}, f32[1,64,512]{2,1,0:T(8,128)S(1)}, u32[]{:S(2)}, u32[]{:S(2)}) collective-permute-start(f32[1,64,512]{2,1,0:T(8,128)S(1)} %bitcast_add_fusion), channel_id=1, source_target_pairs={{0,2},{1,3},{2,4},{3,5},{4,0},{5,1},{6,8},{7,9},{8,10},{9,11},{10,... | collective-permute-start | bytes 393224 | tf_op jit(solution)/shard_map/ppermute | solution.py:58
  106.3 3.3 %collective-permute-start.8 = (bf16[3,64,512]{2,1,0:T(8,128)(2,1)S(1)}, bf16[3,64,512]{2,1,0:T(8,128)(2,1)S(1)}, u32[]{:S(2)}, u32[]{:S(2)}) collective-permute-start(bf16[3,64,512]{2,1,0:T(8,128)(2,1)S(1)} %pad_maximum_fusion), channel_id=1, source_target_pairs={{0,1},{1,0},{2,3},{3,2},{4,5},{5,4},{6,7},{7,6},{8,9},{9,8},{10,11... | collective-permute-start | bytes 589832 | tf_op jit(solution)/shard_map/ppermute | solution.py:75
  113.0 31.9 %collective-permute-start.9 = (f32[2048,128]{0,1:T(8,128)S(1)}, f32[2048,128]{0,1:T(8,128)S(1)}, u32[]{:S(2)}, u32[]{:S(2)}) collective-permute-start(f32[2048,128]{0,1:T(8,128)S(1)} %fusion), channel_id=1, source_target_pairs={{0,6},{6,12},{12,18},{18,24},{24,30},{30,36},{36,42},{42,48},{48,5... | collective-permute-start | bytes 3145736 | tf_op jit(solution)/shard_map/ppermute | solution.py:11

commit v4 on v3

--- a/solution.py
+++ b/solution.py
@@ -54,28 +54,48 @@
         keep = lax.dynamic_slice_in_dim(stack, core * half, half, 1)
         return keep + lax.ppermute(give, "aux", aux_pairs(aux_size, 1, 0))
 
+    chip = aux_pos // 2
+    piece = -(-half // chips)
+    piece = -(-piece // 8) * 8
+
     def chip_reduce(summed):
-        others = [lax.ppermute(summed, "aux", aux_pairs(aux_size, 0, d)) for d in range(1, chips)]
-        for other in others:
-            summed = summed + other
-        return summed
+        padded = jnp.pad(summed, ((0, 0), (0, piece * chips - half), (0, 0)))
+        parts = padded.reshape(padded.shape[0], chips, piece, padded.shape[2])
+        mine = lax.dynamic_index_in_dim(parts, chip, 1, keepdims=False)
+        for d in range(1, chips):
+            give = lax.dynamic_index_in_dim(parts, (chip + d) % chips, 1, keepdims=False)
+            mine = mine + lax.ppermute(give, "aux", aux_pairs(aux_size, 0, d))
+        return mine
 
-    def amplitude_half(summed, row_shift, col_shift):
+    def chip_gather(mine):
+        whole = jnp.zeros((mine.shape[0], chips, piece, mine.shape[2]), mine.dtype)
+        whole = lax.dynamic_update_index_in_dim(whole, mine, chip, 1)
+        for d in range(1, chips):
+            got = lax.ppermute(mine, "aux", aux_pairs(aux_size, 0, d))
+            whole = lax.dynamic_update_index_in_dim(whole, got, (chip - d) % chips, 1)
+        return whole.reshape(mine.shape[0], chips * piece, mine.shape[2])[:, :half]
+
+    def amplitude_part(summed, row_shift):
         row_energy = lax.dynamic_slice_in_dim(energy(row_shift, eps_va), core * half, half, 0)
-        col_energy = energy(col_shift, eps_vb)
+        row_energy = jnp.pad(row_energy, (0, piece * chips - half), constant_values=1.0)
+        row_energy = lax.dynamic_slice_in_dim(row_energy, chip * piece, piece, 0)
+        col_energy = energy(0, eps_vb)
         return (spin_scale * summed / (row_energy[:, None] + col_energy[None, :])).astype(jnp.bfloat16)
+
+    def core_gather(halves):
+        other = lax.ppermute(halves, "aux", aux_pairs(aux_size, 1, 0))
+        first = jnp.concatenate([halves, other], axis=1)
+        second = jnp.concatenate([other, halves], axis=1)
+        return jnp.where(core == 0, first, second)
 
     cols_prev = shifted(b_cols, "occ", 1)
     rows_next = shifted(b_rows, "occ", -1)
-    early = chip_reduce(core_reduce([partial_integrals(b_rows, b_cols), partial_integrals(rows_next, b_cols)]))
-    late = chip_reduce(core_reduce([partial_integrals(rows_next, cols_prev)]))
-    amp_halves = jnp.stack([
-        amplitude_half(early[0], 0, 0), amplitude_half(early[1], 1, 0), amplitude_half(late[0], 1, -1)
-    ])
-    amp_other = lax.ppermute(amp_halves, "aux", aux_pairs(aux_size, 1, 0))
-    first = jnp.concatenate([amp_halves, amp_other], axis=1)
-    second = jnp.concatenate([amp_other, amp_halves], axis=1)
-    amps = jnp.where(core == 0, first, second)
+    rows_after = shifted(rows_next, "occ", -1)
+    lefts = [b_rows, rows_next, rows_after]
+    summed = chip_reduce(core_reduce([partial_integrals(left, b_cols) for left in lefts]))
+    amp_halves = chip_gather(jnp.stack([amplitude_part(summed[s], s) for s in range(3)]))
+    far = shifted(amp_halves[2], "occ", 1)
+    amps = core_gather(jnp.stack([amp_halves[0], amp_halves[1], far]))
     own = contribution(b_cols, amps[0])
     onward = contribution(b_cols, amps[1]) + contribution(cols_prev, amps[2])
     return own + shifted(onward, "occ", 1)

time: 148 us -> 153 us (1.034)
  the two profiles are of different devices: /device:TPU:4 before, /device:TPU:1 now
where the time goes in v4:
time: 153 us
  waiting for transfers between devices  77.7 us (51%)
  starting transfers between devices  63.2 us (41%)
  matrix products  7.21 us (5%)
  local copies, waits for them, and re-layouts  3.73 us (2%)
    ppermute x5, waiting for transfers between devices, shifted(): lax.ppermute(value, axis, [(i, (i + by) % size) for i in range(size)])  60.9 us
    ppermute x5, starting transfers between devices, shifted(): lax.ppermute(value, axis, [(i, (i + by) % size) for i in range(size)])  29.4 us
    ppermute x2, starting transfers between devices, chip_reduce(): mine = mine + lax.ppermute(give, 'aux', aux_pairs(aux_size, 0, d))  13.5 us
    ppermute x2, starting transfers between devices, chip_gather(): got = lax.ppermute(mine, 'aux', aux_pairs(aux_size, 0, d))  9.82 us
    ppermute x2, waiting for transfers between devices, chip_reduce(): mine = mine + lax.ppermute(give, 'aux', aux_pairs(aux_size, 0, d))  7.46 us
    ppermute x2, waiting for transfers between devices, chip_gather(): got = lax.ppermute(mine, 'aux', aux_pairs(aux_size, 0, d))  7 us
    ppermute x1, starting transfers between devices, core_gather(): other = lax.ppermute(halves, 'aux', aux_pairs(aux_size, 1, 0))  6.16 us
    ppermute x1, starting transfers between devices, core_reduce(): return keep + lax.ppermute(give, 'aux', aux_pairs(aux_size, 1, 0))  4.28 us
  transfers between devices with their start and end apart: 11, of which 9 were waited for; matrix products, arithmetic and copies ran while one was open for 5% of the time, Pallas kernels for 0%

profile of v4, /device:TPU:1, one launch (start us, length us, event | category | flops | bytes accessed | tf_op | source)
XLA Modules:
  0.0 152.7 jit_solution(10411879281093235419)
XLA Ops:
  0.0 13.7 %collective-permute-start = (bf16[2048,128]{1,0:T(8,128)(2,1)}, bf16[2048,128]{1,0:T(8,128)(2,1)S(1)}, u32[]{:S(2)}, u32[]{:S(2)}) collective-permute-start(bf16[2048,128]{1,0:T(8,128)(2,1)} %param.5), channel_id=1, source_target_pairs={{0,762},{6,0},{12,6},{18,12},{24,18},{30,24},{36,30},{42,36},{48,4... | collective-permute-start | bytes 1572872 | tf_op jit(solution)/shard_map/ppermute | solution.py:11
  13.7 1.9 %collective-permute-start.9 = (bf16[2048,512]{1,0:T(8,128)(2,1)}, bf16[2048,512]{1,0:T(8,128)(2,1)}, u32[]{:S(2)}, u32[]{:S(2)}) collective-permute-start(bf16[2048,512]{1,0:T(8,128)(2,1)} %param.6), channel_id=1, source_target_pairs={{0,6},{6,12},{12,18},{18,24},{24,30},{30,36},{36,42},{42,48},{48,5... | collective-permute-start | bytes 6291464 | tf_op jit(solution)/shard_map/ppermute | solution.py:11
  15.6 8.9 %collective-permute-done = bf16[2048,128]{1,0:T(8,128)(2,1)S(1)} collective-permute-done((bf16[2048,128]{1,0:T(8,128)(2,1)}, bf16[2048,128]{1,0:T(8,128)(2,1)S(1)}, u32[]{:S(2)}, u32[]{:S(2)}) %collective-permute-start) | collective-permute-done | bytes 524320 | tf_op jit(solution)/shard_map/ppermute | solution.py:11
  24.6 10.0 %collective-permute-start.1 = (bf16[2048,128]{1,0:T(8,128)(2,1)S(1)}, bf16[2048,128]{1,0:T(8,128)(2,1)S(1)}, u32[]{:S(2)}, u32[]{:S(2)}) collective-permute-start(bf16[2048,128]{1,0:T(8,128)(2,1)S(1)} %collective-permute-done), channel_id=1, source_target_pairs={{0,762},{6,0},{12,6},{18,12},{24,18},{30,24},{36,30},{42,36},{48,4... | collective-permute-start | bytes 1572872 | tf_op jit(solution)/shard_map/ppermute | solution.py:11
  34.6 0.9 fusion.10
  35.5 2.2 %convolution_bitcast_fusion.3 = f32[1,128,512]{2,1,0:T(8,128)S(1)} fusion(bf16[2048,128]{1,0:T(8,128)(2,1)} %param.5, bf16[2048,512]{1,0:T(8,128)(2,1)} %param.6), kind=kOutput, calls=%fused_computation.5 | convolution fusion | flops 268435456 | bytes 2883584 | tf_op jit(solution)/shard_map/dot_general | solution.py:24
  37.7 0.0 copy-done
  37.7 0.5 convolution_bitcast_fusion.2
  38.2 0.0 copy-start.2
  38.2 0.0 copy-start.1
  38.2 6.1 %collective-permute-done.1 = bf16[2048,128]{1,0:T(8,128)(2,1)S(1)} collective-permute-done((bf16[2048,128]{1,0:T(8,128)(2,1)S(1)}, bf16[2048,128]{1,0:T(8,128)(2,1)S(1)}, u32[]{:S(2)}, u32[]{:S(2)}) %collective-permute-start.1) | collective-permute-done | bytes 524320 | tf_op jit(solution)/shard_map/ppermute | solution.py:11
  44.3 0.5 convolution_bitcast_fusion.1
  44.8 0.1 pad_maximum_fusion
  44.9 0.8 constant_dynamic-slice_fusion
  45.6 4.3 %collective-permute-start.2 = (f32[3,64,512]{2,1,0:T(8,128)}, f32[3,64,512]{2,1,0:T(8,128)S(1)}, u32[]{:S(2)}, u32[]{:S(2)}) collective-permute-start(f32[3,64,512]{2,1,0:T(8,128)} %constant_dynamic-slice_fusion), channel_id=1, source_target_pairs={{0,1},{1,0},{2,3},{3,2},{4,5},{5,4},{6,7},{7,6},{8,9},{9,8},{10,11... | collective-permute-start | bytes 1179656 | tf_op jit(solution)/shard_map/ppermute | solution.py:55
  49.9 0.1 broadcast_subtract_fusion.2
  50.0 0.1 sub.99
  50.1 0.1 dynamic_slice.52
  50.2 0.1 subtract_bitcast_fusion
  50.2 1.2 collective-permute-done.2
  51.5 0.1 dynamic-slice_add_fusion
  51.6 10.3 %collective-permute-start.3 = (f32[3,24,512]{2,1,0:T(8,128)S(1)}, f32[3,24,512]{2,1,0:T(8,128)S(1)}, u32[]{:S(2)}, u32[]{:S(2)}) collective-permute-start(f32[3,24,512]{2,1,0:T(8,128)S(1)} %get-tuple-element.5), channel_id=1, source_target_pairs={{0,2},{1,3},{2,4},{3,5},{4,0},{5,1},{6,8},{7,9},{8,10},{9,11},{10,... | collective-permute-start | bytes 442376 | tf_op jit(solution)/shard_map/ppermute | solution.py:67
  61.9 3.2 %collective-permute-start.4 = (f32[3,24,512]{2,1,0:T(8,128)S(1)}, f32[3,24,512]{2,1,0:T(8,128)S(1)}, u32[]{:S(2)}, u32[]{:S(2)}) collective-permute-start(f32[3,24,512]{2,1,0:T(8,128)S(1)} %get-tuple-element.6), channel_id=1, source_target_pairs={{0,4},{1,5},{2,0},{3,1},{4,2},{5,3},{6,10},{7,11},{8,6},{9,7},{10,... | collective-permute-start | bytes 442376 | tf_op jit(solution)/shard_map/ppermute | solution.py:67
  65.1 0.1 pad_dynamic-slice_fusion.2
  65.2 0.1 sub.106
  65.3 0.1 dynamic_slice.55
  65.4 0.1 sub.109
  65.4 0.1 dynamic_slice.58
  65.5 0.1 pad_dynamic-slice_fusion
  65.6 7.2 %collective-permute-done.3 = f32[3,24,512]{2,1,0:T(8,128)S(1)} collective-permute-done((f32[3,24,512]{2,1,0:T(8,128)S(1)}, f32[3,24,512]{2,1,0:T(8,128)S(1)}, u32[]{:S(2)}, u32[]{:S(2)}) %collective-permute-start.3) | collective-permute-done | bytes 147488 | tf_op jit(solution)/shard_map/ppermute | solution.py:67
  72.8 0.2 collective-permute-done.4
  73.1 0.1 fusion.9
  73.2 7.9 %collective-permute-start.5 = (bf16[3,24,512]{2,1,0:T(8,128)(2,1)S(1)}, bf16[3,24,512]{2,1,0:T(8,128)(2,1)S(1)}, u32[]{:S(2)}, u32[]{:S(2)}) collective-permute-start(bf16[3,24,512]{2,1,0:T(8,128)(2,1)S(1)} %pad_maximum_fusion.2), channel_id=1, source_target_pairs={{0,2},{1,3},{2,4},{3,5},{4,0},{5,1},{6,8},{7,9},{8,10},{9,11},{10,... | collective-permute-start | bytes 221192 | tf_op jit(solution)/shard_map/ppermute | solution.py:74
  81.1 1.9 %collective-permute-start.6 = (bf16[3,24,512]{2,1,0:T(8,128)(2,1)S(1)}, bf16[3,24,512]{2,1,0:T(8,128)(2,1)S(1)}, u32[]{:S(2)}, u32[]{:S(2)}) collective-permute-start(bf16[3,24,512]{2,1,0:T(8,128)(2,1)S(1)} %pad_maximum_fusion.2), channel_id=1, source_target_pairs={{0,4},{1,5},{2,0},{3,1},{4,2},{5,3},{6,10},{7,11},{8,6},{9,7},{10,... | collective-permute-start | bytes 221192 | tf_op jit(solution)/shard_map/ppermute | solution.py:74
  83.1 0.0 collective-permute-done.5
  83.1 7.0 %collective-permute-done.6 = bf16[3,24,512]{2,1,0:T(8,128)(2,1)S(1)} collective-permute-done((bf16[3,24,512]{2,1,0:T(8,128)(2,1)S(1)}, bf16[3,24,512]{2,1,0:T(8,128)(2,1)S(1)}, u32[]{:S(2)}, u32[]{:S(2)}) %collective-permute-start.6) | collective-permute-done | bytes 73760 | tf_op jit(solution)/shard_map/ppermute | solution.py:74
  90.2 1.9 %collective-permute-start.7 = (bf16[64,512]{1,0:T(8,128)(2,1)S(1)}, bf16[64,512]{1,0:T(8,128)(2,1)S(1)}, u32[]{:S(2)}, u32[]{:S(2)}) collective-permute-start(bf16[64,512]{1,0:T(8,128)(2,1)S(1)} %slice_bitcast_fusion.8), channel_id=1, source_target_pairs={{0,6},{6,12},{12,18},{18,24},{24,30},{30,36},{36,42},{42,48},{48,5... | collective-permute-start | bytes 196616 | tf_op jit(solution)/shard_map/ppermute | solution.py:11
  92.1 15.6 %collective-permute-done.7 = bf16[64,512]{1,0:T(8,128)(2,1)S(1)} collective-permute-done((bf16[64,512]{1,0:T(8,128)(2,1)S(1)}, bf16[64,512]{1,0:T(8,128)(2,1)S(1)}, u32[]{:S(2)}, u32[]{:S(2)}) %collective-permute-start.7) | collective-permute-done | bytes 65568 | tf_op jit(solution)/shard_map/ppermute | solution.py:11
  107.7 6.2 %collective-permute-start.8 = (bf16[3,64,512]{2,1,0:T(8,128)(2,1)S(1)}, bf16[3,64,512]{2,1,0:T(8,128)(2,1)S(1)}, u32[]{:S(2)}, u32[]{:S(2)}) collective-permute-start(bf16[3,64,512]{2,1,0:T(8,128)(2,1)S(1)} %pad_maximum_fusion.1), channel_id=1, source_target_pairs={{0,1},{1,0},{2,3},{3,2},{4,5},{5,4},{6,7},{7,6},{8,9},{9,8},{10,11... | collective-permute-start | bytes 589832 | tf_op jit(solution)/shard_map/ppermute | solution.py:86
  113.9 1.0 collective-permute-done.8
  114.9 0.1 maximum_select_fusion
  115.1 0.8 fusion.2
  115.9 0.0 collective-permute-done.9
  115.9 2.4 %fusion = f32[2048,128]{0,1:T(8,128)S(1)} fusion(f32[128,2048]{1,0:T(8,128)S(1)} %fusion.2, bf16[2048,512]{1,0:T(8,128)(2,1)} %collective-permute-done.9, bf16[3,128,512]{2,1,0:T(8,128)(2,1)S(1)} %maximum_select_fusion), kind=kOutput, calls=%fused_computation.1 | convolution fusion | flops 268697600 | bytes 4325376 | tf_op jit(solution)/shard_map/dot_general | solution.py:30
  118.3 1.9 %collective-permute-start.10 = (f32[2048,128]{0,1:T(8,128)S(1)}, f32[2048,128]{0,1:T(8,128)S(1)}, u32[]{:S(2)}, u32[]{:S(2)}) collective-permute-start(f32[2048,128]{0,1:T(8,128)S(1)} %fusion), channel_id=1, source_target_pairs={{0,6},{6,12},{12,18},{18,24},{24,30},{30,36},{36,42},{42,48},{48,5... | collective-permute-start | bytes 3145736 | tf_op jit(solution)/shard_map/ppermute | solution.py:11
  120.2 30.3 %collective-permute-done.10 = f32[2048,128]{0,1:T(8,128)S(1)} collective-permute-done((f32[2048,128]{0,1:T(8,128)S(1)}, f32[2048,128]{0,1:T(8,128)S(1)}, u32[]{:S(2)}, u32[]{:S(2)}) %collective-permute-start.10) | collective-permute-done | bytes 1048608 | tf_op jit(solution)/shard_map/ppermute | solution.py:11
  150.6 0.8 fusion.3
  151.4 1.3 copy.9
  (15 shorter events, 0.2 us)
Async XLA Ops:
  0.0 37.7 %copy-start = (bf16[2048,512]{1,0:T(8,128)(2,1)S(1)}, bf16[2048,512]{1,0:T(8,128)(2,1)}, u32[]{:S(2)}) copy-start(bf16[2048,512]{1,0:T(8,128)(2,1)} %param.6) | copy-start | bytes 6291460
  0.0 24.6 %collective-permute-start = (bf16[2048,128]{1,0:T(8,128)(2,1)}, bf16[2048,128]{1,0:T(8,128)(2,1)S(1)}, u32[]{:S(2)}, u32[]{:S(2)}) collective-permute-start(bf16[2048,128]{1,0:T(8,128)(2,1)} %param.5), channel_id=1, source_target_pairs={{0,762},{6,0},{12,6},{18,12},{24,18},{30,24},{36,30},{42,36},{48,4... | collective-permute-start | bytes 1572872 | tf_op jit(solution)/shard_map/ppermute | solution.py:11
  13.7 102.2 %collective-permute-start.9 = (bf16[2048,512]{1,0:T(8,128)(2,1)}, bf16[2048,512]{1,0:T(8,128)(2,1)}, u32[]{:S(2)}, u32[]{:S(2)}) collective-permute-start(bf16[2048,512]{1,0:T(8,128)(2,1)} %param.6), channel_id=1, source_target_pairs={{0,6},{6,12},{12,18},{18,24},{24,30},{30,36},{36,42},{42,48},{48,5... | collective-permute-start | bytes 6291464 | tf_op jit(solution)/shard_map/ppermute | solution.py:11
  24.6 19.7 %collective-permute-start.1 = (bf16[2048,128]{1,0:T(8,128)(2,1)S(1)}, bf16[2048,128]{1,0:T(8,128)(2,1)S(1)}, u32[]{:S(2)}, u32[]{:S(2)}) collective-permute-start(bf16[2048,128]{1,0:T(8,128)(2,1)S(1)} %collective-permute-done), channel_id=1, source_target_pairs={{0,762},{6,0},{12,6},{18,12},{24,18},{30,24},{36,30},{42,36},{48,4... | collective-permute-start | bytes 1572872 | tf_op jit(solution)/shard_map/ppermute | solution.py:11
  38.2 11.7 %copy-start.2 = (f32[64]{0:T(128)S(1)}, f32[64]{0:T(128)}, u32[]{:S(2)}) copy-start(f32[64]{0:T(128)} %param.8) | copy-start | bytes 772
  38.2 11.9 %copy-start.1 = (f32[256]{0:T(256)S(1)}, f32[256]{0:T(256)}, u32[]{:S(2)}) copy-start(f32[256]{0:T(256)} %param.9) | copy-start | bytes 3076
  45.6 5.8 %collective-permute-start.2 = (f32[3,64,512]{2,1,0:T(8,128)}, f32[3,64,512]{2,1,0:T(8,128)S(1)}, u32[]{:S(2)}, u32[]{:S(2)}) collective-permute-start(f32[3,64,512]{2,1,0:T(8,128)} %constant_dynamic-slice_fusion), channel_id=1, source_target_pairs={{0,1},{1,0},{2,3},{3,2},{4,5},{5,4},{6,7},{7,6},{8,9},{9,8},{10,11... | collective-permute-start | bytes 1179656 | tf_op jit(solution)/shard_map/ppermute | solution.py:55
  51.6 21.2 %collective-permute-start.3 = (f32[3,24,512]{2,1,0:T(8,128)S(1)}, f32[3,24,512]{2,1,0:T(8,128)S(1)}, u32[]{:S(2)}, u32[]{:S(2)}) collective-permute-start(f32[3,24,512]{2,1,0:T(8,128)S(1)} %get-tuple-element.5), channel_id=1, source_target_pairs={{0,2},{1,3},{2,4},{3,5},{4,0},{5,1},{6,8},{7,9},{8,10},{9,11},{10,... | collective-permute-start | bytes 442376 | tf_op jit(solution)/shard_map/ppermute | solution.py:67
  61.9 11.1 %collective-permute-start.4 = (f32[3,24,512]{2,1,0:T(8,128)S(1)}, f32[3,24,512]{2,1,0:T(8,128)S(1)}, u32[]{:S(2)}, u32[]{:S(2)}) collective-permute-start(f32[3,24,512]{2,1,0:T(8,128)S(1)} %get-tuple-element.6), channel_id=1, source_target_pairs={{0,4},{1,5},{2,0},{3,1},{4,2},{5,3},{6,10},{7,11},{8,6},{9,7},{10,... | collective-permute-start | bytes 442376 | tf_op jit(solution)/shard_map/ppermute | solution.py:67
  73.2 9.9 %collective-permute-start.5 = (bf16[3,24,512]{2,1,0:T(8,128)(2,1)S(1)}, bf16[3,24,512]{2,1,0:T(8,128)(2,1)S(1)}, u32[]{:S(2)}, u32[]{:S(2)}) collective-permute-start(bf16[3,24,512]{2,1,0:T(8,128)(2,1)S(1)} %pad_maximum_fusion.2), channel_id=1, source_target_pairs={{0,2},{1,3},{2,4},{3,5},{4,0},{5,1},{6,8},{7,9},{8,10},{9,11},{10,... | collective-permute-start | bytes 221192 | tf_op jit(solution)/shard_map/ppermute | solution.py:74
  81.1 9.0 %collective-permute-start.6 = (bf16[3,24,512]{2,1,0:T(8,128)(2,1)S(1)}, bf16[3,24,512]{2,1,0:T(8,128)(2,1)S(1)}, u32[]{:S(2)}, u32[]{:S(2)}) collective-permute-start(bf16[3,24,512]{2,1,0:T(8,128)(2,1)S(1)} %pad_maximum_fusion.2), channel_id=1, source_target_pairs={{0,4},{1,5},{2,0},{3,1},{4,2},{5,3},{6,10},{7,11},{8,6},{9,7},{10,... | collective-permute-start | bytes 221192 | tf_op jit(solution)/shard_map/ppermute | solution.py:74
  90.2 17.5 %collective-permute-start.7 = (bf16[64,512]{1,0:T(8,128)(2,1)S(1)}, bf16[64,512]{1,0:T(8,128)(2,1)S(1)}, u32[]{:S(2)}, u32[]{:S(2)}) collective-permute-start(bf16[64,512]{1,0:T(8,128)(2,1)S(1)} %slice_bitcast_fusion.8), channel_id=1, source_target_pairs={{0,6},{6,12},{12,18},{18,24},{24,30},{30,36},{36,42},{42,48},{48,5... | collective-permute-start | bytes 196616 | tf_op jit(solution)/shard_map/ppermute | solution.py:11
  107.7 7.2 %collective-permute-start.8 = (bf16[3,64,512]{2,1,0:T(8,128)(2,1)S(1)}, bf16[3,64,512]{2,1,0:T(8,128)(2,1)S(1)}, u32[]{:S(2)}, u32[]{:S(2)}) collective-permute-start(bf16[3,64,512]{2,1,0:T(8,128)(2,1)S(1)} %pad_maximum_fusion.1), channel_id=1, source_target_pairs={{0,1},{1,0},{2,3},{3,2},{4,5},{5,4},{6,7},{7,6},{8,9},{9,8},{10,11... | collective-permute-start | bytes 589832 | tf_op jit(solution)/shard_map/ppermute | solution.py:86
  118.3 32.3 %collective-permute-start.10 = (f32[2048,128]{0,1:T(8,128)S(1)}, f32[2048,128]{0,1:T(8,128)S(1)}, u32[]{:S(2)}, u32[]{:S(2)}) collective-permute-start(f32[2048,128]{0,1:T(8,128)S(1)} %fusion), channel_id=1, source_target_pairs={{0,6},{6,12},{12,18},{18,24},{24,30},{30,36},{36,42},{42,48},{48,5... | collective-permute-start | bytes 3145736 | tf_op jit(solution)/shard_map/ppermute | solution.py:11

commit v5 on v4

--- a/solution.py
+++ b/solution.py
@@ -88,14 +88,24 @@
         second = jnp.concatenate([other, halves], axis=1)
         return jnp.where(core == 0, first, second)
 
+    def chip_exchange(summed):
+        others = [lax.ppermute(summed, "aux", aux_pairs(aux_size, 0, d)) for d in range(1, chips)]
+        for other in others:
+            summed = summed + other
+        return summed
+
+    def amplitude_half(summed, row_shift, col_shift):
+        row_energy = lax.dynamic_slice_in_dim(energy(row_shift, eps_va), core * half, half, 0)
+        col_energy = energy(col_shift, eps_vb)
+        return (spin_scale * summed / (row_energy[:, None] + col_energy[None, :])).astype(jnp.bfloat16)
+
     cols_prev = shifted(b_cols, "occ", 1)
     rows_next = shifted(b_rows, "occ", -1)
-    rows_after = shifted(rows_next, "occ", -1)
-    lefts = [b_rows, rows_next, rows_after]
-    summed = chip_reduce(core_reduce([partial_integrals(left, b_cols) for left in lefts]))
-    amp_halves = chip_gather(jnp.stack([amplitude_part(summed[s], s) for s in range(3)]))
-    far = shifted(amp_halves[2], "occ", 1)
-    amps = core_gather(jnp.stack([amp_halves[0], amp_halves[1], far]))
+    early = chip_reduce(core_reduce([partial_integrals(b_rows, b_cols), partial_integrals(rows_next, b_cols)]))
+    early_amps = chip_gather(jnp.stack([amplitude_part(early[0], 0), amplitude_part(early[1], 1)]))
+    late = chip_exchange(core_reduce([partial_integrals(rows_next, cols_prev)]))
+    amp_halves = jnp.concatenate([early_amps, amplitude_half(late[0], 1, -1)[None]])
+    amps = core_gather(amp_halves)
     own = contribution(b_cols, amps[0])
     onward = contribution(b_cols, amps[1]) + contribution(cols_prev, amps[2])
     return own + shifted(onward, "occ", 1)

time: 153 us -> 154 us (level)
  starting transfers between devices: 63.2 us -> 68.9 us
  waiting for transfers between devices: 77.7 us -> 72.4 us
  local copies, waits for them, and re-layouts: 3.73 us -> 1.92 us
  matrix products: 7.21 us -> 8.81 us
    ppermute x0 -> x2, starting transfers between devices: none -> 17 us  [chip_exchange(): lax.ppermute(summed, 'aux', aux_pairs(aux_size, 0, d))]
    ppermute x5 -> x3, starting transfers between devices: 29.4 us -> 17.5 us  [shifted(): lax.ppermute(value, axis, [(i, (i + by) % size) for i in range(size)])]
    ppermute x0 -> x2, waiting for transfers between devices: none -> 8.24 us  [chip_exchange(): lax.ppermute(summed, 'aux', aux_pairs(aux_size, 0, d))]
    ppermute x5 -> x3, waiting for transfers between devices: 60.9 us -> 53 us  [shifted(): lax.ppermute(value, axis, [(i, (i + by) % size) for i in range(size)])]
    ppermute x2, waiting for transfers between devices: 7 us -> 0.01 us  [chip_gather(): got = lax.ppermute(mine, 'aux', aux_pairs(aux_size, 0, d))]
    ppermute x1 -> x2, starting transfers between devices: 4.28 us -> 8.25 us  [core_reduce(): return keep + lax.ppermute(give, 'aux', aux_pairs(aux_size, 1, 0))]
    ppermute x1, starting transfers between devices: 6.16 us -> 3.41 us  [core_gather(): other = lax.ppermute(halves, 'aux', aux_pairs(aux_size, 1, 0))]
    dot_general x3, matrix products: 3.17 us -> 4.75 us  [partial_integrals(): lax.dot_general(left_block, right_block, (((0,), (0,)), ((), ())), prefer...]
  transfers between devices with their start and end apart: 11 -> 12, of which waited for: 9 -> 10; matrix products, arithmetic and copies ran while one was open for 5% -> 4% of each run, Pallas kernels for 0% -> 0%
where the time goes in v5:
time: 154 us
  waiting for transfers between devices  72.4 us (47%)
  starting transfers between devices  68.9 us (45%)
  matrix products  8.81 us (6%)
  local copies, waits for them, and re-layouts  1.92 us (1%)
    ppermute x3, waiting for transfers between devices, shifted(): lax.ppermute(value, axis, [(i, (i + by) % size) for i in range(size)])  53 us
    ppermute x3, starting transfers between devices, shifted(): lax.ppermute(value, axis, [(i, (i + by) % size) for i in range(size)])  17.5 us
    ppermute x2, starting transfers between devices, chip_exchange(): lax.ppermute(summed, 'aux', aux_pairs(aux_size, 0, d))  17 us
    ppermute x2, starting transfers between devices, chip_reduce(): mine = mine + lax.ppermute(give, 'aux', aux_pairs(aux_size, 0, d))  13.5 us
    ppermute x2, starting transfers between devices, chip_gather(): got = lax.ppermute(mine, 'aux', aux_pairs(aux_size, 0, d))  9.19 us
    ppermute x2, waiting for transfers between devices, chip_reduce(): mine = mine + lax.ppermute(give, 'aux', aux_pairs(aux_size, 0, d))  8.35 us
    ppermute x2, starting transfers between devices, core_reduce(): return keep + lax.ppermute(give, 'aux', aux_pairs(aux_size, 1, 0))  8.25 us
    ppermute x2, waiting for transfers between devices, chip_exchange(): lax.ppermute(summed, 'aux', aux_pairs(aux_size, 0, d))  8.24 us
  transfers between devices with their start and end apart: 12, of which 10 were waited for; matrix products, arithmetic and copies ran while one was open for 4% of the time, Pallas kernels for 0%

profile of v5, /device:TPU:1, one launch (start us, length us, event | category | flops | bytes accessed | tf_op | source)
XLA Modules:
  0.0 153.7 jit_solution(15538211843738250657)
XLA Ops:
  0.0 13.7 %collective-permute-start = (bf16[2048,128]{1,0:T(8,128)(2,1)}, bf16[2048,128]{1,0:T(8,128)(2,1)S(1)}, u32[]{:S(2)}, u32[]{:S(2)}) collective-permute-start(bf16[2048,128]{1,0:T(8,128)(2,1)} %param.5), channel_id=1, source_target_pairs={{0,762},{6,0},{12,6},{18,12},{24,18},{30,24},{36,30},{42,36},{48,4... | collective-permute-start | bytes 1572872 | tf_op jit(solution)/shard_map/ppermute | solution.py:11
  13.7 1.9 %collective-permute-start.6 = (bf16[2048,512]{1,0:T(8,128)(2,1)}, bf16[2048,512]{1,0:T(8,128)(2,1)}, u32[]{:S(2)}, u32[]{:S(2)}) collective-permute-start(bf16[2048,512]{1,0:T(8,128)(2,1)} %param.6), channel_id=1, source_target_pairs={{0,6},{6,12},{12,18},{18,24},{24,30},{30,36},{36,42},{42,48},{48,5... | collective-permute-start | bytes 6291464 | tf_op jit(solution)/shard_map/ppermute | solution.py:11
  15.6 2.2 %convolution_bitcast_fusion.2 = f32[1,128,512]{2,1,0:T(8,128)S(1)} fusion(bf16[2048,128]{1,0:T(8,128)(2,1)} %param.5, bf16[2048,512]{1,0:T(8,128)(2,1)} %param.6), kind=kOutput, calls=%fused_computation.4 | convolution fusion | flops 268435456 | bytes 2883584 | tf_op jit(solution)/shard_map/dot_general | solution.py:24
  17.8 0.0 copy-start.3
  17.8 0.0 copy-start.2
  17.9 0.0 copy-done.1
  18.0 0.1 fusion.11
  18.0 6.5 %collective-permute-done = bf16[2048,128]{1,0:T(8,128)(2,1)S(1)} collective-permute-done((bf16[2048,128]{1,0:T(8,128)(2,1)}, bf16[2048,128]{1,0:T(8,128)(2,1)S(1)}, u32[]{:S(2)}, u32[]{:S(2)}) %collective-permute-start) | collective-permute-done | bytes 524320 | tf_op jit(solution)/shard_map/ppermute | solution.py:11
  24.6 0.0 copy-done
  24.6 0.5 convolution_bitcast_fusion.1
  25.0 0.7 fusion.1
  25.8 3.4 %collective-permute-start.1 = (f32[2,64,512]{2,1,0:T(8,128)}, f32[2,64,512]{2,1,0:T(8,128)S(1)}, u32[]{:S(2)}, u32[]{:S(2)}) collective-permute-start(f32[2,64,512]{2,1,0:T(8,128)} %fusion.1), channel_id=1, source_target_pairs={{0,1},{1,0},{2,3},{3,2},{4,5},{5,4},{6,7},{7,6},{8,9},{9,8},{10,11... | collective-permute-start | bytes 786440 | tf_op jit(solution)/shard_map/ppermute | solution.py:55
  29.2 0.0 copy-done.3
  29.2 0.1 broadcast_subtract_fusion.1
  29.4 0.1 sub.103
  29.4 0.1 sub.110
  29.5 0.1 dynamic_slice.53
  29.6 0.1 dynamic_slice.56
  29.7 0.1 subtract_bitcast_fusion.1
  29.7 0.8 collective-permute-done.1
  30.7 10.3 %collective-permute-start.2 = (f32[2,24,512]{2,1,0:T(8,128)S(1)}, f32[2,24,512]{2,1,0:T(8,128)S(1)}, u32[]{:S(2)}, u32[]{:S(2)}) collective-permute-start(f32[2,24,512]{2,1,0:T(8,128)S(1)} %get-tuple-element.5), channel_id=1, source_target_pairs={{0,2},{1,3},{2,4},{3,5},{4,0},{5,1},{6,8},{7,9},{8,10},{9,11},{10,... | collective-permute-start | bytes 294920 | tf_op jit(solution)/shard_map/ppermute | solution.py:67
  41.0 3.2 %collective-permute-start.3 = (f32[2,24,512]{2,1,0:T(8,128)S(1)}, f32[2,24,512]{2,1,0:T(8,128)S(1)}, u32[]{:S(2)}, u32[]{:S(2)}) collective-permute-start(f32[2,24,512]{2,1,0:T(8,128)S(1)} %get-tuple-element.6), channel_id=1, source_target_pairs={{0,4},{1,5},{2,0},{3,1},{4,2},{5,3},{6,10},{7,11},{8,6},{9,7},{10,... | collective-permute-start | bytes 294920 | tf_op jit(solution)/shard_map/ppermute | solution.py:67
  44.2 0.1 pad_dynamic-slice_fusion.4
  44.3 6.4 %collective-permute-done.2 = f32[2,24,512]{2,1,0:T(8,128)S(1)} collective-permute-done((f32[2,24,512]{2,1,0:T(8,128)S(1)}, f32[2,24,512]{2,1,0:T(8,128)S(1)}, u32[]{:S(2)}, u32[]{:S(2)}) %collective-permute-start.2) | collective-permute-done | bytes 98336 | tf_op jit(solution)/shard_map/ppermute | solution.py:67
  50.7 2.0 %collective-permute-done.3 = f32[2,24,512]{2,1,0:T(8,128)S(1)} collective-permute-done((f32[2,24,512]{2,1,0:T(8,128)S(1)}, f32[2,24,512]{2,1,0:T(8,128)S(1)}, u32[]{:S(2)}, u32[]{:S(2)}) %collective-permute-start.3) | collective-permute-done | bytes 98336 | tf_op jit(solution)/shard_map/ppermute | solution.py:67
  52.6 0.1 fusion.10
  52.7 6.9 %collective-permute-start.4 = (bf16[2,24,512]{2,1,0:T(8,128)(2,1)S(1)}, bf16[2,24,512]{2,1,0:T(8,128)(2,1)S(1)}, u32[]{:S(2)}, u32[]{:S(2)}) collective-permute-start(bf16[2,24,512]{2,1,0:T(8,128)(2,1)S(1)} %pad_maximum_fusion.1), channel_id=1, source_target_pairs={{0,2},{1,3},{2,4},{3,5},{4,0},{5,1},{6,8},{7,9},{8,10},{9,11},{10,... | collective-permute-start | bytes 147464 | tf_op jit(solution)/shard_map/ppermute | solution.py:74
  59.6 2.3 %collective-permute-start.5 = (bf16[2,24,512]{2,1,0:T(8,128)(2,1)S(1)}, bf16[2,24,512]{2,1,0:T(8,128)(2,1)S(1)}, u32[]{:S(2)}, u32[]{:S(2)}) collective-permute-start(bf16[2,24,512]{2,1,0:T(8,128)(2,1)S(1)} %pad_maximum_fusion.1), channel_id=1, source_target_pairs={{0,4},{1,5},{2,0},{3,1},{4,2},{5,3},{6,10},{7,11},{8,6},{9,7},{10,... | collective-permute-start | bytes 147464 | tf_op jit(solution)/shard_map/ppermute | solution.py:74
  62.0 8.9 %collective-permute-done.6 = bf16[2048,512]{1,0:T(8,128)(2,1)} collective-permute-done((bf16[2048,512]{1,0:T(8,128)(2,1)}, bf16[2048,512]{1,0:T(8,128)(2,1)}, u32[]{:S(2)}, u32[]{:S(2)}) %collective-permute-start.6) | collective-permute-done | bytes 2097184 | tf_op jit(solution)/shard_map/ppermute | solution.py:11
  70.9 2.1 %fusion.12 = f32[128,512]{1,0:T(8,128)S(1)} fusion(bf16[2048,128]{1,0:T(8,128)(2,1)S(1)} %collective-permute-done, bf16[2048,512]{1,0:T(8,128)(2,1)} %collective-permute-done.6), kind=kOutput, calls=%fused_computation.43 | convolution fusion | flops 268435456 | bytes 2883584 | tf_op jit(solution)/shard_map/dot_general | solution.py:24
  73.0 4.8 %collective-permute-start.7 = (f32[1,64,512]{2,1,0:T(8,128)S(1)}, f32[1,64,512]{2,1,0:T(8,128)S(1)}, u32[]{:S(2)}, u32[]{:S(2)}) collective-permute-start(f32[1,64,512]{2,1,0:T(8,128)S(1)} %dynamic-slice_bitcast_fusion), channel_id=1, source_target_pairs={{0,1},{1,0},{2,3},{3,2},{4,5},{5,4},{6,7},{7,6},{8,9},{9,8},{10,11... | collective-permute-start | bytes 393224 | tf_op jit(solution)/shard_map/ppermute | solution.py:55
  77.8 0.0 collective-permute-done.4
  77.8 0.9 collective-permute-done.7
  78.8 15.1 %collective-permute-start.9 = (f32[1,64,512]{2,1,0:T(8,128)S(1)}, f32[1,64,512]{2,1,0:T(8,128)S(1)}, u32[]{:S(2)}, u32[]{:S(2)}) collective-permute-start(f32[1,64,512]{2,1,0:T(8,128)S(1)} %bitcast_add_fusion), channel_id=1, source_target_pairs={{0,4},{1,5},{2,0},{3,1},{4,2},{5,3},{6,10},{7,11},{8,6},{9,7},{10,... | collective-permute-start | bytes 393224 | tf_op jit(solution)/shard_map/ppermute | solution.py:92
  93.9 1.9 %collective-permute-start.8 = (f32[1,64,512]{2,1,0:T(8,128)S(1)}, f32[1,64,512]{2,1,0:T(8,128)S(1)}, u32[]{:S(2)}, u32[]{:S(2)}) collective-permute-start(f32[1,64,512]{2,1,0:T(8,128)S(1)} %bitcast_add_fusion), channel_id=1, source_target_pairs={{0,2},{1,3},{2,4},{3,5},{4,0},{5,1},{6,8},{7,9},{8,10},{9,11},{10,... | collective-permute-start | bytes 393224 | tf_op jit(solution)/shard_map/ppermute | solution.py:92
  95.8 0.0 collective-permute-done.5
  95.9 3.3 %collective-permute-done.9 = f32[1,64,512]{2,1,0:T(8,128)S(1)} collective-permute-done((f32[1,64,512]{2,1,0:T(8,128)S(1)}, f32[1,64,512]{2,1,0:T(8,128)S(1)}, u32[]{:S(2)}, u32[]{:S(2)}) %collective-permute-start.9) | collective-permute-done | bytes 131104 | tf_op jit(solution)/shard_map/ppermute | solution.py:92
  99.2 4.9 %collective-permute-done.8 = f32[1,64,512]{2,1,0:T(8,128)S(1)} collective-permute-done((f32[1,64,512]{2,1,0:T(8,128)S(1)}, f32[1,64,512]{2,1,0:T(8,128)S(1)}, u32[]{:S(2)}, u32[]{:S(2)}) %collective-permute-start.8) | collective-permute-done | bytes 131104 | tf_op jit(solution)/shard_map/ppermute | solution.py:92
  104.1 0.1 divide_convert_fusion
  104.2 3.4 %collective-permute-start.10 = (bf16[3,64,512]{2,1,0:T(8,128)(2,1)S(1)}, bf16[3,64,512]{2,1,0:T(8,128)(2,1)S(1)}, u32[]{:S(2)}, u32[]{:S(2)}) collective-permute-start(bf16[3,64,512]{2,1,0:T(8,128)(2,1)S(1)} %pad_maximum_fusion), channel_id=1, source_target_pairs={{0,1},{1,0},{2,3},{3,2},{4,5},{5,4},{6,7},{7,6},{8,9},{9,8},{10,11... | collective-permute-start | bytes 589832 | tf_op jit(solution)/shard_map/ppermute | solution.py:86
  107.7 1.0 collective-permute-done.10
  108.7 0.1 maximum_select_fusion
  108.8 0.8 fusion.4
  109.6 2.4 %fusion = f32[2048,128]{0,1:T(8,128)S(1)} fusion(f32[128,2048]{1,0:T(8,128)S(1)} %fusion.4, bf16[2048,512]{1,0:T(8,128)(2,1)} %collective-permute-done.6, bf16[3,128,512]{2,1,0:T(8,128)(2,1)S(1)} %maximum_select_fusion), kind=kOutput, calls=%fused_computation.1 | convolution fusion | flops 268697600 | bytes 4325376 | tf_op jit(solution)/shard_map/dot_general | solution.py:30
  112.1 1.9 %collective-permute-start.11 = (f32[2048,128]{0,1:T(8,128)S(1)}, f32[2048,128]{0,1:T(8,128)S(1)}, u32[]{:S(2)}, u32[]{:S(2)}) collective-permute-start(f32[2048,128]{0,1:T(8,128)S(1)} %fusion), channel_id=1, source_target_pairs={{0,6},{6,12},{12,18},{18,24},{24,30},{30,36},{36,42},{42,48},{48,5... | collective-permute-start | bytes 3145736 | tf_op jit(solution)/shard_map/ppermute | solution.py:11
  114.0 37.6 %collective-permute-done.11 = f32[2048,128]{0,1:T(8,128)S(1)} collective-permute-done((f32[2048,128]{0,1:T(8,128)S(1)}, f32[2048,128]{0,1:T(8,128)S(1)}, u32[]{:S(2)}, u32[]{:S(2)}) %collective-permute-start.11) | collective-permute-done | bytes 1048608 | tf_op jit(solution)/shard_map/ppermute | solution.py:11
  151.6 0.8 fusion.5
  152.4 1.3 copy.9
  (18 shorter events, 0.2 us)
Async XLA Ops:
  0.0 24.6 %copy-start = (bf16[2048,512]{1,0:T(8,128)(2,1)S(1)}, bf16[2048,512]{1,0:T(8,128)(2,1)}, u32[]{:S(2)}) copy-start(bf16[2048,512]{1,0:T(8,128)(2,1)} %param.6) | copy-start | bytes 6291460
  0.0 17.9 %copy-start.1 = (f32[256]{0:T(256)S(1)}, f32[256]{0:T(256)}, u32[]{:S(2)}) copy-start(f32[256]{0:T(256)} %param.7) | copy-start | bytes 3076
  0.0 24.6 %collective-permute-start = (bf16[2048,128]{1,0:T(8,128)(2,1)}, bf16[2048,128]{1,0:T(8,128)(2,1)S(1)}, u32[]{:S(2)}, u32[]{:S(2)}) collective-permute-start(bf16[2048,128]{1,0:T(8,128)(2,1)} %param.5), channel_id=1, source_target_pairs={{0,762},{6,0},{12,6},{18,12},{24,18},{30,24},{36,30},{42,36},{48,4... | collective-permute-start | bytes 1572872 | tf_op jit(solution)/shard_map/ppermute | solution.py:11
  13.7 57.2 %collective-permute-start.6 = (bf16[2048,512]{1,0:T(8,128)(2,1)}, bf16[2048,512]{1,0:T(8,128)(2,1)}, u32[]{:S(2)}, u32[]{:S(2)}) collective-permute-start(bf16[2048,512]{1,0:T(8,128)(2,1)} %param.6), channel_id=1, source_target_pairs={{0,6},{6,12},{12,18},{18,24},{24,30},{30,36},{36,42},{42,48},{48,5... | collective-permute-start | bytes 6291464 | tf_op jit(solution)/shard_map/ppermute | solution.py:11
  17.8 11.4 %copy-start.3 = (f32[64]{0:T(128)S(1)}, f32[64]{0:T(128)}, u32[]{:S(2)}) copy-start(f32[64]{0:T(128)} %param.8) | copy-start | bytes 772
  17.8 11.8 %copy-start.2 = (f32[256]{0:T(256)S(1)}, f32[256]{0:T(256)}, u32[]{:S(2)}) copy-start(f32[256]{0:T(256)} %param.9) | copy-start | bytes 3076
  25.8 4.8 %collective-permute-start.1 = (f32[2,64,512]{2,1,0:T(8,128)}, f32[2,64,512]{2,1,0:T(8,128)S(1)}, u32[]{:S(2)}, u32[]{:S(2)}) collective-permute-start(f32[2,64,512]{2,1,0:T(8,128)} %fusion.1), channel_id=1, source_target_pairs={{0,1},{1,0},{2,3},{3,2},{4,5},{5,4},{6,7},{7,6},{8,9},{9,8},{10,11... | collective-permute-start | bytes 786440 | tf_op jit(solution)/shard_map/ppermute | solution.py:55
  30.7 20.0 %collective-permute-start.2 = (f32[2,24,512]{2,1,0:T(8,128)S(1)}, f32[2,24,512]{2,1,0:T(8,128)S(1)}, u32[]{:S(2)}, u32[]{:S(2)}) collective-permute-start(f32[2,24,512]{2,1,0:T(8,128)S(1)} %get-tuple-element.5), channel_id=1, source_target_pairs={{0,2},{1,3},{2,4},{3,5},{4,0},{5,1},{6,8},{7,9},{8,10},{9,11},{10,... | collective-permute-start | bytes 294920 | tf_op jit(solution)/shard_map/ppermute | solution.py:67
  41.0 11.6 %collective-permute-start.3 = (f32[2,24,512]{2,1,0:T(8,128)S(1)}, f32[2,24,512]{2,1,0:T(8,128)S(1)}, u32[]{:S(2)}, u32[]{:S(2)}) collective-permute-start(f32[2,24,512]{2,1,0:T(8,128)S(1)} %get-tuple-element.6), channel_id=1, source_target_pairs={{0,4},{1,5},{2,0},{3,1},{4,2},{5,3},{6,10},{7,11},{8,6},{9,7},{10,... | collective-permute-start | bytes 294920 | tf_op jit(solution)/shard_map/ppermute | solution.py:67
  52.7 25.1 %collective-permute-start.4 = (bf16[2,24,512]{2,1,0:T(8,128)(2,1)S(1)}, bf16[2,24,512]{2,1,0:T(8,128)(2,1)S(1)}, u32[]{:S(2)}, u32[]{:S(2)}) collective-permute-start(bf16[2,24,512]{2,1,0:T(8,128)(2,1)S(1)} %pad_maximum_fusion.1), channel_id=1, source_target_pairs={{0,2},{1,3},{2,4},{3,5},{4,0},{5,1},{6,8},{7,9},{8,10},{9,11},{10,... | collective-permute-start | bytes 147464 | tf_op jit(solution)/shard_map/ppermute | solution.py:74
  59.6 36.2 %collective-permute-start.5 = (bf16[2,24,512]{2,1,0:T(8,128)(2,1)S(1)}, bf16[2,24,512]{2,1,0:T(8,128)(2,1)S(1)}, u32[]{:S(2)}, u32[]{:S(2)}) collective-permute-start(bf16[2,24,512]{2,1,0:T(8,128)(2,1)S(1)} %pad_maximum_fusion.1), channel_id=1, source_target_pairs={{0,4},{1,5},{2,0},{3,1},{4,2},{5,3},{6,10},{7,11},{8,6},{9,7},{10,... | collective-permute-start | bytes 147464 | tf_op jit(solution)/shard_map/ppermute | solution.py:74
  73.0 5.8 %collective-permute-start.7 = (f32[1,64,512]{2,1,0:T(8,128)S(1)}, f32[1,64,512]{2,1,0:T(8,128)S(1)}, u32[]{:S(2)}, u32[]{:S(2)}) collective-permute-start(f32[1,64,512]{2,1,0:T(8,128)S(1)} %dynamic-slice_bitcast_fusion), channel_id=1, source_target_pairs={{0,1},{1,0},{2,3},{3,2},{4,5},{5,4},{6,7},{7,6},{8,9},{9,8},{10,11... | collective-permute-start | bytes 393224 | tf_op jit(solution)/shard_map/ppermute | solution.py:55
  78.8 20.4 %collective-permute-start.9 = (f32[1,64,512]{2,1,0:T(8,128)S(1)}, f32[1,64,512]{2,1,0:T(8,128)S(1)}, u32[]{:S(2)}, u32[]{:S(2)}) collective-permute-start(f32[1,64,512]{2,1,0:T(8,128)S(1)} %bitcast_add_fusion), channel_id=1, source_target_pairs={{0,4},{1,5},{2,0},{3,1},{4,2},{5,3},{6,10},{7,11},{8,6},{9,7},{10,... | collective-permute-start | bytes 393224 | tf_op jit(solution)/shard_map/ppermute | solution.py:92
  93.9 10.2 %collective-permute-start.8 = (f32[1,64,512]{2,1,0:T(8,128)S(1)}, f32[1,64,512]{2,1,0:T(8,128)S(1)}, u32[]{:S(2)}, u32[]{:S(2)}) collective-permute-start(f32[1,64,512]{2,1,0:T(8,128)S(1)} %bitcast_add_fusion), channel_id=1, source_target_pairs={{0,2},{1,3},{2,4},{3,5},{4,0},{5,1},{6,8},{7,9},{8,10},{9,11},{10,... | collective-permute-start | bytes 393224 | tf_op jit(solution)/shard_map/ppermute | solution.py:92
  104.2 4.5 %collective-permute-start.10 = (bf16[3,64,512]{2,1,0:T(8,128)(2,1)S(1)}, bf16[3,64,512]{2,1,0:T(8,128)(2,1)S(1)}, u32[]{:S(2)}, u32[]{:S(2)}) collective-permute-start(bf16[3,64,512]{2,1,0:T(8,128)(2,1)S(1)} %pad_maximum_fusion), channel_id=1, source_target_pairs={{0,1},{1,0},{2,3},{3,2},{4,5},{5,4},{6,7},{7,6},{8,9},{9,8},{10,11... | collective-permute-start | bytes 589832 | tf_op jit(solution)/shard_map/ppermute | solution.py:86
  112.1 39.5 %collective-permute-start.11 = (f32[2048,128]{0,1:T(8,128)S(1)}, f32[2048,128]{0,1:T(8,128)S(1)}, u32[]{:S(2)}, u32[]{:S(2)}) collective-permute-start(f32[2048,128]{0,1:T(8,128)S(1)} %fusion), channel_id=1, source_target_pairs={{0,6},{6,12},{12,18},{18,24},{24,30},{30,36},{36,42},{42,48},{48,5... | collective-permute-start | bytes 3145736 | tf_op jit(solution)/shard_map/ppermute | solution.py:11

commit v6 on v3

v6 whole, which is shorter than its diff:
```python
import jax
import jax.numpy as jnp
from jax import lax
from jax.sharding import PartitionSpec as P

spin_scale = 1.3


def shifted(value, axis, by):
    size = lax.axis_size(axis)
    return lax.ppermute(value, axis, [(i, (i + by) % size) for i in range(size)])


def partial_integrals(left_block, right_block):
    return lax.dot_general(
        left_block, right_block, (((0,), (0,)), ((), ())), preferred_element_type=jnp.float32
    )


def contribution(right_block, amplitude):
    return lax.dot_general(
        right_block, amplitude, (((1,), (1,)), ((), ())), preferred_element_type=jnp.float32
    )


def per_device(b_rows, b_cols, eps_occ, eps_va, eps_vb):
    per_block = b_rows.shape[1] // eps_va.shape[0]
    cycle_size = lax.axis_size("occ")
    position = lax.axis_index("occ")
    aux_size = lax.axis_size("aux")
    aux_pos = lax.axis_index("aux")
    rows = b_rows.shape[1]

    def energy(offset, virt_energy):
        which = (position + offset) % cycle_size
        occ_energy = lax.dynamic_slice_in_dim(eps_occ, which * per_block, per_block)
        return (virt_energy[None, :] - occ_energy[:, None]).reshape(-1)

    piece = -(-rows // aux_size)
    piece = -(-piece // 8) * 8
    padded_rows = piece * aux_size

    def aux_reduce(partials):
        stack = jnp.pad(jnp.stack(partials), ((0, 0), (0, padded_rows - rows), (0, 0)))
        parts = stack.reshape(stack.shape[0], aux_size, piece, stack.shape[2])
        got = lax.all_to_all(parts, "aux", 1, 1, tiled=True)
        return got.sum(axis=1)

    def aux_gather(mine):
        spread = jnp.broadcast_to(mine[:, None], (mine.shape[0], aux_size) + mine.shape[1:])
        got = lax.all_to_all(spread, "aux", 1, 1, tiled=True)
        return got.reshape(mine.shape[0], padded_rows, mine.shape[2])[:, :rows]

    def amplitude_part(summed, row_shift):
        row_energy = jnp.pad(energy(row_shift, eps_va), (0, padded_rows - rows), constant_values=1.0)
        row_energy = lax.dynamic_slice_in_dim(row_energy, aux_pos * piece, piece, 0)
        col_energy = energy(0, eps_vb)
        return (spin_scale * summed / (row_energy[:, None] + col_energy[None, :])).astype(jnp.bfloat16)

    cols_prev = shifted(b_cols, "occ", 1)
    rows_next = shifted(b_rows, "occ", -1)
    rows_after = shifted(rows_next, "occ", -1)
    lefts = [b_rows, rows_next, rows_after]
    summed = aux_reduce([partial_integrals(left, b_cols) for left in lefts])
    amp_parts = [amplitude_part(summed[s], s) for s in range(3)]
    far = shifted(amp_parts[2], "occ", 1)
    amps = aux_gather(jnp.stack([amp_parts[0], amp_parts[1], far]))
    own = contribution(b_cols, amps[0])
    onward = contribution(b_cols, amps[1]) + contribution(cols_prev, amps[2])
    return own + shifted(onward, "occ", 1)


def solution(mesh):
    return jax.shard_map(
        per_device,
        mesh=mesh,
        in_specs=(P("aux", "occ"), P("aux", "occ"), P(), P(), P()),
        out_specs=P("aux", "occ"),
        check_vma=False,
    )
```

time: 148 us -> 193 us (1.30)
  the two profiles are of different devices: /device:TPU:4 before, /device:TPU:1 now
where the time goes in v6:
time: 193 us
  waiting for transfers between devices  117 us (61%)
  starting transfers between devices  43 us (22%)
  blocking collectives  21.5 us (11%)
  matrix products  7.18 us (4%)
  local copies, waits for them, and re-layouts  2.85 us (1%)
    ppermute x5, waiting for transfers between devices, shifted(): lax.ppermute(value, axis, [(i, (i + by) % size) for i in range(size)])  94.6 us
    ppermute x5, starting transfers between devices, shifted(): lax.ppermute(value, axis, [(i, (i + by) % size) for i in range(size)])  29.4 us
    all_to_all x1, waiting for transfers between devices, aux_reduce(): got = lax.all_to_all(parts, 'aux', 1, 1, tiled=True)  22.8 us
    all_to_all x1, blocking collectives, aux_gather(): got = lax.all_to_all(spread, 'aux', 1, 1, tiled=True)  21.5 us
    all_to_all x1, starting transfers between devices, aux_reduce(): got = lax.all_to_all(parts, 'aux', 1, 1, tiled=True)  13.6 us
    dot_general x3, matrix products, contribution(): lax.dot_general(right_block, amplitude, (((1,), (1,)), ((), ())), preferr...  4.01 us
  transfers between devices with their start and end apart: 6, of which 5 were waited for; matrix products, arithmetic and copies ran while one was open for 3% of the time, Pallas kernels for 0%

profile of v6, /device:TPU:1, one launch (start us, length us, event | category | flops | bytes accessed | tf_op | source)
XLA Modules:
  0.0 192.9 jit_solution(16191716742393556103)
XLA Ops:
  0.0 0.0 copy-start
  0.0 13.7 %collective-permute-start = (bf16[2048,128]{1,0:T(8,128)(2,1)}, bf16[2048,128]{1,0:T(8,128)(2,1)S(1)}, u32[]{:S(2)}, u32[]{:S(2)}) collective-permute-start(bf16[2048,128]{1,0:T(8,128)(2,1)} %param.5), channel_id=1, source_target_pairs={{0,762},{6,0},{12,6},{18,12},{24,18},{30,24},{36,30},{42,36},{48,4... | collective-permute-start | bytes 1572872 | tf_op jit(solution)/shard_map/ppermute | solution.py:11
  13.7 10.9 %collective-permute-done = bf16[2048,128]{1,0:T(8,128)(2,1)S(1)} collective-permute-done((bf16[2048,128]{1,0:T(8,128)(2,1)}, bf16[2048,128]{1,0:T(8,128)(2,1)S(1)}, u32[]{:S(2)}, u32[]{:S(2)}) %collective-permute-start) | collective-permute-done | bytes 524320 | tf_op jit(solution)/shard_map/ppermute | solution.py:11
  24.6 10.0 %collective-permute-start.1 = (bf16[2048,128]{1,0:T(8,128)(2,1)S(1)}, bf16[2048,128]{1,0:T(8,128)(2,1)S(1)}, u32[]{:S(2)}, u32[]{:S(2)}) collective-permute-start(bf16[2048,128]{1,0:T(8,128)(2,1)S(1)} %collective-permute-done), channel_id=1, source_target_pairs={{0,762},{6,0},{12,6},{18,12},{24,18},{30,24},{36,30},{42,36},{48,4... | collective-permute-start | bytes 1572872 | tf_op jit(solution)/shard_map/ppermute | solution.py:11
  34.6 2.2 %convolution_bitcast_fusion.3 = f32[1,128,512]{2,1,0:T(8,128)S(1)} fusion(bf16[2048,128]{1,0:T(8,128)(2,1)} %param.5, bf16[2048,512]{1,0:T(8,128)(2,1)} %param.6), kind=kOutput, calls=%fused_computation.5 | convolution fusion | flops 268435456 | bytes 2883584 | tf_op jit(solution)/shard_map/dot_general | solution.py:15
  36.8 0.0 copy-done
  36.8 0.5 convolution_bitcast_fusion.2
  37.3 7.0 %collective-permute-done.1 = bf16[2048,128]{1,0:T(8,128)(2,1)S(1)} collective-permute-done((bf16[2048,128]{1,0:T(8,128)(2,1)S(1)}, bf16[2048,128]{1,0:T(8,128)(2,1)S(1)}, u32[]{:S(2)}, u32[]{:S(2)}) %collective-permute-start.1) | collective-permute-done | bytes 524320 | tf_op jit(solution)/shard_map/ppermute | solution.py:11
  44.3 0.5 convolution_bitcast_fusion.1
  44.8 0.1 select_maximum_fusion
  44.9 0.0 copy-start.1
  44.9 0.0 copy-start.3
  44.9 0.0 copy-start.2
  44.9 1.0 copy.9
  45.9 13.6 %all-to-all-start = ((f32[3,6,24,512]{3,2,0,1:T(8,128)}), f32[3,6,24,512]{3,2,0,1:T(8,128)S(1)}, u32[]{:S(2)}, u32[]{:S(2)}) async-start(f32[3,6,24,512]{3,2,0,1:T(8,128)} %copy.9), calls=%async_computation | async-start | bytes 1769472 | tf_op jit(solution)/shard_map/all_to_all | solution.py:46
  59.5 1.9 collective-permute-start.3
  61.5 0.0 copy-done.1
  61.5 0.1 fusion.9
  61.6 0.0 copy-done.3
  61.6 0.1 broadcast_subtract_fusion.2
  61.6 0.1 sub.94
  61.7 0.0 copy-done.2
  61.7 0.1 subtract_bitcast_fusion
  61.8 0.1 pad_dynamic-slice_fusion
  61.9 0.1 sub.84
  61.9 0.1 sub.91
  62.0 0.1 pad_dynamic-slice_fusion.1
  62.1 22.8 %all-to-all-done = f32[3,6,24,512]{3,2,0,1:T(8,128)S(1)} async-done(((f32[3,6,24,512]{3,2,0,1:T(8,128)}), f32[3,6,24,512]{3,2,0,1:T(8,128)S(1)}, u32[]{:S(2)}, u32[]{:S(2)}) %all-to-all-start) | async-done | bytes 884768 | tf_op jit(solution)/shard_map/all_to_all | solution.py:46
  85.0 0.1 reduce_sum.9
  85.0 0.1 fusion.4
  85.1 1.9 collective-permute-start.2
  87.0 0.1 fusion.8
  87.1 47.3 %collective-permute-done.2 = bf16[24,512]{1,0:T(8,128)(2,1)S(1)} collective-permute-done((bf16[24,512]{1,0:T(8,128)(2,1)S(1)}, bf16[24,512]{1,0:T(8,128)(2,1)S(1)}, u32[]{:S(2)}, u32[]{:S(2)}) %collective-permute-start.2) | collective-permute-done | bytes 24608 | tf_op jit(solution)/shard_map/ppermute | solution.py:11
  134.4 21.5 %all_to_all.10 = bf16[3,6,24,512]{3,2,0,1:T(8,128)(2,1)S(1)} all-to-all(bf16[3,6,24,512]{3,2,0,1:T(8,128)(2,1)S(1)} %broadcast_in_dim.2), channel_id=1, replica_groups=mesh['occ'=128,'aux'=6] {'aux'}, dimensions={1} | all-to-all | bytes 884736 | tf_op jit(solution)/shard_map/all_to_all | solution.py:51
  156.0 0.8 fusion.1
  156.8 0.0 collective-permute-done.3
  156.8 2.4 %fusion = f32[2048,128]{0,1:T(8,128)S(1)} fusion(f32[128,2048]{1,0:T(8,128)S(1)} %fusion.1, bf16[2048,512]{1,0:T(8,128)(2,1)} %collective-permute-done.3, bf16[3,144,512]{2,1,0:T(8,128)(2,1)S(1)} %bitcast.42), kind=kOutput, calls=%fused_computation.1 | convolution fusion | flops 268697600 | bytes 4325376 | tf_op jit(solution)/shard_map/dot_general | solution.py:21
  159.2 1.9 collective-permute-start.4
  161.2 0.8 convolution_bitcast_fusion
  162.0 29.5 %collective-permute-done.4 = f32[2048,128]{0,1:T(8,128)S(1)} collective-permute-done((f32[2048,128]{0,1:T(8,128)S(1)}, f32[2048,128]{0,1:T(8,128)S(1)}, u32[]{:S(2)}, u32[]{:S(2)}) %collective-permute-start.4) | collective-permute-done | bytes 1048608 | tf_op jit(solution)/shard_map/ppermute | solution.py:11
  191.4 0.1 add.123
  191.6 1.3 copy.11
  (4 shorter events, 0.1 us)
Async XLA Ops:
  0.0 36.8 %copy-start = (bf16[2048,512]{1,0:T(8,128)(2,1)S(1)}, bf16[2048,512]{1,0:T(8,128)(2,1)}, u32[]{:S(2)}) copy-start(bf16[2048,512]{1,0:T(8,128)(2,1)} %param.6) | copy-start | bytes 6291460
  0.0 24.6 %collective-permute-start = (bf16[2048,128]{1,0:T(8,128)(2,1)}, bf16[2048,128]{1,0:T(8,128)(2,1)S(1)}, u32[]{:S(2)}, u32[]{:S(2)}) collective-permute-start(bf16[2048,128]{1,0:T(8,128)(2,1)} %param.5), channel_id=1, source_target_pairs={{0,762},{6,0},{12,6},{18,12},{24,18},{30,24},{36,30},{42,36},{48,4... | collective-permute-start | bytes 1572872 | tf_op jit(solution)/shard_map/ppermute | solution.py:11
  24.6 19.7 %collective-permute-start.1 = (bf16[2048,128]{1,0:T(8,128)(2,1)S(1)}, bf16[2048,128]{1,0:T(8,128)(2,1)S(1)}, u32[]{:S(2)}, u32[]{:S(2)}) collective-permute-start(bf16[2048,128]{1,0:T(8,128)(2,1)S(1)} %collective-permute-done), channel_id=1, source_target_pairs={{0,762},{6,0},{12,6},{18,12},{24,18},{30,24},{36,30},{42,36},{48,4... | collective-permute-start | bytes 1572872 | tf_op jit(solution)/shard_map/ppermute | solution.py:11
  44.9 16.6 %copy-start.1 = (f32[256]{0:T(256)S(1)}, f32[256]{0:T(256)}, u32[]{:S(2)}) copy-start(f32[256]{0:T(256)} %param.7) | copy-start | bytes 3076
  44.9 16.7 %copy-start.3 = (f32[64]{0:T(128)S(1)}, f32[64]{0:T(128)}, u32[]{:S(2)}) copy-start(f32[64]{0:T(128)} %param.8) | copy-start | bytes 772
  44.9 16.8 %copy-start.2 = (f32[256]{0:T(256)S(1)}, f32[256]{0:T(256)}, u32[]{:S(2)}) copy-start(f32[256]{0:T(256)} %param.9) | copy-start | bytes 3076
  45.9 39.1 %all-to-all-start = ((f32[3,6,24,512]{3,2,0,1:T(8,128)}), f32[3,6,24,512]{3,2,0,1:T(8,128)S(1)}, u32[]{:S(2)}, u32[]{:S(2)}) async-start(f32[3,6,24,512]{3,2,0,1:T(8,128)} %copy.9), calls=%async_computation | async-start | bytes 1769472 | tf_op jit(solution)/shard_map/all_to_all | solution.py:46
  59.5 97.3 %collective-permute-start.3 = (bf16[2048,512]{1,0:T(8,128)(2,1)S(1)}, bf16[2048,512]{1,0:T(8,128)(2,1)}, u32[]{:S(2)}, u32[]{:S(2)}) collective-permute-start(bf16[2048,512]{1,0:T(8,128)(2,1)S(1)} %copy-done), channel_id=1, source_target_pairs={{0,6},{6,12},{12,18},{18,24},{24,30},{30,36},{36,42},{42,48},{48,5... | collective-permute-start | bytes 6291464 | tf_op jit(solution)/shard_map/ppermute | solution.py:11
  85.1 49.3 %collective-permute-start.2 = (bf16[24,512]{1,0:T(8,128)(2,1)S(1)}, bf16[24,512]{1,0:T(8,128)(2,1)S(1)}, u32[]{:S(2)}, u32[]{:S(2)}) collective-permute-start(bf16[24,512]{1,0:T(8,128)(2,1)S(1)} %fusion.4), channel_id=1, source_target_pairs={{0,6},{6,12},{12,18},{18,24},{24,30},{30,36},{36,42},{42,48},{48,5... | collective-permute-start | bytes 73736 | tf_op jit(solution)/shard_map/ppermute | solution.py:11
  159.2 32.2 %collective-permute-start.4 = (f32[2048,128]{0,1:T(8,128)S(1)}, f32[2048,128]{0,1:T(8,128)S(1)}, u32[]{:S(2)}, u32[]{:S(2)}) collective-permute-start(f32[2048,128]{0,1:T(8,128)S(1)} %fusion), channel_id=1, source_target_pairs={{0,6},{6,12},{12,18},{18,24},{24,30},{30,36},{36,42},{42,48},{48,5... | collective-permute-start | bytes 3145736 | tf_op jit(solution)/shard_map/ppermute | solution.py:11

commit v7 on v3

--- a/solution.py
+++ b/solution.py
@@ -72,13 +72,20 @@
     amp_halves = jnp.stack([
         amplitude_half(early[0], 0, 0), amplitude_half(early[1], 1, 0), amplitude_half(late[0], 1, -1)
     ])
+    near_first = contribution(b_cols, amp_halves[1]) + contribution(cols_prev, amp_halves[2])
+    sent_first = shifted(near_first, "occ", 1)
     amp_other = lax.ppermute(amp_halves, "aux", aux_pairs(aux_size, 1, 0))
-    first = jnp.concatenate([amp_halves, amp_other], axis=1)
-    second = jnp.concatenate([amp_other, amp_halves], axis=1)
-    amps = jnp.where(core == 0, first, second)
-    own = contribution(b_cols, amps[0])
-    onward = contribution(b_cols, amps[1]) + contribution(cols_prev, amps[2])
-    return own + shifted(onward, "occ", 1)
+    near_second = contribution(b_cols, amp_other[1]) + contribution(cols_prev, amp_other[2])
+    sent_second = shifted(near_second, "occ", 1)
+    first = jnp.concatenate([amp_halves[0], amp_other[0]], axis=0)
+    second = jnp.concatenate([amp_other[0], amp_halves[0]], axis=0)
+    own = contribution(b_cols, jnp.where(core == 0, first, second))
+    sent = jnp.where(
+        core == 0,
+        jnp.concatenate([sent_first, sent_second], axis=1),
+        jnp.concatenate([sent_second, sent_first], axis=1),
+    )
+    return own + sent
 
 
 def solution(mesh):

time: 148 us -> 146 us (0.986)
  the two profiles are of different devices: /device:TPU:4 before, /device:TPU:1 now
where the time goes in v7:
time: 146 us
  starting transfers between devices  66.6 us (46%)
  waiting for transfers between devices  60.1 us (41%)
  matrix products  14.2 us (10%)
  local copies, waits for them, and re-layouts  3.38 us (2%)
    ppermute x4, waiting for transfers between devices, shifted(): lax.ppermute(value, axis, [(i, (i + by) % size) for i in range(size)])  48.1 us
    ppermute x4, starting transfers between devices, chip_reduce(): lax.ppermute(summed, 'aux', aux_pairs(aux_size, 0, d))  23.5 us
    ppermute x2, starting transfers between devices, core_reduce(): return keep + lax.ppermute(give, 'aux', aux_pairs(aux_size, 1, 0))  21.3 us
    ppermute x4, starting transfers between devices, shifted(): lax.ppermute(value, axis, [(i, (i + by) % size) for i in range(size)])  19.4 us
    ppermute x4, waiting for transfers between devices, chip_reduce(): lax.ppermute(summed, 'aux', aux_pairs(aux_size, 0, d))  10.3 us
    dot_general x5, matrix products, contribution(): lax.dot_general(right_block, amplitude, (((1,), (1,)), ((), ())), preferr...  9.43 us
    dot_general x3, matrix products, partial_integrals(): lax.dot_general(left_block, right_block, (((0,), (0,)), ((), ())), prefer...  4.75 us
  transfers between devices with their start and end apart: 11, of which 8 were waited for; matrix products, arithmetic and copies ran while one was open for 10% of the time, Pallas kernels for 0%

profile of v7, /device:TPU:1, one launch (start us, length us, event | category | flops | bytes accessed | tf_op | source)
XLA Modules:
  0.0 145.8 jit_solution(9500620899639793409)
XLA Ops:
  0.0 4.1 %collective-permute-start.4 = (bf16[2048,512]{1,0:T(8,128)(2,1)}, bf16[2048,512]{1,0:T(8,128)(2,1)}, u32[]{:S(2)}, u32[]{:S(2)}) collective-permute-start(bf16[2048,512]{1,0:T(8,128)(2,1)} %param.6), channel_id=1, source_target_pairs={{0,6},{6,12},{12,18},{18,24},{24,30},{30,36},{36,42},{42,48},{48,5... | collective-permute-start | bytes 6291464 | tf_op jit(solution)/shard_map/ppermute | solution.py:11
  4.2 11.4 %collective-permute-start = (bf16[2048,128]{1,0:T(8,128)(2,1)}, bf16[2048,128]{1,0:T(8,128)(2,1)S(1)}, u32[]{:S(2)}, u32[]{:S(2)}) collective-permute-start(bf16[2048,128]{1,0:T(8,128)(2,1)} %param.5), channel_id=1, source_target_pairs={{0,762},{6,0},{12,6},{18,12},{24,18},{30,24},{36,30},{42,36},{48,4... | collective-permute-start | bytes 1572872 | tf_op jit(solution)/shard_map/ppermute | solution.py:11
  15.7 0.9 fusion.26
  16.6 2.2 %convolution_bitcast_fusion.2 = f32[1,128,512]{2,1,0:T(8,128)S(1)} fusion(bf16[2048,128]{1,0:T(8,128)(2,1)} %param.5, bf16[2048,512]{1,0:T(8,128)(2,1)} %param.6), kind=kOutput, calls=%fused_computation.6 | convolution fusion | flops 268435456 | bytes 2883584 | tf_op jit(solution)/shard_map/dot_general | solution.py:24
  18.8 0.0 copy-start.3
  18.8 0.0 copy-start.2
  18.8 3.2 %collective-permute-done = bf16[2048,128]{1,0:T(8,128)(2,1)S(1)} collective-permute-done((bf16[2048,128]{1,0:T(8,128)(2,1)}, bf16[2048,128]{1,0:T(8,128)(2,1)S(1)}, u32[]{:S(2)}, u32[]{:S(2)}) %collective-permute-start) | collective-permute-done | bytes 524320 | tf_op jit(solution)/shard_map/ppermute | solution.py:11
  22.0 0.0 copy-done
  22.0 0.5 convolution_bitcast_fusion.1
  22.5 0.7 fusion.3
  23.2 9.3 %collective-permute-start.1 = (f32[2,64,512]{2,1,0:T(8,128)}, f32[2,64,512]{2,1,0:T(8,128)S(1)}, u32[]{:S(2)}, u32[]{:S(2)}) collective-permute-start(f32[2,64,512]{2,1,0:T(8,128)} %fusion.3), channel_id=1, source_target_pairs={{0,1},{1,0},{2,3},{3,2},{4,5},{5,4},{6,7},{7,6},{8,9},{9,8},{10,11... | collective-permute-start | bytes 786440 | tf_op jit(solution)/shard_map/ppermute | solution.py:55
  32.6 0.0 copy-done.3
  32.6 0.1 broadcast_subtract_fusion.1
  32.7 0.1 sub.92
  32.7 0.1 sub.99
  32.8 0.1 dynamic_slice.34
  32.9 0.1 dynamic_slice.36
  33.0 0.1 subtract_bitcast_fusion.1
  33.1 0.9 collective-permute-done.1
  34.0 10.1 %collective-permute-start.3 = (f32[2,64,512]{2,1,0:T(8,128)S(1)}, f32[2,64,512]{2,1,0:T(8,128)S(1)}, u32[]{:S(2)}, u32[]{:S(2)}) collective-permute-start(f32[2,64,512]{2,1,0:T(8,128)S(1)} %fusion.5), channel_id=1, source_target_pairs={{0,4},{1,5},{2,0},{3,1},{4,2},{5,3},{6,10},{7,11},{8,6},{9,7},{10,... | collective-permute-start | bytes 786440 | tf_op jit(solution)/shard_map/ppermute | solution.py:58
  44.1 1.9 %collective-permute-start.2 = (f32[2,64,512]{2,1,0:T(8,128)S(1)}, f32[2,64,512]{2,1,0:T(8,128)S(1)}, u32[]{:S(2)}, u32[]{:S(2)}) collective-permute-start(f32[2,64,512]{2,1,0:T(8,128)S(1)} %fusion.5), channel_id=1, source_target_pairs={{0,2},{1,3},{2,4},{3,5},{4,0},{5,1},{6,8},{7,9},{8,10},{9,11},{10,... | collective-permute-start | bytes 786440 | tf_op jit(solution)/shard_map/ppermute | solution.py:58
  46.0 13.3 %collective-permute-done.4 = bf16[2048,512]{1,0:T(8,128)(2,1)} collective-permute-done((bf16[2048,512]{1,0:T(8,128)(2,1)}, bf16[2048,512]{1,0:T(8,128)(2,1)}, u32[]{:S(2)}, u32[]{:S(2)}) %collective-permute-start.4) | collective-permute-done | bytes 2097184 | tf_op jit(solution)/shard_map/ppermute | solution.py:11
  59.4 2.1 %fusion.27 = f32[128,512]{1,0:T(8,128)S(1)} fusion(bf16[2048,128]{1,0:T(8,128)(2,1)S(1)} %collective-permute-done, bf16[2048,512]{1,0:T(8,128)(2,1)} %collective-permute-done.4), kind=kOutput, calls=%fused_computation.56 | convolution fusion | flops 268435456 | bytes 2883584 | tf_op jit(solution)/shard_map/dot_general | solution.py:24
  61.5 11.9 %collective-permute-start.5 = (f32[1,64,512]{2,1,0:T(8,128)S(1)}, f32[1,64,512]{2,1,0:T(8,128)S(1)}, u32[]{:S(2)}, u32[]{:S(2)}) collective-permute-start(f32[1,64,512]{2,1,0:T(8,128)S(1)} %dynamic-slice_bitcast_fusion), channel_id=1, source_target_pairs={{0,1},{1,0},{2,3},{3,2},{4,5},{5,4},{6,7},{7,6},{8,9},{9,8},{10,11... | collective-permute-start | bytes 393224 | tf_op jit(solution)/shard_map/ppermute | solution.py:55
  73.4 0.0 collective-permute-done.3
  73.4 0.0 collective-permute-done.2
  73.4 0.1 add_add_fusion
  73.5 0.8 collective-permute-done.5
  74.4 9.5 %collective-permute-start.7 = (f32[1,64,512]{2,1,0:T(8,128)S(1)}, f32[1,64,512]{2,1,0:T(8,128)S(1)}, u32[]{:S(2)}, u32[]{:S(2)}) collective-permute-start(f32[1,64,512]{2,1,0:T(8,128)S(1)} %bitcast_add_fusion), channel_id=1, source_target_pairs={{0,4},{1,5},{2,0},{3,1},{4,2},{5,3},{6,10},{7,11},{8,6},{9,7},{10,... | collective-permute-start | bytes 393224 | tf_op jit(solution)/shard_map/ppermute | solution.py:58
  83.9 1.9 %collective-permute-start.6 = (f32[1,64,512]{2,1,0:T(8,128)S(1)}, f32[1,64,512]{2,1,0:T(8,128)S(1)}, u32[]{:S(2)}, u32[]{:S(2)}) collective-permute-start(f32[1,64,512]{2,1,0:T(8,128)S(1)} %bitcast_add_fusion), channel_id=1, source_target_pairs={{0,2},{1,3},{2,4},{3,5},{4,0},{5,1},{6,8},{7,9},{8,10},{9,11},{10,... | collective-permute-start | bytes 393224 | tf_op jit(solution)/shard_map/ppermute | solution.py:58
  85.8 0.8 fusion.15
  86.6 0.1 collective-permute-done.7
  86.7 10.1 %collective-permute-done.6 = f32[1,64,512]{2,1,0:T(8,128)S(1)} collective-permute-done((f32[1,64,512]{2,1,0:T(8,128)S(1)}, f32[1,64,512]{2,1,0:T(8,128)S(1)}, u32[]{:S(2)}, u32[]{:S(2)}) %collective-permute-start.6) | collective-permute-done | bytes 131104 | tf_op jit(solution)/shard_map/ppermute | solution.py:58
  96.8 0.1 divide_convert_fusion.2
  97.0 2.4 %collective-permute-start.8 = (bf16[3,64,512]{2,1,0:T(8,128)(2,1)S(1)}, bf16[3,64,512]{2,1,0:T(8,128)(2,1)S(1)}, u32[]{:S(2)}, u32[]{:S(2)}) collective-permute-start(bf16[3,64,512]{2,1,0:T(8,128)(2,1)S(1)} %pad_maximum_fusion), channel_id=1, source_target_pairs={{0,1},{1,0},{2,3},{3,2},{4,5},{5,4},{6,7},{7,6},{8,9},{9,8},{10,11... | collective-permute-start | bytes 589832 | tf_op jit(solution)/shard_map/ppermute | solution.py:77
  99.4 2.4 %fusion = f32[2048,64]{0,1:T(8,128)S(1)} fusion(f32[64,2048]{1,0:T(8,128)S(1)} %fusion.15, bf16[2048,512]{1,0:T(8,128)(2,1)} %collective-permute-done.4, f32[512]{0:T(512)S(1)} %bitcast.59, f32[64]{0:T(128)S(1)} %dynamic_slice.36, f32[1,64,512]{2,1,0:T(8,128)S(1)} %collective-permute-done.7, f32[1,64,512]{2,1,0:T(8,128)S(1)} %bitcast_add_fusion, ...), kind=kOutput, calls=%fused_computation.3 | convolution fusion | flops 134545408 | bytes 3541248 | tf_op jit(solution)/shard_map/dot_general | solution.py:30
  101.8 1.9 %collective-permute-start.9 = (f32[2048,64]{0,1:T(8,128)S(1)}, f32[2048,64]{0,1:T(8,128)}, u32[]{:S(2)}, u32[]{:S(2)}) collective-permute-start(f32[2048,64]{0,1:T(8,128)S(1)} %fusion), channel_id=1, source_target_pairs={{0,6},{6,12},{12,18},{18,24},{24,30},{30,36},{36,42},{42,48},{48,5... | collective-permute-start | bytes 1572872 | tf_op jit(solution)/shard_map/ppermute | solution.py:11
  103.7 0.0 collective-permute-done.8
  103.8 2.4 %fusion.18 = f32[64,2048]{1,0:T(8,128)S(1)} fusion(bf16[2048,512]{1,0:T(8,128)(2,1)} %collective-permute-done.4, bf16[3,64,512]{2,1,0:T(8,128)(2,1)S(1)} %collective-permute-done.8), kind=kOutput, calls=%fused_computation.41 | convolution fusion | flops 134217728 | bytes 2686976 | tf_op jit(solution)/shard_map/dot_general | solution.py:30
  106.2 1.6 %fusion.1 = f32[2048,64]{0,1:T(8,128)} fusion(f32[64,2048]{1,0:T(8,128)S(1)} %fusion.18, bf16[2048,512]{1,0:T(8,128)(2,1)S(1)} %copy-done, bf16[3,64,512]{2,1,0:T(8,128)(2,1)S(1)} %collective-permute-done.8), kind=kOutput, calls=%fused_computation.4 | convolution fusion | flops 134348800 | bytes 3211264 | tf_op jit(solution)/shard_map/dot_general | solution.py:30
  107.7 0.0 copy-done.1
  107.7 1.9 %collective-permute-start.10 = (f32[2048,64]{0,1:T(8,128)}, f32[2048,64]{0,1:T(8,128)}, u32[]{:S(2)}, u32[]{:S(2)}) collective-permute-start(f32[2048,64]{0,1:T(8,128)} %fusion.1), channel_id=1, source_target_pairs={{0,6},{6,12},{12,18},{18,24},{24,30},{30,36},{36,42},{42,48},{48,5... | collective-permute-start | bytes 1572872 | tf_op jit(solution)/shard_map/ppermute | solution.py:11
  109.6 0.1 fusion.13
  109.7 0.8 slice_bitcast_fusion.4
  110.6 20.3 %collective-permute-done.9 = f32[2048,64]{0,1:T(8,128)} collective-permute-done((f32[2048,64]{0,1:T(8,128)S(1)}, f32[2048,64]{0,1:T(8,128)}, u32[]{:S(2)}, u32[]{:S(2)}) %collective-permute-start.9) | collective-permute-done | bytes 524320 | tf_op jit(solution)/shard_map/ppermute | solution.py:11
  130.9 11.2 %collective-permute-done.10 = f32[2048,64]{0,1:T(8,128)} collective-permute-done((f32[2048,64]{0,1:T(8,128)}, f32[2048,64]{0,1:T(8,128)}, u32[]{:S(2)}, u32[]{:S(2)}) %collective-permute-start.10) | collective-permute-done | bytes 524320 | tf_op jit(solution)/shard_map/ppermute | solution.py:11
  142.1 2.3 %fusion.2 = f32[2048,128]{0,1:T(8,128)S(1)} fusion(f32[2048,64]{0,1:T(8,128)} %collective-permute-done.10, f32[2048,64]{0,1:T(8,128)} %collective-permute-done.9, pred[]{:T(512)S(6)} %eq.12, bf16[2048,512]{1,0:T(8,128)(2,1)S(1)} %copy-done, bf16[64,512]{1,0:T(8,128)(2,1)S(1)} %slice_bitcast_fusion.4, bf16[64,512]{1,0:T(8,128)(2,1)S(1)} %fusion.13), kind=kOutput, calls=%fused_computation.8 | convolution fusion | flops 270073856 | bytes 4325377 | tf_op jit(solution)/shard_map/dot_general | solution.py:30
  144.5 1.3 copy.6
  (9 shorter events, 0.1 us)
Async XLA Ops:
  0.0 22.0 %copy-start = (bf16[2048,512]{1,0:T(8,128)(2,1)S(1)}, bf16[2048,512]{1,0:T(8,128)(2,1)}, u32[]{:S(2)}) copy-start(bf16[2048,512]{1,0:T(8,128)(2,1)} %param.6) | copy-start | bytes 6291460
  0.0 59.4 %collective-permute-start.4 = (bf16[2048,512]{1,0:T(8,128)(2,1)}, bf16[2048,512]{1,0:T(8,128)(2,1)}, u32[]{:S(2)}, u32[]{:S(2)}) collective-permute-start(bf16[2048,512]{1,0:T(8,128)(2,1)} %param.6), channel_id=1, source_target_pairs={{0,6},{6,12},{12,18},{18,24},{24,30},{30,36},{36,42},{42,48},{48,5... | collective-permute-start | bytes 6291464 | tf_op jit(solution)/shard_map/ppermute | solution.py:11
  4.2 17.9 %collective-permute-start = (bf16[2048,128]{1,0:T(8,128)(2,1)}, bf16[2048,128]{1,0:T(8,128)(2,1)S(1)}, u32[]{:S(2)}, u32[]{:S(2)}) collective-permute-start(bf16[2048,128]{1,0:T(8,128)(2,1)} %param.5), channel_id=1, source_target_pairs={{0,762},{6,0},{12,6},{18,12},{24,18},{30,24},{36,30},{42,36},{48,4... | collective-permute-start | bytes 1572872 | tf_op jit(solution)/shard_map/ppermute | solution.py:11
  18.8 13.8 %copy-start.3 = (f32[64]{0:T(128)S(1)}, f32[64]{0:T(128)}, u32[]{:S(2)}) copy-start(f32[64]{0:T(128)} %param.8) | copy-start | bytes 772
  18.8 14.2 %copy-start.2 = (f32[256]{0:T(256)S(1)}, f32[256]{0:T(256)}, u32[]{:S(2)}) copy-start(f32[256]{0:T(256)} %param.9) | copy-start | bytes 3076
  23.2 10.7 %collective-permute-start.1 = (f32[2,64,512]{2,1,0:T(8,128)}, f32[2,64,512]{2,1,0:T(8,128)S(1)}, u32[]{:S(2)}, u32[]{:S(2)}) collective-permute-start(f32[2,64,512]{2,1,0:T(8,128)} %fusion.3), channel_id=1, source_target_pairs={{0,1},{1,0},{2,3},{3,2},{4,5},{5,4},{6,7},{7,6},{8,9},{9,8},{10,11... | collective-permute-start | bytes 786440 | tf_op jit(solution)/shard_map/ppermute | solution.py:55
  34.0 39.4 %collective-permute-start.3 = (f32[2,64,512]{2,1,0:T(8,128)S(1)}, f32[2,64,512]{2,1,0:T(8,128)S(1)}, u32[]{:S(2)}, u32[]{:S(2)}) collective-permute-start(f32[2,64,512]{2,1,0:T(8,128)S(1)} %fusion.5), channel_id=1, source_target_pairs={{0,4},{1,5},{2,0},{3,1},{4,2},{5,3},{6,10},{7,11},{8,6},{9,7},{10,... | collective-permute-start | bytes 786440 | tf_op jit(solution)/shard_map/ppermute | solution.py:58
  44.1 29.3 %collective-permute-start.2 = (f32[2,64,512]{2,1,0:T(8,128)S(1)}, f32[2,64,512]{2,1,0:T(8,128)S(1)}, u32[]{:S(2)}, u32[]{:S(2)}) collective-permute-start(f32[2,64,512]{2,1,0:T(8,128)S(1)} %fusion.5), channel_id=1, source_target_pairs={{0,2},{1,3},{2,4},{3,5},{4,0},{5,1},{6,8},{7,9},{8,10},{9,11},{10,... | collective-permute-start | bytes 786440 | tf_op jit(solution)/shard_map/ppermute | solution.py:58
  61.5 12.9 %collective-permute-start.5 = (f32[1,64,512]{2,1,0:T(8,128)S(1)}, f32[1,64,512]{2,1,0:T(8,128)S(1)}, u32[]{:S(2)}, u32[]{:S(2)}) collective-permute-start(f32[1,64,512]{2,1,0:T(8,128)S(1)} %dynamic-slice_bitcast_fusion), channel_id=1, source_target_pairs={{0,1},{1,0},{2,3},{3,2},{4,5},{5,4},{6,7},{7,6},{8,9},{9,8},{10,11... | collective-permute-start | bytes 393224 | tf_op jit(solution)/shard_map/ppermute | solution.py:55
  74.4 12.3 %collective-permute-start.7 = (f32[1,64,512]{2,1,0:T(8,128)S(1)}, f32[1,64,512]{2,1,0:T(8,128)S(1)}, u32[]{:S(2)}, u32[]{:S(2)}) collective-permute-start(f32[1,64,512]{2,1,0:T(8,128)S(1)} %bitcast_add_fusion), channel_id=1, source_target_pairs={{0,4},{1,5},{2,0},{3,1},{4,2},{5,3},{6,10},{7,11},{8,6},{9,7},{10,... | collective-permute-start | bytes 393224 | tf_op jit(solution)/shard_map/ppermute | solution.py:58
  83.9 13.0 %collective-permute-start.6 = (f32[1,64,512]{2,1,0:T(8,128)S(1)}, f32[1,64,512]{2,1,0:T(8,128)S(1)}, u32[]{:S(2)}, u32[]{:S(2)}) collective-permute-start(f32[1,64,512]{2,1,0:T(8,128)S(1)} %bitcast_add_fusion), channel_id=1, source_target_pairs={{0,2},{1,3},{2,4},{3,5},{4,0},{5,1},{6,8},{7,9},{8,10},{9,11},{10,... | collective-permute-start | bytes 393224 | tf_op jit(solution)/shard_map/ppermute | solution.py:58
  97.0 6.7 %collective-permute-start.8 = (bf16[3,64,512]{2,1,0:T(8,128)(2,1)S(1)}, bf16[3,64,512]{2,1,0:T(8,128)(2,1)S(1)}, u32[]{:S(2)}, u32[]{:S(2)}) collective-permute-start(bf16[3,64,512]{2,1,0:T(8,128)(2,1)S(1)} %pad_maximum_fusion), channel_id=1, source_target_pairs={{0,1},{1,0},{2,3},{3,2},{4,5},{5,4},{6,7},{7,6},{8,9},{9,8},{10,11... | collective-permute-start | bytes 589832 | tf_op jit(solution)/shard_map/ppermute | solution.py:77
  101.8 29.1 %collective-permute-start.9 = (f32[2048,64]{0,1:T(8,128)S(1)}, f32[2048,64]{0,1:T(8,128)}, u32[]{:S(2)}, u32[]{:S(2)}) collective-permute-start(f32[2048,64]{0,1:T(8,128)S(1)} %fusion), channel_id=1, source_target_pairs={{0,6},{6,12},{12,18},{18,24},{24,30},{30,36},{36,42},{42,48},{48,5... | collective-permute-start | bytes 1572872 | tf_op jit(solution)/shard_map/ppermute | solution.py:11
  103.7 4.0 %copy-start.1 = (bf16[3,64,512]{2,1,0:T(8,128)(2,1)}, bf16[3,64,512]{2,1,0:T(8,128)(2,1)S(1)}, u32[]{:S(2)}) copy-start(bf16[3,64,512]{2,1,0:T(8,128)(2,1)S(1)} %collective-permute-done.8) | copy-start | bytes 589828
  107.7 34.4 %collective-permute-start.10 = (f32[2048,64]{0,1:T(8,128)}, f32[2048,64]{0,1:T(8,128)}, u32[]{:S(2)}, u32[]{:S(2)}) collective-permute-start(f32[2048,64]{0,1:T(8,128)} %fusion.1), channel_id=1, source_target_pairs={{0,6},{6,12},{12,18},{18,24},{24,30},{30,36},{36,42},{42,48},{48,5... | collective-permute-start | bytes 1572872 | tf_op jit(solution)/shard_map/ppermute | solution.py:11

commit v8 on v7

--- a/solution.py
+++ b/solution.py
@@ -69,17 +69,19 @@
     rows_next = shifted(b_rows, "occ", -1)
     early = chip_reduce(core_reduce([partial_integrals(b_rows, b_cols), partial_integrals(rows_next, b_cols)]))
     late = chip_reduce(core_reduce([partial_integrals(rows_next, cols_prev)]))
-    amp_halves = jnp.stack([
-        amplitude_half(early[0], 0, 0), amplitude_half(early[1], 1, 0), amplitude_half(late[0], 1, -1)
-    ])
-    near_first = contribution(b_cols, amp_halves[1]) + contribution(cols_prev, amp_halves[2])
-    sent_first = shifted(near_first, "occ", 1)
-    amp_other = lax.ppermute(amp_halves, "aux", aux_pairs(aux_size, 1, 0))
-    near_second = contribution(b_cols, amp_other[1]) + contribution(cols_prev, amp_other[2])
-    sent_second = shifted(near_second, "occ", 1)
-    first = jnp.concatenate([amp_halves[0], amp_other[0]], axis=0)
-    second = jnp.concatenate([amp_other[0], amp_halves[0]], axis=0)
-    own = contribution(b_cols, jnp.where(core == 0, first, second))
+    early_halves = jnp.stack([amplitude_half(early[0], 0, 0), amplitude_half(early[1], 1, 0)])
+    early_other = lax.ppermute(early_halves, "aux", aux_pairs(aux_size, 1, 0))
+    first = jnp.concatenate([early_halves, early_other], axis=1)
+    second = jnp.concatenate([early_other, early_halves], axis=1)
+    early_amps = jnp.where(core == 0, first, second)
+    own = contribution(b_cols, early_amps[0])
+    near = contribution(b_cols, early_amps[1])
+    lo = lax.dynamic_slice_in_dim(near, core * half, half, 1)
+    hi = lax.dynamic_slice_in_dim(near, (1 - core) * half, half, 1)
+    far_half = amplitude_half(late[0], 1, -1)
+    sent_first = shifted(lo + contribution(cols_prev, far_half), "occ", 1)
+    far_other = lax.ppermute(far_half, "aux", aux_pairs(aux_size, 1, 0))
+    sent_second = shifted(hi + contribution(cols_prev, far_other), "occ", 1)
     sent = jnp.where(
         core == 0,
         jnp.concatenate([sent_first, sent_second], axis=1),

time: 146 us -> 161 us (1.10)
  waiting for transfers between devices: 60.1 us -> 72.2 us
  starting transfers between devices: 66.6 us -> 71.7 us
  matrix products: 14.2 us -> 11.1 us
  other arithmetic: 1.27 us -> 3.02 us
  local copies, waits for them, and re-layouts: 3.38 us -> 1.75 us
    ppermute x4, waiting for transfers between devices: 10.3 us -> 31.1 us  [chip_reduce(): lax.ppermute(summed, 'aux', aux_pairs(aux_size, 0, d))]
    ppermute x4, starting transfers between devices: 23.5 us -> 37.8 us  [chip_reduce(): lax.ppermute(summed, 'aux', aux_pairs(aux_size, 0, d))]
    ppermute x2, starting transfers between devices: 21.3 us -> 8.57 us  [core_reduce(): return keep + lax.ppermute(give, 'aux', aux_pairs(aux_size, 1, 0))]
    ppermute x4, waiting for transfers between devices: 48.1 us -> 39 us  [shifted(): lax.ppermute(value, axis, [(i, (i + by) % size) for i in range(size)])]
    ppermute x1 -> x2, starting transfers between devices: 2.42 us -> 5.93 us  [the longest x1 3.41 us: per_device(): far_other = lax.ppermute(far_half, 'aux', aux_pairs(aux_size, 1, 0))]
    dot_general x5 -> x4, matrix products: 9.43 us -> 6.32 us  [contribution(): lax.dot_general(right_block, amplitude, (((1,), (1,)), ((), ())), preferr...]
  transfers between devices with their start and end apart: 11 -> 12, of which waited for: 8 -> 9; matrix products, arithmetic and copies ran while one was open for 10% -> 8% of each run, Pallas kernels for 0% -> 0%
where the time goes in v8:
time: 161 us; the launch traced here: 160 us
  waiting for transfers between devices  72.2 us (45%)
  starting transfers between devices  71.7 us (45%)
  matrix products  11.1 us (7%)
  other arithmetic  3.02 us (2%)
  local copies, waits for them, and re-layouts  1.75 us (1%)
    ppermute x4, waiting for transfers between devices, shifted(): lax.ppermute(value, axis, [(i, (i + by) % size) for i in range(size)])  39 us
    ppermute x4, starting transfers between devices, chip_reduce(): lax.ppermute(summed, 'aux', aux_pairs(aux_size, 0, d))  37.8 us
    ppermute x4, waiting for transfers between devices, chip_reduce(): lax.ppermute(summed, 'aux', aux_pairs(aux_size, 0, d))  31.1 us
    ppermute x4, starting transfers between devices, shifted(): lax.ppermute(value, axis, [(i, (i + by) % size) for i in range(size)])  19.4 us
    ppermute x2, starting transfers between devices, core_reduce(): return keep + lax.ppermute(give, 'aux', aux_pairs(aux_size, 1, 0))  8.57 us
    dot_general x4, matrix products, contribution(): lax.dot_general(right_block, amplitude, (((1,), (1,)), ((), ())), preferr...  6.32 us
    dot_general x3, matrix products, partial_integrals(): lax.dot_general(left_block, right_block, (((0,), (0,)), ((), ())), prefer...  4.76 us
    ppermute x1, starting transfers between devices, per_device(): far_other = lax.ppermute(far_half, 'aux', aux_pairs(aux_size, 1, 0))  3.41 us
  transfers between devices with their start and end apart: 12, of which 9 were waited for; matrix products, arithmetic and copies ran while one was open for 8% of the time, Pallas kernels for 0%

profile of v8, /device:TPU:1, one launch (start us, length us, event | category | flops | bytes accessed | tf_op | source)
XLA Modules:
  0.0 160.1 jit_solution(5507975434252382901)
XLA Ops:
  0.0 13.7 %collective-permute-start = (bf16[2048,128]{1,0:T(8,128)(2,1)}, bf16[2048,128]{1,0:T(8,128)(2,1)S(1)}, u32[]{:S(2)}, u32[]{:S(2)}) collective-permute-start(bf16[2048,128]{1,0:T(8,128)(2,1)} %param.5), channel_id=1, source_target_pairs={{0,762},{6,0},{12,6},{18,12},{24,18},{30,24},{36,30},{42,36},{48,4... | collective-permute-start | bytes 1572872 | tf_op jit(solution)/shard_map/ppermute | solution.py:11
  13.7 1.9 %collective-permute-start.5 = (bf16[2048,512]{1,0:T(8,128)(2,1)}, bf16[2048,512]{1,0:T(8,128)(2,1)}, u32[]{:S(2)}, u32[]{:S(2)}) collective-permute-start(bf16[2048,512]{1,0:T(8,128)(2,1)} %param.6), channel_id=1, source_target_pairs={{0,6},{6,12},{12,18},{18,24},{24,30},{30,36},{36,42},{42,48},{48,5... | collective-permute-start | bytes 6291464 | tf_op jit(solution)/shard_map/ppermute | solution.py:11
  15.6 2.2 %convolution_bitcast_fusion.2 = f32[1,128,512]{2,1,0:T(8,128)S(1)} fusion(bf16[2048,128]{1,0:T(8,128)(2,1)} %param.5, bf16[2048,512]{1,0:T(8,128)(2,1)} %param.6), kind=kOutput, calls=%fused_computation.6 | convolution fusion | flops 268435456 | bytes 2883584 | tf_op jit(solution)/shard_map/dot_general | solution.py:24
  17.9 0.0 copy-start.1
  17.9 0.0 copy-start.3
  17.9 0.0 copy-start.2
  17.9 6.7 %collective-permute-done = bf16[2048,128]{1,0:T(8,128)(2,1)S(1)} collective-permute-done((bf16[2048,128]{1,0:T(8,128)(2,1)}, bf16[2048,128]{1,0:T(8,128)(2,1)S(1)}, u32[]{:S(2)}, u32[]{:S(2)}) %collective-permute-start) | collective-permute-done | bytes 524320 | tf_op jit(solution)/shard_map/ppermute | solution.py:11
  24.6 0.5 convolution_bitcast_fusion.1
  25.0 0.7 fusion.3
  25.8 3.4 %collective-permute-start.1 = (f32[2,64,512]{2,1,0:T(8,128)}, f32[2,64,512]{2,1,0:T(8,128)S(1)}, u32[]{:S(2)}, u32[]{:S(2)}) collective-permute-start(f32[2,64,512]{2,1,0:T(8,128)} %fusion.3), channel_id=1, source_target_pairs={{0,1},{1,0},{2,3},{3,2},{4,5},{5,4},{6,7},{7,6},{8,9},{9,8},{10,11... | collective-permute-start | bytes 786440 | tf_op jit(solution)/shard_map/ppermute | solution.py:55
  29.3 0.1 fusion.12
  29.4 1.2 collective-permute-done.1
  30.6 0.7 fusion.5
  31.3 11.6 %collective-permute-start.3 = (f32[2,64,512]{2,1,0:T(8,128)}, f32[2,64,512]{2,1,0:T(8,128)}, u32[]{:S(2)}, u32[]{:S(2)}) collective-permute-start(f32[2,64,512]{2,1,0:T(8,128)} %fusion.5), channel_id=1, source_target_pairs={{0,4},{1,5},{2,0},{3,1},{4,2},{5,3},{6,10},{7,11},{8,6},{9,7},{10,... | collective-permute-start | bytes 786440 | tf_op jit(solution)/shard_map/ppermute | solution.py:58
  42.9 1.9 %collective-permute-start.2 = (f32[2,64,512]{2,1,0:T(8,128)}, f32[2,64,512]{2,1,0:T(8,128)}, u32[]{:S(2)}, u32[]{:S(2)}) collective-permute-start(f32[2,64,512]{2,1,0:T(8,128)} %fusion.5), channel_id=1, source_target_pairs={{0,2},{1,3},{2,4},{3,5},{4,0},{5,1},{6,8},{7,9},{8,10},{9,11},{10,... | collective-permute-start | bytes 786440 | tf_op jit(solution)/shard_map/ppermute | solution.py:58
  44.8 0.1 broadcast_subtract_fusion.1
  44.9 0.1 sub.93
  45.0 0.1 dynamic_slice.40
  45.0 0.1 sub.100
  45.1 0.1 dynamic_slice.42
  45.2 0.1 subtract_bitcast_fusion.1
  45.3 14.1 %collective-permute-done.3 = f32[2,64,512]{2,1,0:T(8,128)} collective-permute-done((f32[2,64,512]{2,1,0:T(8,128)}, f32[2,64,512]{2,1,0:T(8,128)}, u32[]{:S(2)}, u32[]{:S(2)}) %collective-permute-start.3) | collective-permute-done | bytes 262176 | tf_op jit(solution)/shard_map/ppermute | solution.py:58
  59.3 9.6 %collective-permute-done.2 = f32[2,64,512]{2,1,0:T(8,128)} collective-permute-done((f32[2,64,512]{2,1,0:T(8,128)}, f32[2,64,512]{2,1,0:T(8,128)}, u32[]{:S(2)}, u32[]{:S(2)}) %collective-permute-start.2) | collective-permute-done | bytes 262176 | tf_op jit(solution)/shard_map/ppermute | solution.py:58
  68.9 1.1 add_add_fusion
  70.0 0.1 fusion.10
  70.2 2.5 %collective-permute-start.4 = (bf16[2,64,512]{2,1,0:T(8,128)(2,1)S(1)}, bf16[2,64,512]{2,1,0:T(8,128)(2,1)S(1)}, u32[]{:S(2)}, u32[]{:S(2)}) collective-permute-start(bf16[2,64,512]{2,1,0:T(8,128)(2,1)S(1)} %pad_maximum_fusion), channel_id=1, source_target_pairs={{0,1},{1,0},{2,3},{3,2},{4,5},{5,4},{6,7},{7,6},{8,9},{9,8},{10,11... | collective-permute-start | bytes 393224 | tf_op jit(solution)/shard_map/ppermute | solution.py:73
  72.7 1.5 collective-permute-done.5
  74.2 2.1 %fusion.13 = f32[128,512]{1,0:T(8,128)S(1)} fusion(bf16[2048,128]{1,0:T(8,128)(2,1)S(1)} %collective-permute-done, bf16[2048,512]{1,0:T(8,128)(2,1)} %collective-permute-done.5), kind=kOutput, calls=%fused_computation.37 | convolution fusion | flops 268435456 | bytes 2883584 | tf_op jit(solution)/shard_map/dot_general | solution.py:24
  76.3 5.2 %collective-permute-start.6 = (f32[1,64,512]{2,1,0:T(8,128)S(1)}, f32[1,64,512]{2,1,0:T(8,128)S(1)}, u32[]{:S(2)}, u32[]{:S(2)}) collective-permute-start(f32[1,64,512]{2,1,0:T(8,128)S(1)} %dynamic-slice_bitcast_fusion), channel_id=1, source_target_pairs={{0,1},{1,0},{2,3},{3,2},{4,5},{5,4},{6,7},{7,6},{8,9},{9,8},{10,11... | collective-permute-start | bytes 393224 | tf_op jit(solution)/shard_map/ppermute | solution.py:55
  81.5 0.0 collective-permute-done.4
  81.5 0.1 maximum_select_fusion.1
  81.6 0.9 collective-permute-done.6
  82.5 22.4 %collective-permute-start.8 = (f32[1,64,512]{2,1,0:T(8,128)S(1)}, f32[1,64,512]{2,1,0:T(8,128)S(1)}, u32[]{:S(2)}, u32[]{:S(2)}) collective-permute-start(f32[1,64,512]{2,1,0:T(8,128)S(1)} %bitcast_add_fusion), channel_id=1, source_target_pairs={{0,4},{1,5},{2,0},{3,1},{4,2},{5,3},{6,10},{7,11},{8,6},{9,7},{10,... | collective-permute-start | bytes 393224 | tf_op jit(solution)/shard_map/ppermute | solution.py:58
  104.9 1.9 %collective-permute-start.7 = (f32[1,64,512]{2,1,0:T(8,128)S(1)}, f32[1,64,512]{2,1,0:T(8,128)S(1)}, u32[]{:S(2)}, u32[]{:S(2)}) collective-permute-start(f32[1,64,512]{2,1,0:T(8,128)S(1)} %bitcast_add_fusion), channel_id=1, source_target_pairs={{0,2},{1,3},{2,4},{3,5},{4,0},{5,1},{6,8},{7,9},{8,10},{9,11},{10,... | collective-permute-start | bytes 393224 | tf_op jit(solution)/shard_map/ppermute | solution.py:58
  106.8 0.8 fusion.6
  107.6 0.0 collective-permute-done.8
  107.6 7.5 %collective-permute-done.7 = f32[1,64,512]{2,1,0:T(8,128)S(1)} collective-permute-done((f32[1,64,512]{2,1,0:T(8,128)S(1)}, f32[1,64,512]{2,1,0:T(8,128)S(1)}, u32[]{:S(2)}, u32[]{:S(2)}) %collective-permute-start.7) | collective-permute-done | bytes 131104 | tf_op jit(solution)/shard_map/ppermute | solution.py:58
  115.1 0.1 fusion.11
  115.2 3.4 %collective-permute-start.10 = (bf16[64,512]{1,0:T(8,128)(2,1)S(1)}, bf16[64,512]{1,0:T(8,128)(2,1)S(1)}, u32[]{:S(2)}, u32[]{:S(2)}) collective-permute-start(bf16[64,512]{1,0:T(8,128)(2,1)S(1)} %fusion.11), channel_id=1, source_target_pairs={{0,1},{1,0},{2,3},{3,2},{4,5},{5,4},{6,7},{7,6},{8,9},{9,8},{10,11... | collective-permute-start | bytes 196616 | tf_op jit(solution)/shard_map/ppermute | solution.py:83
  118.6 2.4 %fusion = f32[2048,64]{0,1:T(8,128)S(1)} fusion(bf16[64,512]{1,0:T(8,128)(2,1)S(1)} %fusion.11, bf16[2048,512]{1,0:T(8,128)(2,1)} %collective-permute-done.5, f32[128,2048]{1,0:T(8,128)S(1)} %fusion.6, s32[]{:T(128)S(6)} %select_n.68), kind=kOutput, calls=%fused_computation.3 | convolution fusion | flops 134348800 | bytes 3211268 | tf_op jit(solution)/shard_map/dot_general | solution.py:30
  120.9 1.9 %collective-permute-start.9 = (f32[2048,64]{0,1:T(8,128)S(1)}, f32[2048,64]{0,1:T(8,128)S(1)}, u32[]{:S(2)}, u32[]{:S(2)}) collective-permute-start(f32[2048,64]{0,1:T(8,128)S(1)} %fusion), channel_id=1, source_target_pairs={{0,6},{6,12},{12,18},{18,24},{24,30},{30,36},{36,42},{42,48},{48,5... | collective-permute-start | bytes 1572872 | tf_op jit(solution)/shard_map/ppermute | solution.py:11
  122.9 0.0 collective-permute-done.10
  122.9 2.4 %fusion.1 = f32[2048,64]{0,1:T(8,128)S(1)} fusion(bf16[64,512]{1,0:T(8,128)(2,1)S(1)} %collective-permute-done.10, bf16[2048,512]{1,0:T(8,128)(2,1)} %collective-permute-done.5, f32[128,2048]{1,0:T(8,128)S(1)} %fusion.6, s32[]{:T(128)S(6)} %select_n.69), kind=kOutput, calls=%fused_computation.4 | convolution fusion | flops 134348800 | bytes 3211268 | tf_op jit(solution)/shard_map/dot_general | solution.py:30
  125.2 1.9 %collective-permute-start.11 = (f32[2048,64]{0,1:T(8,128)S(1)}, f32[2048,64]{0,1:T(8,128)S(1)}, u32[]{:S(2)}, u32[]{:S(2)}) collective-permute-start(f32[2048,64]{0,1:T(8,128)S(1)} %fusion.1), channel_id=1, source_target_pairs={{0,6},{6,12},{12,18},{18,24},{24,30},{30,36},{36,42},{42,48},{48,5... | collective-permute-start | bytes 1572872 | tf_op jit(solution)/shard_map/ppermute | solution.py:11
  127.2 19.6 %collective-permute-done.9 = f32[2048,64]{0,1:T(8,128)S(1)} collective-permute-done((f32[2048,64]{0,1:T(8,128)S(1)}, f32[2048,64]{0,1:T(8,128)S(1)}, u32[]{:S(2)}, u32[]{:S(2)}) %collective-permute-start.9) | collective-permute-done | bytes 524320 | tf_op jit(solution)/shard_map/ppermute | solution.py:11
  146.8 11.2 %collective-permute-done.11 = f32[2048,64]{0,1:T(8,128)S(1)} collective-permute-done((f32[2048,64]{0,1:T(8,128)S(1)}, f32[2048,64]{0,1:T(8,128)S(1)}, u32[]{:S(2)}, u32[]{:S(2)}) %collective-permute-start.11) | collective-permute-done | bytes 524320 | tf_op jit(solution)/shard_map/ppermute | solution.py:11
  158.0 0.8 fusion.2
  158.8 1.3 copy.6
  (10 shorter events, 0.1 us)
Async XLA Ops:
  0.0 24.6 %copy-start = (bf16[2048,512]{1,0:T(8,128)(2,1)S(1)}, bf16[2048,512]{1,0:T(8,128)(2,1)}, u32[]{:S(2)}) copy-start(bf16[2048,512]{1,0:T(8,128)(2,1)} %param.6) | copy-start | bytes 6291460
  0.0 24.6 %collective-permute-start = (bf16[2048,128]{1,0:T(8,128)(2,1)}, bf16[2048,128]{1,0:T(8,128)(2,1)S(1)}, u32[]{:S(2)}, u32[]{:S(2)}) collective-permute-start(bf16[2048,128]{1,0:T(8,128)(2,1)} %param.5), channel_id=1, source_target_pairs={{0,762},{6,0},{12,6},{18,12},{24,18},{30,24},{36,30},{42,36},{48,4... | collective-permute-start | bytes 1572872 | tf_op jit(solution)/shard_map/ppermute | solution.py:11
  13.7 60.6 %collective-permute-start.5 = (bf16[2048,512]{1,0:T(8,128)(2,1)}, bf16[2048,512]{1,0:T(8,128)(2,1)}, u32[]{:S(2)}, u32[]{:S(2)}) collective-permute-start(bf16[2048,512]{1,0:T(8,128)(2,1)} %param.6), channel_id=1, source_target_pairs={{0,6},{6,12},{12,18},{18,24},{24,30},{30,36},{36,42},{42,48},{48,5... | collective-permute-start | bytes 6291464 | tf_op jit(solution)/shard_map/ppermute | solution.py:11
  17.9 11.4 %copy-start.1 = (f32[256]{0:T(256)S(1)}, f32[256]{0:T(256)}, u32[]{:S(2)}) copy-start(f32[256]{0:T(256)} %param.7) | copy-start | bytes 3076
  17.9 26.9 %copy-start.3 = (f32[64]{0:T(128)S(1)}, f32[64]{0:T(128)}, u32[]{:S(2)}) copy-start(f32[64]{0:T(128)} %param.8) | copy-start | bytes 772
  17.9 27.3 %copy-start.2 = (f32[256]{0:T(256)S(1)}, f32[256]{0:T(256)}, u32[]{:S(2)}) copy-start(f32[256]{0:T(256)} %param.9) | copy-start | bytes 3076
  25.8 4.8 %collective-permute-start.1 = (f32[2,64,512]{2,1,0:T(8,128)}, f32[2,64,512]{2,1,0:T(8,128)S(1)}, u32[]{:S(2)}, u32[]{:S(2)}) collective-permute-start(f32[2,64,512]{2,1,0:T(8,128)} %fusion.3), channel_id=1, source_target_pairs={{0,1},{1,0},{2,3},{3,2},{4,5},{5,4},{6,7},{7,6},{8,9},{9,8},{10,11... | collective-permute-start | bytes 786440 | tf_op jit(solution)/shard_map/ppermute | solution.py:55
  31.3 28.1 %collective-permute-start.3 = (f32[2,64,512]{2,1,0:T(8,128)}, f32[2,64,512]{2,1,0:T(8,128)}, u32[]{:S(2)}, u32[]{:S(2)}) collective-permute-start(f32[2,64,512]{2,1,0:T(8,128)} %fusion.5), channel_id=1, source_target_pairs={{0,4},{1,5},{2,0},{3,1},{4,2},{5,3},{6,10},{7,11},{8,6},{9,7},{10,... | collective-permute-start | bytes 786440 | tf_op jit(solution)/shard_map/ppermute | solution.py:58
  42.9 26.0 %collective-permute-start.2 = (f32[2,64,512]{2,1,0:T(8,128)}, f32[2,64,512]{2,1,0:T(8,128)}, u32[]{:S(2)}, u32[]{:S(2)}) collective-permute-start(f32[2,64,512]{2,1,0:T(8,128)} %fusion.5), channel_id=1, source_target_pairs={{0,2},{1,3},{2,4},{3,5},{4,0},{5,1},{6,8},{7,9},{8,10},{9,11},{10,... | collective-permute-start | bytes 786440 | tf_op jit(solution)/shard_map/ppermute | solution.py:58
  70.2 11.3 %collective-permute-start.4 = (bf16[2,64,512]{2,1,0:T(8,128)(2,1)S(1)}, bf16[2,64,512]{2,1,0:T(8,128)(2,1)S(1)}, u32[]{:S(2)}, u32[]{:S(2)}) collective-permute-start(bf16[2,64,512]{2,1,0:T(8,128)(2,1)S(1)} %pad_maximum_fusion), channel_id=1, source_target_pairs={{0,1},{1,0},{2,3},{3,2},{4,5},{5,4},{6,7},{7,6},{8,9},{9,8},{10,11... | collective-permute-start | bytes 393224 | tf_op jit(solution)/shard_map/ppermute | solution.py:73
  76.3 6.1 %collective-permute-start.6 = (f32[1,64,512]{2,1,0:T(8,128)S(1)}, f32[1,64,512]{2,1,0:T(8,128)S(1)}, u32[]{:S(2)}, u32[]{:S(2)}) collective-permute-start(f32[1,64,512]{2,1,0:T(8,128)S(1)} %dynamic-slice_bitcast_fusion), channel_id=1, source_target_pairs={{0,1},{1,0},{2,3},{3,2},{4,5},{5,4},{6,7},{7,6},{8,9},{9,8},{10,11... | collective-permute-start | bytes 393224 | tf_op jit(solution)/shard_map/ppermute | solution.py:55
  82.5 25.1 %collective-permute-start.8 = (f32[1,64,512]{2,1,0:T(8,128)S(1)}, f32[1,64,512]{2,1,0:T(8,128)S(1)}, u32[]{:S(2)}, u32[]{:S(2)}) collective-permute-start(f32[1,64,512]{2,1,0:T(8,128)S(1)} %bitcast_add_fusion), channel_id=1, source_target_pairs={{0,4},{1,5},{2,0},{3,1},{4,2},{5,3},{6,10},{7,11},{8,6},{9,7},{10,... | collective-permute-start | bytes 393224 | tf_op jit(solution)/shard_map/ppermute | solution.py:58
  104.9 10.2 %collective-permute-start.7 = (f32[1,64,512]{2,1,0:T(8,128)S(1)}, f32[1,64,512]{2,1,0:T(8,128)S(1)}, u32[]{:S(2)}, u32[]{:S(2)}) collective-permute-start(f32[1,64,512]{2,1,0:T(8,128)S(1)} %bitcast_add_fusion), channel_id=1, source_target_pairs={{0,2},{1,3},{2,4},{3,5},{4,0},{5,1},{6,8},{7,9},{8,10},{9,11},{10,... | collective-permute-start | bytes 393224 | tf_op jit(solution)/shard_map/ppermute | solution.py:58
  115.2 7.7 %collective-permute-start.10 = (bf16[64,512]{1,0:T(8,128)(2,1)S(1)}, bf16[64,512]{1,0:T(8,128)(2,1)S(1)}, u32[]{:S(2)}, u32[]{:S(2)}) collective-permute-start(bf16[64,512]{1,0:T(8,128)(2,1)S(1)} %fusion.11), channel_id=1, source_target_pairs={{0,1},{1,0},{2,3},{3,2},{4,5},{5,4},{6,7},{7,6},{8,9},{9,8},{10,11... | collective-permute-start | bytes 196616 | tf_op jit(solution)/shard_map/ppermute | solution.py:83
  120.9 25.8 %collective-permute-start.9 = (f32[2048,64]{0,1:T(8,128)S(1)}, f32[2048,64]{0,1:T(8,128)S(1)}, u32[]{:S(2)}, u32[]{:S(2)}) collective-permute-start(f32[2048,64]{0,1:T(8,128)S(1)} %fusion), channel_id=1, source_target_pairs={{0,6},{6,12},{12,18},{18,24},{24,30},{30,36},{36,42},{42,48},{48,5... | collective-permute-start | bytes 1572872 | tf_op jit(solution)/shard_map/ppermute | solution.py:11
  125.2 32.8 %collective-permute-start.11 = (f32[2048,64]{0,1:T(8,128)S(1)}, f32[2048,64]{0,1:T(8,128)S(1)}, u32[]{:S(2)}, u32[]{:S(2)}) collective-permute-start(f32[2048,64]{0,1:T(8,128)S(1)} %fusion.1), channel_id=1, source_target_pairs={{0,6},{6,12},{12,18},{18,24},{24,30},{30,36},{36,42},{42,48},{48,5... | collective-permute-start | bytes 1572872 | tf_op jit(solution)/shard_map/ppermute | solution.py:11

commit v9 on v7

--- a/solution.py
+++ b/solution.py
@@ -67,8 +67,11 @@
 
     cols_prev = shifted(b_cols, "occ", 1)
     rows_next = shifted(b_rows, "occ", -1)
-    early = chip_reduce(core_reduce([partial_integrals(b_rows, b_cols), partial_integrals(rows_next, b_cols)]))
-    late = chip_reduce(core_reduce([partial_integrals(rows_next, cols_prev)]))
+    early_core = core_reduce([partial_integrals(b_rows, b_cols), partial_integrals(rows_next, b_cols)])
+    late_core = core_reduce([partial_integrals(rows_next, cols_prev)])
+    early_core, late_core = lax.optimization_barrier((early_core, late_core))
+    summed = chip_reduce(jnp.concatenate([early_core, late_core]))
+    early, late = summed[:2], summed[2:]
     amp_halves = jnp.stack([
         amplitude_half(early[0], 0, 0), amplitude_half(early[1], 1, 0), amplitude_half(late[0], 1, -1)
     ])

time: 146 us -> 157 us (1.075)
  waiting for transfers between devices: 60.1 us -> 84 us
  starting transfers between devices: 66.6 us -> 53.8 us
    ppermute x4 -> x2, waiting for transfers between devices: 10.3 us -> 33.7 us  [chip_reduce(): lax.ppermute(summed, 'aux', aux_pairs(aux_size, 0, d))]
    ppermute x4 -> x2, starting transfers between devices: 23.5 us -> 13.5 us  [chip_reduce(): lax.ppermute(summed, 'aux', aux_pairs(aux_size, 0, d))]
    ppermute x2, starting transfers between devices: 21.3 us -> 18.4 us  [core_reduce(): return keep + lax.ppermute(give, 'aux', aux_pairs(aux_size, 1, 0))]
  transfers between devices with their start and end apart: 11 -> 9, of which waited for: 8 -> 7; matrix products, arithmetic and copies ran while one was open for 10% -> 8% of each run, Pallas kernels for 0% -> 0%
where the time goes in v9:
time: 157 us; the launch traced here: 156 us
  waiting for transfers between devices  84 us (54%)
  starting transfers between devices  53.8 us (34%)
  matrix products  13.4 us (9%)
  local copies, waits for them, and re-layouts  3.42 us (2%)
  other arithmetic  1.58 us (1%)
    ppermute x4, waiting for transfers between devices, shifted(): lax.ppermute(value, axis, [(i, (i + by) % size) for i in range(size)])  49.4 us
    ppermute x2, waiting for transfers between devices, chip_reduce(): lax.ppermute(summed, 'aux', aux_pairs(aux_size, 0, d))  33.7 us
    ppermute x4, starting transfers between devices, shifted(): lax.ppermute(value, axis, [(i, (i + by) % size) for i in range(size)])  19.4 us
    ppermute x2, starting transfers between devices, core_reduce(): return keep + lax.ppermute(give, 'aux', aux_pairs(aux_size, 1, 0))  18.4 us
    ppermute x2, starting transfers between devices, chip_reduce(): lax.ppermute(summed, 'aux', aux_pairs(aux_size, 0, d))  13.5 us
    dot_general x5, matrix products, contribution(): lax.dot_general(right_block, amplitude, (((1,), (1,)), ((), ())), preferr...  8.65 us
    dot_general x3, matrix products, partial_integrals(): lax.dot_general(left_block, right_block, (((0,), (0,)), ((), ())), prefer...  4.76 us
  transfers between devices with their start and end apart: 9, of which 7 were waited for; matrix products, arithmetic and copies ran while one was open for 8% of the time, Pallas kernels for 0%

profile of v9, /device:TPU:1, one launch (start us, length us, event | category | flops | bytes accessed | tf_op | source)
XLA Modules:
  0.0 156.5 jit_solution(4805364178041475665)
XLA Ops:
  0.0 0.0 copy-start
  0.0 4.1 %collective-permute-start.2 = (bf16[2048,512]{1,0:T(8,128)(2,1)}, bf16[2048,512]{1,0:T(8,128)(2,1)}, u32[]{:S(2)}, u32[]{:S(2)}) collective-permute-start(bf16[2048,512]{1,0:T(8,128)(2,1)} %param.6), channel_id=1, source_target_pairs={{0,6},{6,12},{12,18},{18,24},{24,30},{30,36},{36,42},{42,48},{48,5... | collective-permute-start | bytes 6291464 | tf_op jit(solution)/shard_map/ppermute | solution.py:11
  4.2 11.4 %collective-permute-start = (bf16[2048,128]{1,0:T(8,128)(2,1)}, bf16[2048,128]{1,0:T(8,128)(2,1)S(1)}, u32[]{:S(2)}, u32[]{:S(2)}) collective-permute-start(bf16[2048,128]{1,0:T(8,128)(2,1)} %param.5), channel_id=1, source_target_pairs={{0,762},{6,0},{12,6},{18,12},{24,18},{30,24},{36,30},{42,36},{48,4... | collective-permute-start | bytes 1572872 | tf_op jit(solution)/shard_map/ppermute | solution.py:11
  15.7 0.9 fusion.28
  16.6 2.2 %convolution_bitcast_fusion.2 = f32[1,128,512]{2,1,0:T(8,128)S(1)} fusion(bf16[2048,128]{1,0:T(8,128)(2,1)} %param.5, bf16[2048,512]{1,0:T(8,128)(2,1)} %param.6), kind=kOutput, calls=%fused_computation.6 | convolution fusion | flops 268435456 | bytes 2883584 | tf_op jit(solution)/shard_map/dot_general | solution.py:24
  18.8 3.2 %collective-permute-done = bf16[2048,128]{1,0:T(8,128)(2,1)S(1)} collective-permute-done((bf16[2048,128]{1,0:T(8,128)(2,1)}, bf16[2048,128]{1,0:T(8,128)(2,1)S(1)}, u32[]{:S(2)}, u32[]{:S(2)}) %collective-permute-start) | collective-permute-done | bytes 524320 | tf_op jit(solution)/shard_map/ppermute | solution.py:11
  22.0 0.0 copy-done
  22.0 0.5 convolution_bitcast_fusion.1
  22.5 0.0 copy-start.3
  22.5 0.0 copy-start.2
  22.6 9.4 %collective-permute-start.1 = (f32[2,64,512]{2,1,0:T(8,128)S(1)}, f32[2,64,512]{2,1,0:T(8,128)S(1)}, u32[]{:S(2)}, u32[]{:S(2)}) collective-permute-start(f32[2,64,512]{2,1,0:T(8,128)S(1)} %fusion.3), channel_id=1, source_target_pairs={{0,1},{1,0},{2,3},{3,2},{4,5},{5,4},{6,7},{7,6},{8,9},{9,8},{10,11... | collective-permute-start | bytes 786440 | tf_op jit(solution)/shard_map/ppermute | solution.py:55
  31.9 21.5 %collective-permute-done.2 = bf16[2048,512]{1,0:T(8,128)(2,1)} collective-permute-done((bf16[2048,512]{1,0:T(8,128)(2,1)}, bf16[2048,512]{1,0:T(8,128)(2,1)}, u32[]{:S(2)}, u32[]{:S(2)}) %collective-permute-start.2) | collective-permute-done | bytes 2097184 | tf_op jit(solution)/shard_map/ppermute | solution.py:11
  53.4 2.1 %fusion.29 = f32[128,512]{1,0:T(8,128)S(1)} fusion(bf16[2048,128]{1,0:T(8,128)(2,1)S(1)} %collective-permute-done, bf16[2048,512]{1,0:T(8,128)(2,1)} %collective-permute-done.2), kind=kOutput, calls=%fused_computation.60 | convolution fusion | flops 268435456 | bytes 2883584 | tf_op jit(solution)/shard_map/dot_general | solution.py:24
  55.5 9.1 %collective-permute-start.3 = (f32[1,64,512]{2,1,0:T(8,128)S(1)}, f32[1,64,512]{2,1,0:T(8,128)S(1)}, u32[]{:S(2)}, u32[]{:S(2)}) collective-permute-start(f32[1,64,512]{2,1,0:T(8,128)S(1)} %dynamic-slice_bitcast_fusion), channel_id=1, source_target_pairs={{0,1},{1,0},{2,3},{3,2},{4,5},{5,4},{6,7},{7,6},{8,9},{9,8},{10,11... | collective-permute-start | bytes 393224 | tf_op jit(solution)/shard_map/ppermute | solution.py:55
  64.6 0.0 collective-permute-done.1
  64.6 0.9 collective-permute-done.3
  65.6 10.3 %collective-permute-start.4 = (f32[3,64,512]{2,1,0:T(8,128)S(1)}, f32[3,64,512]{2,1,0:T(8,128)S(1)}, u32[]{:S(2)}, u32[]{:S(2)}) collective-permute-start(f32[3,64,512]{2,1,0:T(8,128)S(1)} %constant_dynamic-update-slice_fusion), channel_id=1, source_target_pairs={{0,2},{1,3},{2,4},{3,5},{4,0},{5,1},{6,8},{7,9},{8,10},{9,11},{10,... | collective-permute-start | bytes 1179656 | tf_op jit(solution)/shard_map/ppermute | solution.py:58
  75.9 3.2 %collective-permute-start.5 = (f32[3,64,512]{2,1,0:T(8,128)S(1)}, f32[3,64,512]{2,1,0:T(8,128)}, u32[]{:S(2)}, u32[]{:S(2)}) collective-permute-start(f32[3,64,512]{2,1,0:T(8,128)S(1)} %constant_dynamic-update-slice_fusion), channel_id=1, source_target_pairs={{0,4},{1,5},{2,0},{3,1},{4,2},{5,3},{6,10},{7,11},{8,6},{9,7},{10,... | collective-permute-start | bytes 1179656 | tf_op jit(solution)/shard_map/ppermute | solution.py:58
  79.1 0.0 copy-done.3
  79.1 0.1 broadcast_subtract_fusion.1
  79.2 0.1 sub.99
  79.3 0.1 dynamic_slice.38
  79.3 0.0 copy-done.2
  79.4 0.1 subtract_bitcast_fusion.1
  79.4 0.1 sub.92
  79.5 0.1 dynamic_slice.36
  79.6 31.9 %collective-permute-done.4 = f32[3,64,512]{2,1,0:T(8,128)S(1)} collective-permute-done((f32[3,64,512]{2,1,0:T(8,128)S(1)}, f32[3,64,512]{2,1,0:T(8,128)S(1)}, u32[]{:S(2)}, u32[]{:S(2)}) %collective-permute-start.4) | collective-permute-done | bytes 393248 | tf_op jit(solution)/shard_map/ppermute | solution.py:58
  111.5 1.8 %collective-permute-done.5 = f32[3,64,512]{2,1,0:T(8,128)} collective-permute-done((f32[3,64,512]{2,1,0:T(8,128)S(1)}, f32[3,64,512]{2,1,0:T(8,128)}, u32[]{:S(2)}, u32[]{:S(2)}) %collective-permute-start.5) | collective-permute-done | bytes 393248 | tf_op jit(solution)/shard_map/ppermute | solution.py:58
  113.3 1.1 add_add_fusion
  114.4 0.8 fusion.15
  115.2 0.1 divide_convert_fusion.2
  115.3 2.4 %collective-permute-start.6 = (bf16[3,64,512]{2,1,0:T(8,128)(2,1)S(1)}, bf16[3,64,512]{2,1,0:T(8,128)(2,1)S(1)}, u32[]{:S(2)}, u32[]{:S(2)}) collective-permute-start(bf16[3,64,512]{2,1,0:T(8,128)(2,1)S(1)} %pad_maximum_fusion), channel_id=1, source_target_pairs={{0,1},{1,0},{2,3},{3,2},{4,5},{5,4},{6,7},{7,6},{8,9},{9,8},{10,11... | collective-permute-start | bytes 589832 | tf_op jit(solution)/shard_map/ppermute | solution.py:80
  117.7 2.4 %fusion = f32[2048,64]{0,1:T(8,128)S(1)} fusion(f32[64,2048]{1,0:T(8,128)S(1)} %fusion.15, bf16[2048,512]{1,0:T(8,128)(2,1)} %collective-permute-done.2, f32[3,64,512]{2,1,0:T(8,128)S(1)} %add_add_fusion, f32[512]{0:T(512)S(1)} %bitcast.59, f32[64]{0:T(128)S(1)} %dynamic_slice.38), kind=kOutput, calls=%fused_computation.3 | convolution fusion | flops 134479872 | bytes 3279360 | tf_op jit(solution)/shard_map/dot_general | solution.py:30
  120.1 1.9 %collective-permute-start.7 = (f32[2048,64]{0,1:T(8,128)S(1)}, f32[2048,64]{0,1:T(8,128)}, u32[]{:S(2)}, u32[]{:S(2)}) collective-permute-start(f32[2048,64]{0,1:T(8,128)S(1)} %fusion), channel_id=1, source_target_pairs={{0,6},{6,12},{12,18},{18,24},{24,30},{30,36},{36,42},{42,48},{48,5... | collective-permute-start | bytes 1572872 | tf_op jit(solution)/shard_map/ppermute | solution.py:11
  122.0 0.0 collective-permute-done.6
  122.1 0.0 copy-start.1
  122.1 2.4 %fusion.18 = f32[64,2048]{1,0:T(8,128)S(1)} fusion(bf16[2048,512]{1,0:T(8,128)(2,1)} %collective-permute-done.2, bf16[3,64,512]{2,1,0:T(8,128)(2,1)S(1)} %collective-permute-done.6), kind=kOutput, calls=%fused_computation.41 | convolution fusion | flops 134217728 | bytes 2686976 | tf_op jit(solution)/shard_map/dot_general | solution.py:30
  124.5 0.8 fusion.1
  125.2 0.0 copy-done.1
  125.3 1.9 %collective-permute-start.8 = (f32[2048,64]{0,1:T(8,128)S(1)}, f32[2048,64]{0,1:T(8,128)}, u32[]{:S(2)}, u32[]{:S(2)}) collective-permute-start(f32[2048,64]{0,1:T(8,128)S(1)} %fusion.1), channel_id=1, source_target_pairs={{0,6},{6,12},{12,18},{18,24},{24,30},{30,36},{36,42},{42,48},{48,5... | collective-permute-start | bytes 1572872 | tf_op jit(solution)/shard_map/ppermute | solution.py:11
  127.2 0.1 fusion.13
  127.3 0.8 slice_bitcast_fusion.4
  128.1 13.5 %collective-permute-done.7 = f32[2048,64]{0,1:T(8,128)} collective-permute-done((f32[2048,64]{0,1:T(8,128)S(1)}, f32[2048,64]{0,1:T(8,128)}, u32[]{:S(2)}, u32[]{:S(2)}) %collective-permute-start.7) | collective-permute-done | bytes 524320 | tf_op jit(solution)/shard_map/ppermute | solution.py:11
  141.6 11.2 %collective-permute-done.8 = f32[2048,64]{0,1:T(8,128)} collective-permute-done((f32[2048,64]{0,1:T(8,128)S(1)}, f32[2048,64]{0,1:T(8,128)}, u32[]{:S(2)}, u32[]{:S(2)}) %collective-permute-start.8) | collective-permute-done | bytes 524320 | tf_op jit(solution)/shard_map/ppermute | solution.py:11
  152.8 2.3 %fusion.2 = f32[2048,128]{0,1:T(8,128)S(1)} fusion(f32[2048,64]{0,1:T(8,128)} %collective-permute-done.8, f32[2048,64]{0,1:T(8,128)} %collective-permute-done.7, pred[]{:T(512)S(6)} %eq.12, bf16[2048,512]{1,0:T(8,128)(2,1)S(1)} %copy-done, bf16[64,512]{1,0:T(8,128)(2,1)S(1)} %slice_bitcast_fusion.4, bf16[64,512]{1,0:T(8,128)(2,1)S(1)} %fusion.13), kind=kOutput, calls=%fused_computation.8 | convolution fusion | flops 270073856 | bytes 4325377 | tf_op jit(solution)/shard_map/dot_general | solution.py:30
  155.2 1.3 copy.6
  (9 shorter events, 0.2 us)
Async XLA Ops:
  0.0 22.0 %copy-start = (bf16[2048,512]{1,0:T(8,128)(2,1)S(1)}, bf16[2048,512]{1,0:T(8,128)(2,1)}, u32[]{:S(2)}) copy-start(bf16[2048,512]{1,0:T(8,128)(2,1)} %param.6) | copy-start | bytes 6291460
  0.0 53.4 %collective-permute-start.2 = (bf16[2048,512]{1,0:T(8,128)(2,1)}, bf16[2048,512]{1,0:T(8,128)(2,1)}, u32[]{:S(2)}, u32[]{:S(2)}) collective-permute-start(bf16[2048,512]{1,0:T(8,128)(2,1)} %param.6), channel_id=1, source_target_pairs={{0,6},{6,12},{12,18},{18,24},{24,30},{30,36},{36,42},{42,48},{48,5... | collective-permute-start | bytes 6291464 | tf_op jit(solution)/shard_map/ppermute | solution.py:11
  4.2 17.9 %collective-permute-start = (bf16[2048,128]{1,0:T(8,128)(2,1)}, bf16[2048,128]{1,0:T(8,128)(2,1)S(1)}, u32[]{:S(2)}, u32[]{:S(2)}) collective-permute-start(bf16[2048,128]{1,0:T(8,128)(2,1)} %param.5), channel_id=1, source_target_pairs={{0,762},{6,0},{12,6},{18,12},{24,18},{30,24},{36,30},{42,36},{48,4... | collective-permute-start | bytes 1572872 | tf_op jit(solution)/shard_map/ppermute | solution.py:11
  22.5 56.6 %copy-start.3 = (f32[64]{0:T(128)S(1)}, f32[64]{0:T(128)}, u32[]{:S(2)}) copy-start(f32[64]{0:T(128)} %param.8) | copy-start | bytes 772
  22.5 56.8 %copy-start.2 = (f32[256]{0:T(256)S(1)}, f32[256]{0:T(256)}, u32[]{:S(2)}) copy-start(f32[256]{0:T(256)} %param.9) | copy-start | bytes 3076
  22.6 42.0 %collective-permute-start.1 = (f32[2,64,512]{2,1,0:T(8,128)S(1)}, f32[2,64,512]{2,1,0:T(8,128)S(1)}, u32[]{:S(2)}, u32[]{:S(2)}) collective-permute-start(f32[2,64,512]{2,1,0:T(8,128)S(1)} %fusion.3), channel_id=1, source_target_pairs={{0,1},{1,0},{2,3},{3,2},{4,5},{5,4},{6,7},{7,6},{8,9},{9,8},{10,11... | collective-permute-start | bytes 786440 | tf_op jit(solution)/shard_map/ppermute | solution.py:55
  55.5 10.1 %collective-permute-start.3 = (f32[1,64,512]{2,1,0:T(8,128)S(1)}, f32[1,64,512]{2,1,0:T(8,128)S(1)}, u32[]{:S(2)}, u32[]{:S(2)}) collective-permute-start(f32[1,64,512]{2,1,0:T(8,128)S(1)} %dynamic-slice_bitcast_fusion), channel_id=1, source_target_pairs={{0,1},{1,0},{2,3},{3,2},{4,5},{5,4},{6,7},{7,6},{8,9},{9,8},{10,11... | collective-permute-start | bytes 393224 | tf_op jit(solution)/shard_map/ppermute | solution.py:55
  65.6 45.9 %collective-permute-start.4 = (f32[3,64,512]{2,1,0:T(8,128)S(1)}, f32[3,64,512]{2,1,0:T(8,128)S(1)}, u32[]{:S(2)}, u32[]{:S(2)}) collective-permute-start(f32[3,64,512]{2,1,0:T(8,128)S(1)} %constant_dynamic-update-slice_fusion), channel_id=1, source_target_pairs={{0,2},{1,3},{2,4},{3,5},{4,0},{5,1},{6,8},{7,9},{8,10},{9,11},{10,... | collective-permute-start | bytes 1179656 | tf_op jit(solution)/shard_map/ppermute | solution.py:58
  75.9 37.4 %collective-permute-start.5 = (f32[3,64,512]{2,1,0:T(8,128)S(1)}, f32[3,64,512]{2,1,0:T(8,128)}, u32[]{:S(2)}, u32[]{:S(2)}) collective-permute-start(f32[3,64,512]{2,1,0:T(8,128)S(1)} %constant_dynamic-update-slice_fusion), channel_id=1, source_target_pairs={{0,4},{1,5},{2,0},{3,1},{4,2},{5,3},{6,10},{7,11},{8,6},{9,7},{10,... | collective-permute-start | bytes 1179656 | tf_op jit(solution)/shard_map/ppermute | solution.py:58
  115.3 6.7 %collective-permute-start.6 = (bf16[3,64,512]{2,1,0:T(8,128)(2,1)S(1)}, bf16[3,64,512]{2,1,0:T(8,128)(2,1)S(1)}, u32[]{:S(2)}, u32[]{:S(2)}) collective-permute-start(bf16[3,64,512]{2,1,0:T(8,128)(2,1)S(1)} %pad_maximum_fusion), channel_id=1, source_target_pairs={{0,1},{1,0},{2,3},{3,2},{4,5},{5,4},{6,7},{7,6},{8,9},{9,8},{10,11... | collective-permute-start | bytes 589832 | tf_op jit(solution)/shard_map/ppermute | solution.py:80
  120.1 21.5 %collective-permute-start.7 = (f32[2048,64]{0,1:T(8,128)S(1)}, f32[2048,64]{0,1:T(8,128)}, u32[]{:S(2)}, u32[]{:S(2)}) collective-permute-start(f32[2048,64]{0,1:T(8,128)S(1)} %fusion), channel_id=1, source_target_pairs={{0,6},{6,12},{12,18},{18,24},{24,30},{30,36},{36,42},{42,48},{48,5... | collective-permute-start | bytes 1572872 | tf_op jit(solution)/shard_map/ppermute | solution.py:11
  122.1 3.2 %copy-start.1 = (bf16[3,64,512]{2,1,0:T(8,128)(2,1)}, bf16[3,64,512]{2,1,0:T(8,128)(2,1)S(1)}, u32[]{:S(2)}) copy-start(bf16[3,64,512]{2,1,0:T(8,128)(2,1)S(1)} %collective-permute-done.6) | copy-start | bytes 589828
  125.3 27.6 %collective-permute-start.8 = (f32[2048,64]{0,1:T(8,128)S(1)}, f32[2048,64]{0,1:T(8,128)}, u32[]{:S(2)}, u32[]{:S(2)}) collective-permute-start(f32[2048,64]{0,1:T(8,128)S(1)} %fusion.1), channel_id=1, source_target_pairs={{0,6},{6,12},{12,18},{18,24},{24,30},{30,36},{36,42},{42,48},{48,5... | collective-permute-start | bytes 1572872 | tf_op jit(solution)/shard_map/ppermute | solution.py:11

commit v10 on v9

--- a/solution.py
+++ b/solution.py
@@ -70,11 +70,29 @@
     early_core = core_reduce([partial_integrals(b_rows, b_cols), partial_integrals(rows_next, b_cols)])
     late_core = core_reduce([partial_integrals(rows_next, cols_prev)])
     early_core, late_core = lax.optimization_barrier((early_core, late_core))
-    summed = chip_reduce(jnp.concatenate([early_core, late_core]))
-    early, late = summed[:2], summed[2:]
-    amp_halves = jnp.stack([
-        amplitude_half(early[0], 0, 0), amplitude_half(early[1], 1, 0), amplitude_half(late[0], 1, -1)
-    ])
+    chip = aux_pos // 2
+    piece = -(-(-(-half // chips)) // 8) * 8
+    padded = jnp.pad(jnp.concatenate([early_core, late_core]), ((0, 0), (0, piece * chips - half), (0, 0)))
+    parts = padded.reshape(padded.shape[0], chips, piece, padded.shape[2])
+    mine = lax.dynamic_index_in_dim(parts, chip, 1, keepdims=False)
+    for d in range(1, chips):
+        give = lax.dynamic_index_in_dim(parts, (chip + d) % chips, 1, keepdims=False)
+        mine = mine + lax.ppermute(give, "aux", aux_pairs(aux_size, 0, d))
+
+    def amplitude_part(summed, row_shift, col_shift):
+        row_energy = lax.dynamic_slice_in_dim(energy(row_shift, eps_va), core * half, half, 0)
+        row_energy = jnp.pad(row_energy, (0, piece * chips - half), constant_values=1.0)
+        row_energy = lax.dynamic_slice_in_dim(row_energy, chip * piece, piece, 0)
+        col_energy = energy(col_shift, eps_vb)
+        return (spin_scale * summed / (row_energy[:, None] + col_energy[None, :])).astype(jnp.bfloat16)
+
+    amp_mine = jnp.stack([amplitude_part(mine[0], 0, 0), amplitude_part(mine[1], 1, 0), amplitude_part(mine[2], 1, -1)])
+    whole = jnp.zeros((3, chips, piece, amp_mine.shape[2]), amp_mine.dtype)
+    whole = lax.dynamic_update_index_in_dim(whole, amp_mine, chip, 1)
+    for d in range(1, chips):
+        got = lax.ppermute(amp_mine, "aux", aux_pairs(aux_size, 0, d))
+        whole = lax.dynamic_update_index_in_dim(whole, got, (chip - d) % chips, 1)
+    amp_halves = whole.reshape(3, chips * piece, amp_mine.shape[2])[:, :half]
     near_first = contribution(b_cols, amp_halves[1]) + contribution(cols_prev, amp_halves[2])
     sent_first = shifted(near_first, "occ", 1)
     amp_other = lax.ppermute(amp_halves, "aux", aux_pairs(aux_size, 1, 0))

time: 157 us -> 153 us (0.975)
  waiting for transfers between devices: 84 us -> 67.3 us
  starting transfers between devices: 53.8 us -> 66.3 us
    ppermute x2 -> x4, waiting for transfers between devices: 33.7 us -> 19.3 us  [the longest x2 12.5 us: per_device(): mine = mine + lax.ppermute(give, 'aux', aux_pairs(aux_size, 0, d))]
    ppermute x2 -> x4, starting transfers between devices: 13.5 us -> 22.7 us  [the longest x2 13.5 us: per_device(): mine = mine + lax.ppermute(give, 'aux', aux_pairs(aux_size, 0, d))]
    ppermute x4, waiting for transfers between devices: 49.4 us -> 47.1 us  [shifted(): lax.ppermute(value, axis, [(i, (i + by) % size) for i in range(size)])]
    ppermute x1, starting transfers between devices: 2.4 us -> 4.2 us  [per_device(): amp_other = lax.ppermute(amp_halves, 'aux', aux_pairs(aux_size, 1, 0))]
  transfers between devices with their start and end apart: 9 -> 11, of which waited for: 7 -> 8; matrix products, arithmetic and copies ran while one was open for 8% -> 9% of each run, Pallas kernels for 0% -> 0%
where the time goes in v10:
time: 153 us; the launch traced here: 152 us
  waiting for transfers between devices  67.3 us (44%)
  starting transfers between devices  66.3 us (43%)
  matrix products  13.3 us (9%)
  local copies, waits for them, and re-layouts  3.55 us (2%)
    ppermute x4, waiting for transfers between devices, shifted(): lax.ppermute(value, axis, [(i, (i + by) % size) for i in range(size)])  47.1 us
    ppermute x4, starting transfers between devices, shifted(): lax.ppermute(value, axis, [(i, (i + by) % size) for i in range(size)])  21 us
    ppermute x2, starting transfers between devices, core_reduce(): return keep + lax.ppermute(give, 'aux', aux_pairs(aux_size, 1, 0))  18.4 us
    ppermute x2, starting transfers between devices, per_device(): mine = mine + lax.ppermute(give, 'aux', aux_pairs(aux_size, 0, d))  13.5 us
    ppermute x2, waiting for transfers between devices, per_device(): mine = mine + lax.ppermute(give, 'aux', aux_pairs(aux_size, 0, d))  12.5 us
    ppermute x2, starting transfers between devices, per_device(): got = lax.ppermute(amp_mine, 'aux', aux_pairs(aux_size, 0, d))  9.19 us
    dot_general x5, matrix products, contribution(): lax.dot_general(right_block, amplitude, (((1,), (1,)), ((), ())), preferr...  8.59 us
    ppermute x2, waiting for transfers between devices, per_device(): got = lax.ppermute(amp_mine, 'aux', aux_pairs(aux_size, 0, d))  6.8 us
  transfers between devices with their start and end apart: 11, of which 8 were waited for; matrix products, arithmetic and copies ran while one was open for 9% of the time, Pallas kernels for 0%

profile of v10, /device:TPU:1, one launch (start us, length us, event | category | flops | bytes accessed | tf_op | source)
XLA Modules:
  0.0 152.0 jit_solution(46435722592034701)
XLA Ops:
  0.0 0.0 copy-start
  0.0 4.1 %collective-permute-start.2 = (bf16[2048,512]{1,0:T(8,128)(2,1)}, bf16[2048,512]{1,0:T(8,128)(2,1)}, u32[]{:S(2)}, u32[]{:S(2)}) collective-permute-start(bf16[2048,512]{1,0:T(8,128)(2,1)} %param.6), channel_id=1, source_target_pairs={{0,6},{6,12},{12,18},{18,24},{24,30},{30,36},{36,42},{42,48},{48,5... | collective-permute-start | bytes 6291464 | tf_op jit(solution)/shard_map/ppermute | solution.py:11
  4.2 11.4 %collective-permute-start = (bf16[2048,128]{1,0:T(8,128)(2,1)}, bf16[2048,128]{1,0:T(8,128)(2,1)S(1)}, u32[]{:S(2)}, u32[]{:S(2)}) collective-permute-start(bf16[2048,128]{1,0:T(8,128)(2,1)} %param.5), channel_id=1, source_target_pairs={{0,762},{6,0},{12,6},{18,12},{24,18},{30,24},{36,30},{42,36},{48,4... | collective-permute-start | bytes 1572872 | tf_op jit(solution)/shard_map/ppermute | solution.py:11
  15.7 0.9 fusion.22
  16.6 0.8 subtract_bitcast_fusion.1
  17.4 2.2 %convolution_bitcast_fusion.2 = f32[1,128,512]{2,1,0:T(8,128)S(1)} fusion(bf16[2048,128]{1,0:T(8,128)(2,1)} %param.5, bf16[2048,512]{1,0:T(8,128)(2,1)} %param.6), kind=kOutput, calls=%fused_computation.6 | convolution fusion | flops 268435456 | bytes 2883584 | tf_op jit(solution)/shard_map/dot_general | solution.py:24
  19.6 2.4 %collective-permute-done = bf16[2048,128]{1,0:T(8,128)(2,1)S(1)} collective-permute-done((bf16[2048,128]{1,0:T(8,128)(2,1)}, bf16[2048,128]{1,0:T(8,128)(2,1)S(1)}, u32[]{:S(2)}, u32[]{:S(2)}) %collective-permute-start) | collective-permute-done | bytes 524320 | tf_op jit(solution)/shard_map/ppermute | solution.py:11
  22.0 0.0 copy-done
  22.0 0.5 convolution_bitcast_fusion.1
  22.5 9.4 %collective-permute-start.1 = (f32[2,64,512]{2,1,0:T(8,128)S(1)}, f32[2,64,512]{2,1,0:T(8,128)S(1)}, u32[]{:S(2)}, u32[]{:S(2)}) collective-permute-start(f32[2,64,512]{2,1,0:T(8,128)S(1)} %fusion.3), channel_id=1, source_target_pairs={{0,1},{1,0},{2,3},{3,2},{4,5},{5,4},{6,7},{7,6},{8,9},{9,8},{10,11... | collective-permute-start | bytes 786440 | tf_op jit(solution)/shard_map/ppermute | solution.py:55
  31.9 21.5 %collective-permute-done.2 = bf16[2048,512]{1,0:T(8,128)(2,1)} collective-permute-done((bf16[2048,512]{1,0:T(8,128)(2,1)}, bf16[2048,512]{1,0:T(8,128)(2,1)}, u32[]{:S(2)}, u32[]{:S(2)}) %collective-permute-start.2) | collective-permute-done | bytes 2097184 | tf_op jit(solution)/shard_map/ppermute | solution.py:11
  53.4 2.1 %fusion.23 = f32[128,512]{1,0:T(8,128)S(1)} fusion(bf16[2048,128]{1,0:T(8,128)(2,1)S(1)} %collective-permute-done, bf16[2048,512]{1,0:T(8,128)(2,1)} %collective-permute-done.2), kind=kOutput, calls=%fused_computation.60 | convolution fusion | flops 268435456 | bytes 2883584 | tf_op jit(solution)/shard_map/dot_general | solution.py:24
  55.4 0.0 copy-start.2
  55.5 9.1 %collective-permute-start.3 = (f32[1,64,512]{2,1,0:T(8,128)S(1)}, f32[1,64,512]{2,1,0:T(8,128)S(1)}, u32[]{:S(2)}, u32[]{:S(2)}) collective-permute-start(f32[1,64,512]{2,1,0:T(8,128)S(1)} %dynamic-slice_bitcast_fusion.2), channel_id=1, source_target_pairs={{0,1},{1,0},{2,3},{3,2},{4,5},{5,4},{6,7},{7,6},{8,9},{9,8},{10,11... | collective-permute-start | bytes 393224 | tf_op jit(solution)/shard_map/ppermute | solution.py:55
  64.6 0.0 collective-permute-done.1
  64.6 0.9 collective-permute-done.3
  65.6 10.3 %collective-permute-start.4 = (f32[3,24,512]{2,1,0:T(8,128)S(1)}, f32[3,24,512]{2,1,0:T(8,128)S(1)}, u32[]{:S(2)}, u32[]{:S(2)}) collective-permute-start(f32[3,24,512]{2,1,0:T(8,128)S(1)} %get-tuple-element.9), channel_id=1, source_target_pairs={{0,2},{1,3},{2,4},{3,5},{4,0},{5,1},{6,8},{7,9},{8,10},{9,11},{10,... | collective-permute-start | bytes 442376 | tf_op jit(solution)/shard_map/ppermute | solution.py:80
  76.0 3.2 %collective-permute-start.5 = (f32[3,24,512]{2,1,0:T(8,128)S(1)}, f32[3,24,512]{2,1,0:T(8,128)S(1)}, u32[]{:S(2)}, u32[]{:S(2)}) collective-permute-start(f32[3,24,512]{2,1,0:T(8,128)S(1)} %get-tuple-element.10), channel_id=1, source_target_pairs={{0,4},{1,5},{2,0},{3,1},{4,2},{5,3},{6,10},{7,11},{8,6},{9,7},{10,... | collective-permute-start | bytes 442376 | tf_op jit(solution)/shard_map/ppermute | solution.py:80
  79.1 0.0 copy-done.2
  79.2 0.1 broadcast_subtract_fusion.1
  79.2 0.1 sub.103
  79.3 0.1 dynamic_slice.56
  79.4 0.1 sub.110
  79.5 0.1 dynamic_slice.59
  79.6 0.1 pad_dynamic-slice_fusion.4
  79.6 10.7 %collective-permute-done.4 = f32[3,24,512]{2,1,0:T(8,128)S(1)} collective-permute-done((f32[3,24,512]{2,1,0:T(8,128)S(1)}, f32[3,24,512]{2,1,0:T(8,128)S(1)}, u32[]{:S(2)}, u32[]{:S(2)}) %collective-permute-start.4) | collective-permute-done | bytes 147488 | tf_op jit(solution)/shard_map/ppermute | solution.py:80
  90.3 1.8 %collective-permute-done.5 = f32[3,24,512]{2,1,0:T(8,128)S(1)} collective-permute-done((f32[3,24,512]{2,1,0:T(8,128)S(1)}, f32[3,24,512]{2,1,0:T(8,128)S(1)}, u32[]{:S(2)}, u32[]{:S(2)}) %collective-permute-start.5) | collective-permute-done | bytes 147488 | tf_op jit(solution)/shard_map/ppermute | solution.py:80
  92.1 0.1 fusion.20
  92.2 7.1 %collective-permute-start.6 = (bf16[3,24,512]{2,1,0:T(8,128)(2,1)S(1)}, bf16[3,24,512]{2,1,0:T(8,128)(2,1)S(1)}, u32[]{:S(2)}, u32[]{:S(2)}) collective-permute-start(bf16[3,24,512]{2,1,0:T(8,128)(2,1)S(1)} %pad_maximum_fusion), channel_id=1, source_target_pairs={{0,2},{1,3},{2,4},{3,5},{4,0},{5,1},{6,8},{7,9},{8,10},{9,11},{10,... | collective-permute-start | bytes 221192 | tf_op jit(solution)/shard_map/ppermute | solution.py:93
  99.3 2.1 %collective-permute-start.7 = (bf16[3,24,512]{2,1,0:T(8,128)(2,1)S(1)}, bf16[3,24,512]{2,1,0:T(8,128)(2,1)S(1)}, u32[]{:S(2)}, u32[]{:S(2)}) collective-permute-start(bf16[3,24,512]{2,1,0:T(8,128)(2,1)S(1)} %pad_maximum_fusion), channel_id=1, source_target_pairs={{0,4},{1,5},{2,0},{3,1},{4,2},{5,3},{6,10},{7,11},{8,6},{9,7},{10,... | collective-permute-start | bytes 221192 | tf_op jit(solution)/shard_map/ppermute | solution.py:93
  101.5 0.0 collective-permute-done.6
  101.5 6.8 %collective-permute-done.7 = bf16[3,24,512]{2,1,0:T(8,128)(2,1)S(1)} collective-permute-done((bf16[3,24,512]{2,1,0:T(8,128)(2,1)S(1)}, bf16[3,24,512]{2,1,0:T(8,128)(2,1)S(1)}, u32[]{:S(2)}, u32[]{:S(2)}) %collective-permute-start.7) | collective-permute-done | bytes 73760 | tf_op jit(solution)/shard_map/ppermute | solution.py:93
  108.4 0.7 fusion.14
  109.1 4.2 %collective-permute-start.8 = (bf16[3,64,512]{2,1,0:T(8,128)(2,1)S(1)}, bf16[3,64,512]{2,1,0:T(8,128)(2,1)S(1)}, u32[]{:S(2)}, u32[]{:S(2)}) collective-permute-start(bf16[3,64,512]{2,1,0:T(8,128)(2,1)S(1)} %slice.49), channel_id=1, source_target_pairs={{0,1},{1,0},{2,3},{3,2},{4,5},{5,4},{6,7},{7,6},{8,9},{9,8},{10,11... | collective-permute-start | bytes 589832 | tf_op jit(solution)/shard_map/ppermute | solution.py:98
  113.3 2.3 %fusion = f32[2048,64]{0,1:T(8,128)S(1)} fusion(f32[64,2048]{1,0:T(8,128)S(1)} %fusion.14, bf16[2048,512]{1,0:T(8,128)(2,1)} %collective-permute-done.2, bf16[3,72,512]{2,1,0:T(8,128)(2,1)S(1)} %bitcast.73), kind=kOutput, calls=%fused_computation.3 | convolution fusion | flops 134348800 | bytes 3211264 | tf_op jit(solution)/shard_map/dot_general | solution.py:30
  115.7 2.2 %collective-permute-start.9 = (f32[2048,64]{0,1:T(8,128)S(1)}, f32[2048,64]{0,1:T(8,128)}, u32[]{:S(2)}, u32[]{:S(2)}) collective-permute-start(f32[2048,64]{0,1:T(8,128)S(1)} %fusion), channel_id=1, source_target_pairs={{0,6},{6,12},{12,18},{18,24},{24,30},{30,36},{36,42},{42,48},{48,5... | collective-permute-start | bytes 1572872 | tf_op jit(solution)/shard_map/ppermute | solution.py:11
  117.9 0.0 collective-permute-done.8
  117.9 0.0 copy-start.1
  117.9 2.4 %fusion.13 = f32[64,2048]{1,0:T(8,128)S(1)} fusion(bf16[2048,512]{1,0:T(8,128)(2,1)} %collective-permute-done.2, bf16[3,64,512]{2,1,0:T(8,128)(2,1)S(1)} %collective-permute-done.8), kind=kOutput, calls=%fused_computation.36 | convolution fusion | flops 134217728 | bytes 2686976 | tf_op jit(solution)/shard_map/dot_general | solution.py:30
  120.3 0.8 fusion.1
  121.1 0.0 copy-done.1
  121.1 3.2 %collective-permute-start.10 = (f32[2048,64]{0,1:T(8,128)S(1)}, f32[2048,64]{0,1:T(8,128)}, u32[]{:S(2)}, u32[]{:S(2)}) collective-permute-start(f32[2048,64]{0,1:T(8,128)S(1)} %fusion.1), channel_id=1, source_target_pairs={{0,6},{6,12},{12,18},{18,24},{24,30},{30,36},{36,42},{42,48},{48,5... | collective-permute-start | bytes 1572872 | tf_op jit(solution)/shard_map/ppermute | solution.py:11
  124.3 0.8 slice_bitcast_fusion.8
  125.1 12.0 %collective-permute-done.9 = f32[2048,64]{0,1:T(8,128)} collective-permute-done((f32[2048,64]{0,1:T(8,128)S(1)}, f32[2048,64]{0,1:T(8,128)}, u32[]{:S(2)}, u32[]{:S(2)}) %collective-permute-start.9) | collective-permute-done | bytes 524320 | tf_op jit(solution)/shard_map/ppermute | solution.py:11
  137.1 11.2 %collective-permute-done.10 = f32[2048,64]{0,1:T(8,128)} collective-permute-done((f32[2048,64]{0,1:T(8,128)S(1)}, f32[2048,64]{0,1:T(8,128)}, u32[]{:S(2)}, u32[]{:S(2)}) %collective-permute-start.10) | collective-permute-done | bytes 524320 | tf_op jit(solution)/shard_map/ppermute | solution.py:11
  148.4 2.3 %fusion.2 = f32[2048,128]{0,1:T(8,128)S(1)} fusion(f32[2048,64]{0,1:T(8,128)} %collective-permute-done.10, f32[2048,64]{0,1:T(8,128)} %collective-permute-done.9, pred[]{:T(512)S(6)} %eq.16, bf16[2048,512]{1,0:T(8,128)(2,1)S(1)} %copy-done, bf16[64,512]{1,0:T(8,128)(2,1)S(1)} %slice_bitcast_fusion.8, bf16[64,512]{1,0:T(8,128)(2,1)S(1)} %slice_bitcast_fusion.9), kind=kOutput, calls=%fused_computation.8 | convolution fusion | flops 270073856 | bytes 4325377 | tf_op jit(solution)/shard_map/dot_general | solution.py:30
  150.7 1.3 copy.9
  (16 shorter events, 0.3 us)
Async XLA Ops:
  0.0 22.0 %copy-start = (bf16[2048,512]{1,0:T(8,128)(2,1)S(1)}, bf16[2048,512]{1,0:T(8,128)(2,1)}, u32[]{:S(2)}) copy-start(bf16[2048,512]{1,0:T(8,128)(2,1)} %param.6) | copy-start | bytes 6291460
  0.0 53.4 %collective-permute-start.2 = (bf16[2048,512]{1,0:T(8,128)(2,1)}, bf16[2048,512]{1,0:T(8,128)(2,1)}, u32[]{:S(2)}, u32[]{:S(2)}) collective-permute-start(bf16[2048,512]{1,0:T(8,128)(2,1)} %param.6), channel_id=1, source_target_pairs={{0,6},{6,12},{12,18},{18,24},{24,30},{30,36},{36,42},{42,48},{48,5... | collective-permute-start | bytes 6291464 | tf_op jit(solution)/shard_map/ppermute | solution.py:11
  4.2 17.9 %collective-permute-start = (bf16[2048,128]{1,0:T(8,128)(2,1)}, bf16[2048,128]{1,0:T(8,128)(2,1)S(1)}, u32[]{:S(2)}, u32[]{:S(2)}) collective-permute-start(bf16[2048,128]{1,0:T(8,128)(2,1)} %param.5), channel_id=1, source_target_pairs={{0,762},{6,0},{12,6},{18,12},{24,18},{30,24},{36,30},{42,36},{48,4... | collective-permute-start | bytes 1572872 | tf_op jit(solution)/shard_map/ppermute | solution.py:11
  22.5 42.0 %collective-permute-start.1 = (f32[2,64,512]{2,1,0:T(8,128)S(1)}, f32[2,64,512]{2,1,0:T(8,128)S(1)}, u32[]{:S(2)}, u32[]{:S(2)}) collective-permute-start(f32[2,64,512]{2,1,0:T(8,128)S(1)} %fusion.3), channel_id=1, source_target_pairs={{0,1},{1,0},{2,3},{3,2},{4,5},{5,4},{6,7},{7,6},{8,9},{9,8},{10,11... | collective-permute-start | bytes 786440 | tf_op jit(solution)/shard_map/ppermute | solution.py:55
  55.4 23.7 %copy-start.2 = (f32[64]{0:T(128)S(1)}, f32[64]{0:T(128)}, u32[]{:S(2)}) copy-start(f32[64]{0:T(128)} %param.8) | copy-start | bytes 772
  55.5 10.1 %collective-permute-start.3 = (f32[1,64,512]{2,1,0:T(8,128)S(1)}, f32[1,64,512]{2,1,0:T(8,128)S(1)}, u32[]{:S(2)}, u32[]{:S(2)}) collective-permute-start(f32[1,64,512]{2,1,0:T(8,128)S(1)} %dynamic-slice_bitcast_fusion.2), channel_id=1, source_target_pairs={{0,1},{1,0},{2,3},{3,2},{4,5},{5,4},{6,7},{7,6},{8,9},{9,8},{10,11... | collective-permute-start | bytes 393224 | tf_op jit(solution)/shard_map/ppermute | solution.py:55
  65.6 24.7 %collective-permute-start.4 = (f32[3,24,512]{2,1,0:T(8,128)S(1)}, f32[3,24,512]{2,1,0:T(8,128)S(1)}, u32[]{:S(2)}, u32[]{:S(2)}) collective-permute-start(f32[3,24,512]{2,1,0:T(8,128)S(1)} %get-tuple-element.9), channel_id=1, source_target_pairs={{0,2},{1,3},{2,4},{3,5},{4,0},{5,1},{6,8},{7,9},{8,10},{9,11},{10,... | collective-permute-start | bytes 442376 | tf_op jit(solution)/shard_map/ppermute | solution.py:80
  76.0 16.1 %collective-permute-start.5 = (f32[3,24,512]{2,1,0:T(8,128)S(1)}, f32[3,24,512]{2,1,0:T(8,128)S(1)}, u32[]{:S(2)}, u32[]{:S(2)}) collective-permute-start(f32[3,24,512]{2,1,0:T(8,128)S(1)} %get-tuple-element.10), channel_id=1, source_target_pairs={{0,4},{1,5},{2,0},{3,1},{4,2},{5,3},{6,10},{7,11},{8,6},{9,7},{10,... | collective-permute-start | bytes 442376 | tf_op jit(solution)/shard_map/ppermute | solution.py:80
  92.2 9.3 %collective-permute-start.6 = (bf16[3,24,512]{2,1,0:T(8,128)(2,1)S(1)}, bf16[3,24,512]{2,1,0:T(8,128)(2,1)S(1)}, u32[]{:S(2)}, u32[]{:S(2)}) collective-permute-start(bf16[3,24,512]{2,1,0:T(8,128)(2,1)S(1)} %pad_maximum_fusion), channel_id=1, source_target_pairs={{0,2},{1,3},{2,4},{3,5},{4,0},{5,1},{6,8},{7,9},{8,10},{9,11},{10,... | collective-permute-start | bytes 221192 | tf_op jit(solution)/shard_map/ppermute | solution.py:93
  99.3 9.0 %collective-permute-start.7 = (bf16[3,24,512]{2,1,0:T(8,128)(2,1)S(1)}, bf16[3,24,512]{2,1,0:T(8,128)(2,1)S(1)}, u32[]{:S(2)}, u32[]{:S(2)}) collective-permute-start(bf16[3,24,512]{2,1,0:T(8,128)(2,1)S(1)} %pad_maximum_fusion), channel_id=1, source_target_pairs={{0,4},{1,5},{2,0},{3,1},{4,2},{5,3},{6,10},{7,11},{8,6},{9,7},{10,... | collective-permute-start | bytes 221192 | tf_op jit(solution)/shard_map/ppermute | solution.py:93
  109.1 8.8 %collective-permute-start.8 = (bf16[3,64,512]{2,1,0:T(8,128)(2,1)S(1)}, bf16[3,64,512]{2,1,0:T(8,128)(2,1)S(1)}, u32[]{:S(2)}, u32[]{:S(2)}) collective-permute-start(bf16[3,64,512]{2,1,0:T(8,128)(2,1)S(1)} %slice.49), channel_id=1, source_target_pairs={{0,1},{1,0},{2,3},{3,2},{4,5},{5,4},{6,7},{7,6},{8,9},{9,8},{10,11... | collective-permute-start | bytes 589832 | tf_op jit(solution)/shard_map/ppermute | solution.py:98
  115.7 21.5 %collective-permute-start.9 = (f32[2048,64]{0,1:T(8,128)S(1)}, f32[2048,64]{0,1:T(8,128)}, u32[]{:S(2)}, u32[]{:S(2)}) collective-permute-start(f32[2048,64]{0,1:T(8,128)S(1)} %fusion), channel_id=1, source_target_pairs={{0,6},{6,12},{12,18},{18,24},{24,30},{30,36},{36,42},{42,48},{48,5... | collective-permute-start | bytes 1572872 | tf_op jit(solution)/shard_map/ppermute | solution.py:11
  117.9 3.2 %copy-start.1 = (bf16[3,64,512]{2,1,0:T(8,128)(2,1)}, bf16[3,64,512]{2,1,0:T(8,128)(2,1)S(1)}, u32[]{:S(2)}) copy-start(bf16[3,64,512]{2,1,0:T(8,128)(2,1)S(1)} %collective-permute-done.8) | copy-start | bytes 589828
  121.1 27.3 %collective-permute-start.10 = (f32[2048,64]{0,1:T(8,128)S(1)}, f32[2048,64]{0,1:T(8,128)}, u32[]{:S(2)}, u32[]{:S(2)}) collective-permute-start(f32[2048,64]{0,1:T(8,128)S(1)} %fusion.1), channel_id=1, source_target_pairs={{0,6},{6,12},{12,18},{18,24},{24,30},{30,36},{36,42},{42,48},{48,5... | collective-permute-start | bytes 1572872 | tf_op jit(solution)/shard_map/ppermute | solution.py:11

commit v11 on v5

--- a/solution.py
+++ b/solution.py
@@ -82,12 +82,6 @@
         col_energy = energy(0, eps_vb)
         return (spin_scale * summed / (row_energy[:, None] + col_energy[None, :])).astype(jnp.bfloat16)
 
-    def core_gather(halves):
-        other = lax.ppermute(halves, "aux", aux_pairs(aux_size, 1, 0))
-        first = jnp.concatenate([halves, other], axis=1)
-        second = jnp.concatenate([other, halves], axis=1)
-        return jnp.where(core == 0, first, second)
-
     def chip_exchange(summed):
         others = [lax.ppermute(summed, "aux", aux_pairs(aux_size, 0, d)) for d in range(1, chips)]
         for other in others:
@@ -105,10 +99,18 @@
     early_amps = chip_gather(jnp.stack([amplitude_part(early[0], 0), amplitude_part(early[1], 1)]))
     late = chip_exchange(core_reduce([partial_integrals(rows_next, cols_prev)]))
     amp_halves = jnp.concatenate([early_amps, amplitude_half(late[0], 1, -1)[None]])
-    amps = core_gather(amp_halves)
-    own = contribution(b_cols, amps[0])
-    onward = contribution(b_cols, amps[1]) + contribution(cols_prev, amps[2])
-    return own + shifted(onward, "occ", 1)
+    sent_first = shifted(contribution(b_cols, amp_halves[1]) + contribution(cols_prev, amp_halves[2]), "occ", 1)
+    amp_other = lax.ppermute(amp_halves, "aux", aux_pairs(aux_size, 1, 0))
+    sent_second = shifted(contribution(b_cols, amp_other[1]) + contribution(cols_prev, amp_other[2]), "occ", 1)
+    first = jnp.concatenate([amp_halves[0], amp_other[0]], axis=0)
+    second = jnp.concatenate([amp_other[0], amp_halves[0]], axis=0)
+    own = contribution(b_cols, jnp.where(core == 0, first, second))
+    sent = jnp.where(
+        core == 0,
+        jnp.concatenate([sent_first, sent_second], axis=1),
+        jnp.concatenate([sent_second, sent_first], axis=1),
+    )
+    return own + sent
 
 
 def solution(mesh):

time: 154 us -> 155 us (level)
  waiting for transfers between devices: 72.4 us -> 66.3 us
  matrix products: 8.81 us -> 13.4 us
  starting transfers between devices: 68.9 us -> 70.8 us
    ppermute x3 -> x4, waiting for transfers between devices: 53 us -> 46.9 us  [shifted(): lax.ppermute(value, axis, [(i, (i + by) % size) for i in range(size)])]
    dot_general x3 -> x5, matrix products: 4.05 us -> 8.6 us  [contribution(): lax.dot_general(right_block, amplitude, (((1,), (1,)), ((), ())), preferr...]
    ppermute x3 -> x4, starting transfers between devices: 17.5 us -> 19.4 us  [shifted(): lax.ppermute(value, axis, [(i, (i + by) % size) for i in range(size)])]
    ppermute x2, waiting for transfers between devices: 0.01 us -> 1.85 us  [chip_gather(): got = lax.ppermute(mine, 'aux', aux_pairs(aux_size, 0, d))]
  transfers between devices with their start and end apart: 12 -> 13, of which waited for: 10 -> 11; matrix products, arithmetic and copies ran while one was open for 4% -> 9% of each run, Pallas kernels for 0% -> 0%
where the time goes in v11:
time: 155 us
  starting transfers between devices  70.8 us (46%)
  waiting for transfers between devices  66.3 us (43%)
  matrix products  13.4 us (9%)
  local copies, waits for them, and re-layouts  2.72 us (2%)
    ppermute x4, waiting for transfers between devices, shifted(): lax.ppermute(value, axis, [(i, (i + by) % size) for i in range(size)])  46.9 us
    ppermute x4, starting transfers between devices, shifted(): lax.ppermute(value, axis, [(i, (i + by) % size) for i in range(size)])  19.4 us
    ppermute x2, starting transfers between devices, chip_exchange(): lax.ppermute(summed, 'aux', aux_pairs(aux_size, 0, d))  17 us
    ppermute x2, starting transfers between devices, chip_reduce(): mine = mine + lax.ppermute(give, 'aux', aux_pairs(aux_size, 0, d))  13.5 us
    ppermute x2, starting transfers between devices, chip_gather(): got = lax.ppermute(mine, 'aux', aux_pairs(aux_size, 0, d))  9.19 us
    dot_general x5, matrix products, contribution(): lax.dot_general(right_block, amplitude, (((1,), (1,)), ((), ())), preferr...  8.6 us
    ppermute x2, waiting for transfers between devices, chip_reduce(): mine = mine + lax.ppermute(give, 'aux', aux_pairs(aux_size, 0, d))  8.34 us
    ppermute x2, starting transfers between devices, core_reduce(): return keep + lax.ppermute(give, 'aux', aux_pairs(aux_size, 1, 0))  8.24 us
  transfers between devices with their start and end apart: 13, of which 11 were waited for; matrix products, arithmetic and copies ran while one was open for 9% of the time, Pallas kernels for 0%

profile of v11, /device:TPU:1, one launch (start us, length us, event | category | flops | bytes accessed | tf_op | source)
XLA Modules:
  0.0 154.8 jit_solution(15053626280521960631)
XLA Ops:
  0.0 13.7 %collective-permute-start = (bf16[2048,128]{1,0:T(8,128)(2,1)}, bf16[2048,128]{1,0:T(8,128)(2,1)S(1)}, u32[]{:S(2)}, u32[]{:S(2)}) collective-permute-start(bf16[2048,128]{1,0:T(8,128)(2,1)} %param.5), channel_id=1, source_target_pairs={{0,762},{6,0},{12,6},{18,12},{24,18},{30,24},{36,30},{42,36},{48,4... | collective-permute-start | bytes 1572872 | tf_op jit(solution)/shard_map/ppermute | solution.py:11
  13.7 1.9 %collective-permute-start.6 = (bf16[2048,512]{1,0:T(8,128)(2,1)}, bf16[2048,512]{1,0:T(8,128)(2,1)}, u32[]{:S(2)}, u32[]{:S(2)}) collective-permute-start(bf16[2048,512]{1,0:T(8,128)(2,1)} %param.6), channel_id=1, source_target_pairs={{0,6},{6,12},{12,18},{18,24},{24,30},{30,36},{36,42},{42,48},{48,5... | collective-permute-start | bytes 6291464 | tf_op jit(solution)/shard_map/ppermute | solution.py:11
  15.7 0.9 fusion.24
  16.6 2.2 %convolution_bitcast_fusion.2 = f32[1,128,512]{2,1,0:T(8,128)S(1)} fusion(bf16[2048,128]{1,0:T(8,128)(2,1)} %param.5, bf16[2048,512]{1,0:T(8,128)(2,1)} %param.6), kind=kOutput, calls=%fused_computation.6 | convolution fusion | flops 268435456 | bytes 2883584 | tf_op jit(solution)/shard_map/dot_general | solution.py:24
  18.8 0.0 copy-start.2
  18.8 0.0 copy-start.1
  18.8 5.7 %collective-permute-done = bf16[2048,128]{1,0:T(8,128)(2,1)S(1)} collective-permute-done((bf16[2048,128]{1,0:T(8,128)(2,1)}, bf16[2048,128]{1,0:T(8,128)(2,1)S(1)}, u32[]{:S(2)}, u32[]{:S(2)}) %collective-permute-start) | collective-permute-done | bytes 524320 | tf_op jit(solution)/shard_map/ppermute | solution.py:11
  24.6 0.5 convolution_bitcast_fusion.1
  25.0 0.7 fusion.3
  25.8 3.4 %collective-permute-start.1 = (f32[2,64,512]{2,1,0:T(8,128)}, f32[2,64,512]{2,1,0:T(8,128)S(1)}, u32[]{:S(2)}, u32[]{:S(2)}) collective-permute-start(f32[2,64,512]{2,1,0:T(8,128)} %fusion.3), channel_id=1, source_target_pairs={{0,1},{1,0},{2,3},{3,2},{4,5},{5,4},{6,7},{7,6},{8,9},{9,8},{10,11... | collective-permute-start | bytes 786440 | tf_op jit(solution)/shard_map/ppermute | solution.py:55
  29.2 0.1 broadcast_subtract_fusion.1
  29.4 0.1 sub.103
  29.4 0.1 sub.110
  29.5 0.1 dynamic_slice.53
  29.6 0.1 dynamic_slice.56
  29.7 0.1 subtract_bitcast_fusion.1
  29.7 0.8 collective-permute-done.1
  30.7 10.3 %collective-permute-start.2 = (f32[2,24,512]{2,1,0:T(8,128)S(1)}, f32[2,24,512]{2,1,0:T(8,128)S(1)}, u32[]{:S(2)}, u32[]{:S(2)}) collective-permute-start(f32[2,24,512]{2,1,0:T(8,128)S(1)} %get-tuple-element.5), channel_id=1, source_target_pairs={{0,2},{1,3},{2,4},{3,5},{4,0},{5,1},{6,8},{7,9},{8,10},{9,11},{10,... | collective-permute-start | bytes 294920 | tf_op jit(solution)/shard_map/ppermute | solution.py:67
  41.0 3.2 %collective-permute-start.3 = (f32[2,24,512]{2,1,0:T(8,128)S(1)}, f32[2,24,512]{2,1,0:T(8,128)S(1)}, u32[]{:S(2)}, u32[]{:S(2)}) collective-permute-start(f32[2,24,512]{2,1,0:T(8,128)S(1)} %get-tuple-element.6), channel_id=1, source_target_pairs={{0,4},{1,5},{2,0},{3,1},{4,2},{5,3},{6,10},{7,11},{8,6},{9,7},{10,... | collective-permute-start | bytes 294920 | tf_op jit(solution)/shard_map/ppermute | solution.py:67
  44.2 0.1 pad_dynamic-slice_fusion.4
  44.3 6.4 %collective-permute-done.2 = f32[2,24,512]{2,1,0:T(8,128)S(1)} collective-permute-done((f32[2,24,512]{2,1,0:T(8,128)S(1)}, f32[2,24,512]{2,1,0:T(8,128)S(1)}, u32[]{:S(2)}, u32[]{:S(2)}) %collective-permute-start.2) | collective-permute-done | bytes 98336 | tf_op jit(solution)/shard_map/ppermute | solution.py:67
  50.7 1.9 %collective-permute-done.3 = f32[2,24,512]{2,1,0:T(8,128)S(1)} collective-permute-done((f32[2,24,512]{2,1,0:T(8,128)S(1)}, f32[2,24,512]{2,1,0:T(8,128)S(1)}, u32[]{:S(2)}, u32[]{:S(2)}) %collective-permute-start.3) | collective-permute-done | bytes 98336 | tf_op jit(solution)/shard_map/ppermute | solution.py:67
  52.6 0.1 fusion.22
  52.7 6.8 %collective-permute-start.4 = (bf16[2,24,512]{2,1,0:T(8,128)(2,1)S(1)}, bf16[2,24,512]{2,1,0:T(8,128)(2,1)S(1)}, u32[]{:S(2)}, u32[]{:S(2)}) collective-permute-start(bf16[2,24,512]{2,1,0:T(8,128)(2,1)S(1)} %pad_maximum_fusion.1), channel_id=1, source_target_pairs={{0,2},{1,3},{2,4},{3,5},{4,0},{5,1},{6,8},{7,9},{8,10},{9,11},{10,... | collective-permute-start | bytes 147464 | tf_op jit(solution)/shard_map/ppermute | solution.py:74
  59.6 2.4 %collective-permute-start.5 = (bf16[2,24,512]{2,1,0:T(8,128)(2,1)S(1)}, bf16[2,24,512]{2,1,0:T(8,128)(2,1)S(1)}, u32[]{:S(2)}, u32[]{:S(2)}) collective-permute-start(bf16[2,24,512]{2,1,0:T(8,128)(2,1)S(1)} %pad_maximum_fusion.1), channel_id=1, source_target_pairs={{0,4},{1,5},{2,0},{3,1},{4,2},{5,3},{6,10},{7,11},{8,6},{9,7},{10,... | collective-permute-start | bytes 147464 | tf_op jit(solution)/shard_map/ppermute | solution.py:74
  62.0 1.8 %collective-permute-done.4 = bf16[2,24,512]{2,1,0:T(8,128)(2,1)S(1)} collective-permute-done((bf16[2,24,512]{2,1,0:T(8,128)(2,1)S(1)}, bf16[2,24,512]{2,1,0:T(8,128)(2,1)S(1)}, u32[]{:S(2)}, u32[]{:S(2)}) %collective-permute-start.4) | collective-permute-done | bytes 49184 | tf_op jit(solution)/shard_map/ppermute | solution.py:74
  63.8 7.0 %collective-permute-done.6 = bf16[2048,512]{1,0:T(8,128)(2,1)} collective-permute-done((bf16[2048,512]{1,0:T(8,128)(2,1)}, bf16[2048,512]{1,0:T(8,128)(2,1)}, u32[]{:S(2)}, u32[]{:S(2)}) %collective-permute-start.6) | collective-permute-done | bytes 2097184 | tf_op jit(solution)/shard_map/ppermute | solution.py:11
  70.9 2.1 %fusion.25 = f32[128,512]{1,0:T(8,128)S(1)} fusion(bf16[2048,128]{1,0:T(8,128)(2,1)S(1)} %collective-permute-done, bf16[2048,512]{1,0:T(8,128)(2,1)} %collective-permute-done.6), kind=kOutput, calls=%fused_computation.61 | convolution fusion | flops 268435456 | bytes 2883584 | tf_op jit(solution)/shard_map/dot_general | solution.py:24
  73.0 4.8 %collective-permute-start.7 = (f32[1,64,512]{2,1,0:T(8,128)S(1)}, f32[1,64,512]{2,1,0:T(8,128)S(1)}, u32[]{:S(2)}, u32[]{:S(2)}) collective-permute-start(f32[1,64,512]{2,1,0:T(8,128)S(1)} %dynamic-slice_bitcast_fusion), channel_id=1, source_target_pairs={{0,1},{1,0},{2,3},{3,2},{4,5},{5,4},{6,7},{7,6},{8,9},{9,8},{10,11... | collective-permute-start | bytes 393224 | tf_op jit(solution)/shard_map/ppermute | solution.py:55
  77.8 0.0 collective-permute-done.5
  77.8 0.9 collective-permute-done.7
  78.8 15.1 %collective-permute-start.9 = (f32[1,64,512]{2,1,0:T(8,128)S(1)}, f32[1,64,512]{2,1,0:T(8,128)S(1)}, u32[]{:S(2)}, u32[]{:S(2)}) collective-permute-start(f32[1,64,512]{2,1,0:T(8,128)S(1)} %bitcast_add_fusion), channel_id=1, source_target_pairs={{0,4},{1,5},{2,0},{3,1},{4,2},{5,3},{6,10},{7,11},{8,6},{9,7},{10,... | collective-permute-start | bytes 393224 | tf_op jit(solution)/shard_map/ppermute | solution.py:86
  93.9 1.9 %collective-permute-start.8 = (f32[1,64,512]{2,1,0:T(8,128)S(1)}, f32[1,64,512]{2,1,0:T(8,128)S(1)}, u32[]{:S(2)}, u32[]{:S(2)}) collective-permute-start(f32[1,64,512]{2,1,0:T(8,128)S(1)} %bitcast_add_fusion), channel_id=1, source_target_pairs={{0,2},{1,3},{2,4},{3,5},{4,0},{5,1},{6,8},{7,9},{8,10},{9,11},{10,... | collective-permute-start | bytes 393224 | tf_op jit(solution)/shard_map/ppermute | solution.py:86
  95.8 0.7 fusion.16
  96.6 2.6 %collective-permute-done.9 = f32[1,64,512]{2,1,0:T(8,128)S(1)} collective-permute-done((f32[1,64,512]{2,1,0:T(8,128)S(1)}, f32[1,64,512]{2,1,0:T(8,128)S(1)}, u32[]{:S(2)}, u32[]{:S(2)}) %collective-permute-start.9) | collective-permute-done | bytes 131104 | tf_op jit(solution)/shard_map/ppermute | solution.py:86
  99.2 4.9 %collective-permute-done.8 = f32[1,64,512]{2,1,0:T(8,128)S(1)} collective-permute-done((f32[1,64,512]{2,1,0:T(8,128)S(1)}, f32[1,64,512]{2,1,0:T(8,128)S(1)}, u32[]{:S(2)}, u32[]{:S(2)}) %collective-permute-start.8) | collective-permute-done | bytes 131104 | tf_op jit(solution)/shard_map/ppermute | solution.py:86
  104.1 0.1 divide_convert_fusion
  104.2 3.4 %collective-permute-start.10 = (bf16[3,64,512]{2,1,0:T(8,128)(2,1)S(1)}, bf16[3,64,512]{2,1,0:T(8,128)(2,1)S(1)}, u32[]{:S(2)}, u32[]{:S(2)}) collective-permute-start(bf16[3,64,512]{2,1,0:T(8,128)(2,1)S(1)} %pad_maximum_fusion), channel_id=1, source_target_pairs={{0,1},{1,0},{2,3},{3,2},{4,5},{5,4},{6,7},{7,6},{8,9},{9,8},{10,11... | collective-permute-start | bytes 589832 | tf_op jit(solution)/shard_map/ppermute | solution.py:103
  107.7 2.4 %fusion = f32[2048,64]{0,1:T(8,128)S(1)} fusion(f32[64,2048]{1,0:T(8,128)S(1)} %fusion.16, bf16[2048,512]{1,0:T(8,128)(2,1)} %collective-permute-done.6, f32[512]{0:T(512)S(1)} %bitcast.77, f32[64]{0:T(128)S(1)} %dynamic_slice.56, f32[1,64,512]{2,1,0:T(8,128)S(1)} %collective-permute-done.9, f32[1,64,512]{2,1,0:T(8,128)S(1)} %bitcast_add_fusion, ...), kind=kOutput, calls=%fused_computation.3 | convolution fusion | flops 134545408 | bytes 3541248 | tf_op jit(solution)/shard_map/dot_general | solution.py:30
  110.0 1.9 %collective-permute-start.11 = (f32[2048,64]{0,1:T(8,128)S(1)}, f32[2048,64]{0,1:T(8,128)}, u32[]{:S(2)}, u32[]{:S(2)}) collective-permute-start(f32[2048,64]{0,1:T(8,128)S(1)} %fusion), channel_id=1, source_target_pairs={{0,6},{6,12},{12,18},{18,24},{24,30},{30,36},{36,42},{42,48},{48,5... | collective-permute-start | bytes 1572872 | tf_op jit(solution)/shard_map/ppermute | solution.py:11
  112.0 0.0 collective-permute-done.10
  112.0 2.3 %fusion.15 = f32[64,2048]{1,0:T(8,128)S(1)} fusion(bf16[2048,512]{1,0:T(8,128)(2,1)} %collective-permute-done.6, bf16[3,64,512]{2,1,0:T(8,128)(2,1)S(1)} %collective-permute-done.10), kind=kOutput, calls=%fused_computation.35 | convolution fusion | flops 134217728 | bytes 2686976 | tf_op jit(solution)/shard_map/dot_general | solution.py:30
  114.3 0.8 fusion.1
  115.1 1.9 %collective-permute-start.12 = (f32[2048,64]{0,1:T(8,128)S(1)}, f32[2048,64]{0,1:T(8,128)}, u32[]{:S(2)}, u32[]{:S(2)}) collective-permute-start(f32[2048,64]{0,1:T(8,128)S(1)} %fusion.1), channel_id=1, source_target_pairs={{0,6},{6,12},{12,18},{18,24},{24,30},{30,36},{36,42},{42,48},{48,5... | collective-permute-start | bytes 1572872 | tf_op jit(solution)/shard_map/ppermute | solution.py:11
  117.0 22.9 %collective-permute-done.11 = f32[2048,64]{0,1:T(8,128)} collective-permute-done((f32[2048,64]{0,1:T(8,128)S(1)}, f32[2048,64]{0,1:T(8,128)}, u32[]{:S(2)}, u32[]{:S(2)}) %collective-permute-start.11) | collective-permute-done | bytes 524320 | tf_op jit(solution)/shard_map/ppermute | solution.py:11
  139.9 11.2 %collective-permute-done.12 = f32[2048,64]{0,1:T(8,128)} collective-permute-done((f32[2048,64]{0,1:T(8,128)S(1)}, f32[2048,64]{0,1:T(8,128)}, u32[]{:S(2)}, u32[]{:S(2)}) %collective-permute-start.12) | collective-permute-done | bytes 524320 | tf_op jit(solution)/shard_map/ppermute | solution.py:11
  151.1 2.4 %fusion.2 = f32[2048,128]{0,1:T(8,128)S(1)} fusion(f32[2048,64]{0,1:T(8,128)} %collective-permute-done.12, f32[2048,64]{0,1:T(8,128)} %collective-permute-done.11, pred[]{:T(512)S(6)} %eq.16, bf16[2048,512]{1,0:T(8,128)(2,1)S(1)} %copy-done, bf16[64,512]{1,0:T(8,128)(2,1)S(1)} %slice_bitcast_fusion.6, bf16[64,512]{1,0:T(8,128)(2,1)S(1)} %slice_bitcast_fusion.7), kind=kOutput, calls=%fused_computation.8 | convolution fusion | flops 270073856 | bytes 4325377 | tf_op jit(solution)/shard_map/dot_general | solution.py:30
  153.5 1.3 copy.9
  (21 shorter events, 0.3 us)
Async XLA Ops:
  0.0 24.6 %copy-start = (bf16[2048,512]{1,0:T(8,128)(2,1)S(1)}, bf16[2048,512]{1,0:T(8,128)(2,1)}, u32[]{:S(2)}) copy-start(bf16[2048,512]{1,0:T(8,128)(2,1)} %param.6) | copy-start | bytes 6291460
  0.0 24.6 %collective-permute-start = (bf16[2048,128]{1,0:T(8,128)(2,1)}, bf16[2048,128]{1,0:T(8,128)(2,1)S(1)}, u32[]{:S(2)}, u32[]{:S(2)}) collective-permute-start(bf16[2048,128]{1,0:T(8,128)(2,1)} %param.5), channel_id=1, source_target_pairs={{0,762},{6,0},{12,6},{18,12},{24,18},{30,24},{36,30},{42,36},{48,4... | collective-permute-start | bytes 1572872 | tf_op jit(solution)/shard_map/ppermute | solution.py:11
  13.7 57.2 %collective-permute-start.6 = (bf16[2048,512]{1,0:T(8,128)(2,1)}, bf16[2048,512]{1,0:T(8,128)(2,1)}, u32[]{:S(2)}, u32[]{:S(2)}) collective-permute-start(bf16[2048,512]{1,0:T(8,128)(2,1)} %param.6), channel_id=1, source_target_pairs={{0,6},{6,12},{12,18},{18,24},{24,30},{30,36},{36,42},{42,48},{48,5... | collective-permute-start | bytes 6291464 | tf_op jit(solution)/shard_map/ppermute | solution.py:11
  18.8 10.4 %copy-start.2 = (f32[64]{0:T(128)S(1)}, f32[64]{0:T(128)}, u32[]{:S(2)}) copy-start(f32[64]{0:T(128)} %param.8) | copy-start | bytes 772
  18.8 10.8 %copy-start.1 = (f32[256]{0:T(256)S(1)}, f32[256]{0:T(256)}, u32[]{:S(2)}) copy-start(f32[256]{0:T(256)} %param.9) | copy-start | bytes 3076
  25.8 4.8 %collective-permute-start.1 = (f32[2,64,512]{2,1,0:T(8,128)}, f32[2,64,512]{2,1,0:T(8,128)S(1)}, u32[]{:S(2)}, u32[]{:S(2)}) collective-permute-start(f32[2,64,512]{2,1,0:T(8,128)} %fusion.3), channel_id=1, source_target_pairs={{0,1},{1,0},{2,3},{3,2},{4,5},{5,4},{6,7},{7,6},{8,9},{9,8},{10,11... | collective-permute-start | bytes 786440 | tf_op jit(solution)/shard_map/ppermute | solution.py:55
  30.7 20.0 %collective-permute-start.2 = (f32[2,24,512]{2,1,0:T(8,128)S(1)}, f32[2,24,512]{2,1,0:T(8,128)S(1)}, u32[]{:S(2)}, u32[]{:S(2)}) collective-permute-start(f32[2,24,512]{2,1,0:T(8,128)S(1)} %get-tuple-element.5), channel_id=1, source_target_pairs={{0,2},{1,3},{2,4},{3,5},{4,0},{5,1},{6,8},{7,9},{8,10},{9,11},{10,... | collective-permute-start | bytes 294920 | tf_op jit(solution)/shard_map/ppermute | solution.py:67
  41.0 11.6 %collective-permute-start.3 = (f32[2,24,512]{2,1,0:T(8,128)S(1)}, f32[2,24,512]{2,1,0:T(8,128)S(1)}, u32[]{:S(2)}, u32[]{:S(2)}) collective-permute-start(f32[2,24,512]{2,1,0:T(8,128)S(1)} %get-tuple-element.6), channel_id=1, source_target_pairs={{0,4},{1,5},{2,0},{3,1},{4,2},{5,3},{6,10},{7,11},{8,6},{9,7},{10,... | collective-permute-start | bytes 294920 | tf_op jit(solution)/shard_map/ppermute | solution.py:67
  52.7 11.1 %collective-permute-start.4 = (bf16[2,24,512]{2,1,0:T(8,128)(2,1)S(1)}, bf16[2,24,512]{2,1,0:T(8,128)(2,1)S(1)}, u32[]{:S(2)}, u32[]{:S(2)}) collective-permute-start(bf16[2,24,512]{2,1,0:T(8,128)(2,1)S(1)} %pad_maximum_fusion.1), channel_id=1, source_target_pairs={{0,2},{1,3},{2,4},{3,5},{4,0},{5,1},{6,8},{7,9},{8,10},{9,11},{10,... | collective-permute-start | bytes 147464 | tf_op jit(solution)/shard_map/ppermute | solution.py:74
  59.6 18.2 %collective-permute-start.5 = (bf16[2,24,512]{2,1,0:T(8,128)(2,1)S(1)}, bf16[2,24,512]{2,1,0:T(8,128)(2,1)S(1)}, u32[]{:S(2)}, u32[]{:S(2)}) collective-permute-start(bf16[2,24,512]{2,1,0:T(8,128)(2,1)S(1)} %pad_maximum_fusion.1), channel_id=1, source_target_pairs={{0,4},{1,5},{2,0},{3,1},{4,2},{5,3},{6,10},{7,11},{8,6},{9,7},{10,... | collective-permute-start | bytes 147464 | tf_op jit(solution)/shard_map/ppermute | solution.py:74
  73.0 5.8 %collective-permute-start.7 = (f32[1,64,512]{2,1,0:T(8,128)S(1)}, f32[1,64,512]{2,1,0:T(8,128)S(1)}, u32[]{:S(2)}, u32[]{:S(2)}) collective-permute-start(f32[1,64,512]{2,1,0:T(8,128)S(1)} %dynamic-slice_bitcast_fusion), channel_id=1, source_target_pairs={{0,1},{1,0},{2,3},{3,2},{4,5},{5,4},{6,7},{7,6},{8,9},{9,8},{10,11... | collective-permute-start | bytes 393224 | tf_op jit(solution)/shard_map/ppermute | solution.py:55
  78.8 20.4 %collective-permute-start.9 = (f32[1,64,512]{2,1,0:T(8,128)S(1)}, f32[1,64,512]{2,1,0:T(8,128)S(1)}, u32[]{:S(2)}, u32[]{:S(2)}) collective-permute-start(f32[1,64,512]{2,1,0:T(8,128)S(1)} %bitcast_add_fusion), channel_id=1, source_target_pairs={{0,4},{1,5},{2,0},{3,1},{4,2},{5,3},{6,10},{7,11},{8,6},{9,7},{10,... | collective-permute-start | bytes 393224 | tf_op jit(solution)/shard_map/ppermute | solution.py:86
  93.9 10.2 %collective-permute-start.8 = (f32[1,64,512]{2,1,0:T(8,128)S(1)}, f32[1,64,512]{2,1,0:T(8,128)S(1)}, u32[]{:S(2)}, u32[]{:S(2)}) collective-permute-start(f32[1,64,512]{2,1,0:T(8,128)S(1)} %bitcast_add_fusion), channel_id=1, source_target_pairs={{0,2},{1,3},{2,4},{3,5},{4,0},{5,1},{6,8},{7,9},{8,10},{9,11},{10,... | collective-permute-start | bytes 393224 | tf_op jit(solution)/shard_map/ppermute | solution.py:86
  104.2 7.7 %collective-permute-start.10 = (bf16[3,64,512]{2,1,0:T(8,128)(2,1)S(1)}, bf16[3,64,512]{2,1,0:T(8,128)(2,1)S(1)}, u32[]{:S(2)}, u32[]{:S(2)}) collective-permute-start(bf16[3,64,512]{2,1,0:T(8,128)(2,1)S(1)} %pad_maximum_fusion), channel_id=1, source_target_pairs={{0,1},{1,0},{2,3},{3,2},{4,5},{5,4},{6,7},{7,6},{8,9},{9,8},{10,11... | collective-permute-start | bytes 589832 | tf_op jit(solution)/shard_map/ppermute | solution.py:103
  110.0 29.9 %collective-permute-start.11 = (f32[2048,64]{0,1:T(8,128)S(1)}, f32[2048,64]{0,1:T(8,128)}, u32[]{:S(2)}, u32[]{:S(2)}) collective-permute-start(f32[2048,64]{0,1:T(8,128)S(1)} %fusion), channel_id=1, source_target_pairs={{0,6},{6,12},{12,18},{18,24},{24,30},{30,36},{36,42},{42,48},{48,5... | collective-permute-start | bytes 1572872 | tf_op jit(solution)/shard_map/ppermute | solution.py:11
  115.1 36.1 %collective-permute-start.12 = (f32[2048,64]{0,1:T(8,128)S(1)}, f32[2048,64]{0,1:T(8,128)}, u32[]{:S(2)}, u32[]{:S(2)}) collective-permute-start(f32[2048,64]{0,1:T(8,128)S(1)} %fusion.1), channel_id=1, source_target_pairs={{0,6},{6,12},{12,18},{18,24},{24,30},{30,36},{36,42},{42,48},{48,5... | collective-permute-start | bytes 1572872 | tf_op jit(solution)/shard_map/ppermute | solution.py:11

commit v12 on v7

--- a/solution.py
+++ b/solution.py
@@ -80,12 +80,12 @@
     first = jnp.concatenate([amp_halves[0], amp_other[0]], axis=0)
     second = jnp.concatenate([amp_other[0], amp_halves[0]], axis=0)
     own = contribution(b_cols, jnp.where(core == 0, first, second))
-    sent = jnp.where(
-        core == 0,
-        jnp.concatenate([sent_first, sent_second], axis=1),
-        jnp.concatenate([sent_second, sent_first], axis=1),
-    )
-    return own + sent
+    mine_at = core * half
+    other_at = (1 - core) * half
+    out = lax.dynamic_update_slice_in_dim(
+        own, lax.dynamic_slice_in_dim(own, mine_at, half, 1) + sent_first, mine_at, 1)
+    return lax.dynamic_update_slice_in_dim(
+        out, lax.dynamic_slice_in_dim(own, other_at, half, 1) + sent_second, other_at, 1)
 
 
 def solution(mesh):

time: 146 us -> 153 us (1.048)
  waiting for transfers between devices: 60.1 us -> 80.2 us
  starting transfers between devices: 66.6 us -> 54.9 us
  matrix products: 14.2 us -> 11.8 us
  other arithmetic: 1.27 us -> 3.13 us
  local copies, waits for them, and re-layouts: 3.38 us -> 1.84 us
    ppermute x4, waiting for transfers between devices: 10.3 us -> 38.9 us  [chip_reduce(): lax.ppermute(summed, 'aux', aux_pairs(aux_size, 0, d))]
    ppermute x2, starting transfers between devices: 21.3 us -> 11.9 us  [core_reduce(): return keep + lax.ppermute(give, 'aux', aux_pairs(aux_size, 1, 0))]
    ppermute x4, waiting for transfers between devices: 48.1 us -> 39.9 us  [shifted(): lax.ppermute(value, axis, [(i, (i + by) % size) for i in range(size)])]
    dot_general x5, matrix products: 9.43 us -> 7.04 us  [contribution(): lax.dot_general(right_block, amplitude, (((1,), (1,)), ((), ())), preferr...]
    ppermute x4, starting transfers between devices: 23.5 us -> 21.2 us  [chip_reduce(): lax.ppermute(summed, 'aux', aux_pairs(aux_size, 0, d))]
  transfers between devices with their start and end apart: 11 -> 11, of which waited for: 8 -> 9; matrix products, arithmetic and copies ran while one was open for 10% -> 9% of each run, Pallas kernels for 0% -> 0%
where the time goes in v12:
time: 153 us; the launch traced here: 152 us
  waiting for transfers between devices  80.2 us (52%)
  starting transfers between devices  54.9 us (36%)
  matrix products  11.8 us (8%)
  other arithmetic  3.13 us (2%)
  local copies, waits for them, and re-layouts  1.84 us (1%)
    ppermute x4, waiting for transfers between devices, shifted(): lax.ppermute(value, axis, [(i, (i + by) % size) for i in range(size)])  39.9 us
    ppermute x4, waiting for transfers between devices, chip_reduce(): lax.ppermute(summed, 'aux', aux_pairs(aux_size, 0, d))  38.9 us
    ppermute x4, starting transfers between devices, chip_reduce(): lax.ppermute(summed, 'aux', aux_pairs(aux_size, 0, d))  21.2 us
    ppermute x4, starting transfers between devices, shifted(): lax.ppermute(value, axis, [(i, (i + by) % size) for i in range(size)])  19.4 us
    ppermute x2, starting transfers between devices, core_reduce(): return keep + lax.ppermute(give, 'aux', aux_pairs(aux_size, 1, 0))  11.9 us
    dot_general x5, matrix products, contribution(): lax.dot_general(right_block, amplitude, (((1,), (1,)), ((), ())), preferr...  7.04 us
    dot_general x3, matrix products, partial_integrals(): lax.dot_general(left_block, right_block, (((0,), (0,)), ((), ())), prefer...  4.76 us
  transfers between devices with their start and end apart: 11, of which 9 were waited for; matrix products, arithmetic and copies ran while one was open for 9% of the time, Pallas kernels for 0%

profile of v12, /device:TPU:1, one launch (start us, length us, event | category | flops | bytes accessed | tf_op | source)
XLA Modules:
  0.0 152.2 jit_solution(11558711483295571460)
XLA Ops:
  0.0 4.1 %collective-permute-start.4 = (bf16[2048,512]{1,0:T(8,128)(2,1)}, bf16[2048,512]{1,0:T(8,128)(2,1)}, u32[]{:S(2)}, u32[]{:S(2)}) collective-permute-start(bf16[2048,512]{1,0:T(8,128)(2,1)} %param.6), channel_id=1, source_target_pairs={{0,6},{6,12},{12,18},{18,24},{24,30},{30,36},{36,42},{42,48},{48,5... | collective-permute-start | bytes 6291464 | tf_op jit(solution)/shard_map/ppermute | solution.py:11
  4.2 11.4 %collective-permute-start = (bf16[2048,128]{1,0:T(8,128)(2,1)}, bf16[2048,128]{1,0:T(8,128)(2,1)S(1)}, u32[]{:S(2)}, u32[]{:S(2)}) collective-permute-start(bf16[2048,128]{1,0:T(8,128)(2,1)} %param.5), channel_id=1, source_target_pairs={{0,762},{6,0},{12,6},{18,12},{24,18},{30,24},{36,30},{42,36},{48,4... | collective-permute-start | bytes 1572872 | tf_op jit(solution)/shard_map/ppermute | solution.py:11
  15.6 2.2 %convolution_bitcast_fusion.1 = f32[1,128,512]{2,1,0:T(8,128)S(1)} fusion(bf16[2048,128]{1,0:T(8,128)(2,1)} %param.5, bf16[2048,512]{1,0:T(8,128)(2,1)} %param.6), kind=kOutput, calls=%fused_computation.5 | convolution fusion | flops 268435456 | bytes 2883584 | tf_op jit(solution)/shard_map/dot_general | solution.py:24
  17.9 0.0 copy-start.1
  17.9 0.0 copy-start.3
  17.9 0.0 copy-start.2
  17.9 4.1 %collective-permute-done = bf16[2048,128]{1,0:T(8,128)(2,1)S(1)} collective-permute-done((bf16[2048,128]{1,0:T(8,128)(2,1)}, bf16[2048,128]{1,0:T(8,128)(2,1)S(1)}, u32[]{:S(2)}, u32[]{:S(2)}) %collective-permute-start) | collective-permute-done | bytes 524320 | tf_op jit(solution)/shard_map/ppermute | solution.py:11
  22.0 0.5 convolution_bitcast_fusion
  22.5 0.7 fusion.4
  23.2 9.4 %collective-permute-start.1 = (f32[2,64,512]{2,1,0:T(8,128)}, f32[2,64,512]{2,1,0:T(8,128)S(1)}, u32[]{:S(2)}, u32[]{:S(2)}) collective-permute-start(f32[2,64,512]{2,1,0:T(8,128)} %fusion.4), channel_id=1, source_target_pairs={{0,1},{1,0},{2,3},{3,2},{4,5},{5,4},{6,7},{7,6},{8,9},{9,8},{10,11... | collective-permute-start | bytes 786440 | tf_op jit(solution)/shard_map/ppermute | solution.py:55
  32.6 0.1 fusion.28
  32.7 1.2 collective-permute-done.1
  33.9 0.7 fusion.6
  34.7 10.1 %collective-permute-start.3 = (f32[2,64,512]{2,1,0:T(8,128)}, f32[2,64,512]{2,1,0:T(8,128)}, u32[]{:S(2)}, u32[]{:S(2)}) collective-permute-start(f32[2,64,512]{2,1,0:T(8,128)} %fusion.6), channel_id=1, source_target_pairs={{0,4},{1,5},{2,0},{3,1},{4,2},{5,3},{6,10},{7,11},{8,6},{9,7},{10,... | collective-permute-start | bytes 786440 | tf_op jit(solution)/shard_map/ppermute | solution.py:58
  44.8 1.9 %collective-permute-start.2 = (f32[2,64,512]{2,1,0:T(8,128)}, f32[2,64,512]{2,1,0:T(8,128)}, u32[]{:S(2)}, u32[]{:S(2)}) collective-permute-start(f32[2,64,512]{2,1,0:T(8,128)} %fusion.6), channel_id=1, source_target_pairs={{0,2},{1,3},{2,4},{3,5},{4,0},{5,1},{6,8},{7,9},{8,10},{9,11},{10,... | collective-permute-start | bytes 786440 | tf_op jit(solution)/shard_map/ppermute | solution.py:58
  46.7 0.1 broadcast_subtract_fusion.1
  46.8 0.1 sub.93
  46.9 0.1 dynamic_slice.40
  47.0 0.1 sub.100
  47.1 0.1 dynamic_slice.42
  47.1 0.1 subtract_bitcast_fusion.1
  47.2 15.4 %collective-permute-done.3 = f32[2,64,512]{2,1,0:T(8,128)} collective-permute-done((f32[2,64,512]{2,1,0:T(8,128)}, f32[2,64,512]{2,1,0:T(8,128)}, u32[]{:S(2)}, u32[]{:S(2)}) %collective-permute-start.3) | collective-permute-done | bytes 262176 | tf_op jit(solution)/shard_map/ppermute | solution.py:58
  62.6 8.7 %collective-permute-done.2 = f32[2,64,512]{2,1,0:T(8,128)} collective-permute-done((f32[2,64,512]{2,1,0:T(8,128)}, f32[2,64,512]{2,1,0:T(8,128)}, u32[]{:S(2)}, u32[]{:S(2)}) %collective-permute-start.2) | collective-permute-done | bytes 262176 | tf_op jit(solution)/shard_map/ppermute | solution.py:58
  71.2 1.1 add_add_fusion
  72.3 0.0 collective-permute-done.4
  72.4 2.1 %fusion.29 = f32[128,512]{1,0:T(8,128)S(1)} fusion(bf16[2048,128]{1,0:T(8,128)(2,1)S(1)} %collective-permute-done, bf16[2048,512]{1,0:T(8,128)(2,1)} %collective-permute-done.4), kind=kOutput, calls=%fused_computation.58 | convolution fusion | flops 268435456 | bytes 2883584 | tf_op jit(solution)/shard_map/dot_general | solution.py:24
  74.5 2.5 %collective-permute-start.5 = (f32[1,64,512]{2,1,0:T(8,128)S(1)}, f32[1,64,512]{2,1,0:T(8,128)S(1)}, u32[]{:S(2)}, u32[]{:S(2)}) collective-permute-start(f32[1,64,512]{2,1,0:T(8,128)S(1)} %dynamic-slice_bitcast_fusion), channel_id=1, source_target_pairs={{0,1},{1,0},{2,3},{3,2},{4,5},{5,4},{6,7},{7,6},{8,9},{9,8},{10,11... | collective-permute-start | bytes 393224 | tf_op jit(solution)/shard_map/ppermute | solution.py:55
  77.0 0.8 fusion.17
  77.8 0.2 collective-permute-done.5
  78.0 5.9 %collective-permute-start.7 = (f32[1,64,512]{2,1,0:T(8,128)S(1)}, f32[1,64,512]{2,1,0:T(8,128)S(1)}, u32[]{:S(2)}, u32[]{:S(2)}) collective-permute-start(f32[1,64,512]{2,1,0:T(8,128)S(1)} %bitcast_add_fusion.2), channel_id=1, source_target_pairs={{0,4},{1,5},{2,0},{3,1},{4,2},{5,3},{6,10},{7,11},{8,6},{9,7},{10,... | collective-permute-start | bytes 393224 | tf_op jit(solution)/shard_map/ppermute | solution.py:58
  83.9 3.3 %collective-permute-start.6 = (f32[1,64,512]{2,1,0:T(8,128)S(1)}, f32[1,64,512]{2,1,0:T(8,128)S(1)}, u32[]{:S(2)}, u32[]{:S(2)}) collective-permute-start(f32[1,64,512]{2,1,0:T(8,128)S(1)} %bitcast_add_fusion.2), channel_id=1, source_target_pairs={{0,2},{1,3},{2,4},{3,5},{4,0},{5,1},{6,8},{7,9},{8,10},{9,11},{10,... | collective-permute-start | bytes 393224 | tf_op jit(solution)/shard_map/ppermute | solution.py:58
  87.2 0.1 fusion.15
  87.3 5.2 %collective-permute-done.7 = f32[1,64,512]{2,1,0:T(8,128)S(1)} collective-permute-done((f32[1,64,512]{2,1,0:T(8,128)S(1)}, f32[1,64,512]{2,1,0:T(8,128)S(1)}, u32[]{:S(2)}, u32[]{:S(2)}) %collective-permute-start.7) | collective-permute-done | bytes 131104 | tf_op jit(solution)/shard_map/ppermute | solution.py:58
  92.5 9.7 %collective-permute-done.6 = f32[1,64,512]{2,1,0:T(8,128)S(1)} collective-permute-done((f32[1,64,512]{2,1,0:T(8,128)S(1)}, f32[1,64,512]{2,1,0:T(8,128)S(1)}, u32[]{:S(2)}, u32[]{:S(2)}) %collective-permute-start.6) | collective-permute-done | bytes 131104 | tf_op jit(solution)/shard_map/ppermute | solution.py:58
  102.1 0.1 divide_convert_fusion.2
  102.3 2.4 %collective-permute-start.8 = (bf16[3,64,512]{2,1,0:T(8,128)(2,1)S(1)}, bf16[3,64,512]{2,1,0:T(8,128)(2,1)S(1)}, u32[]{:S(2)}, u32[]{:S(2)}) collective-permute-start(bf16[3,64,512]{2,1,0:T(8,128)(2,1)S(1)} %pad_maximum_fusion), channel_id=1, source_target_pairs={{0,1},{1,0},{2,3},{3,2},{4,5},{5,4},{6,7},{7,6},{8,9},{9,8},{10,11... | collective-permute-start | bytes 589832 | tf_op jit(solution)/shard_map/ppermute | solution.py:77
  104.7 2.4 %fusion = f32[2048,64]{0,1:T(8,128)S(1)} fusion(f32[64,2048]{1,0:T(8,128)S(1)} %fusion.17, bf16[2048,512]{1,0:T(8,128)(2,1)} %collective-permute-done.4, f32[512]{0:T(512)S(1)} %bitcast.65, f32[64]{0:T(128)S(1)} %dynamic_slice.42, f32[1,64,512]{2,1,0:T(8,128)S(1)} %collective-permute-done.7, f32[1,64,512]{2,1,0:T(8,128)S(1)} %bitcast_add_fusion.2, ...), kind=kOutput, calls=%fused_computation.2 | convolution fusion | flops 134545408 | bytes 3541248 | tf_op jit(solution)/shard_map/dot_general | solution.py:30
  107.1 1.9 %collective-permute-start.9 = (f32[2048,64]{0,1:T(8,128)S(1)}, f32[2048,64]{0,1:T(8,128)S(1)}, u32[]{:S(2)}, u32[]{:S(2)}) collective-permute-start(f32[2048,64]{0,1:T(8,128)S(1)} %fusion), channel_id=1, source_target_pairs={{0,6},{6,12},{12,18},{18,24},{24,30},{30,36},{36,42},{42,48},{48,5... | collective-permute-start | bytes 1572872 | tf_op jit(solution)/shard_map/ppermute | solution.py:11
  109.0 2.3 %fusion.20 = f32[64,2048]{1,0:T(8,128)S(1)} fusion(bf16[2048,512]{1,0:T(8,128)(2,1)} %collective-permute-done.4, bf16[3,64,512]{2,1,0:T(8,128)(2,1)S(1)} %collective-permute-done.8), kind=kOutput, calls=%fused_computation.43 | convolution fusion | flops 134217728 | bytes 2686976 | tf_op jit(solution)/shard_map/dot_general | solution.py:30
  111.4 0.8 fusion.1
  112.1 1.9 %collective-permute-start.10 = (f32[2048,64]{0,1:T(8,128)S(1)}, f32[2048,64]{0,1:T(8,128)S(1)}, u32[]{:S(2)}, u32[]{:S(2)}) collective-permute-start(f32[2048,64]{0,1:T(8,128)S(1)} %fusion.1), channel_id=1, source_target_pairs={{0,6},{6,12},{12,18},{18,24},{24,30},{30,36},{36,42},{42,48},{48,5... | collective-permute-start | bytes 1572872 | tf_op jit(solution)/shard_map/ppermute | solution.py:11
  114.1 0.8 fusion.7
  114.9 0.1 copy.9
  115.0 24.6 %collective-permute-done.9 = f32[2048,64]{0,1:T(8,128)S(1)} collective-permute-done((f32[2048,64]{0,1:T(8,128)S(1)}, f32[2048,64]{0,1:T(8,128)S(1)}, u32[]{:S(2)}, u32[]{:S(2)}) %collective-permute-start.9) | collective-permute-done | bytes 524320 | tf_op jit(solution)/shard_map/ppermute | solution.py:11
  139.6 0.1 fusion.3
  139.7 11.2 %collective-permute-done.10 = f32[2048,64]{0,1:T(8,128)S(1)} collective-permute-done((f32[2048,64]{0,1:T(8,128)S(1)}, f32[2048,64]{0,1:T(8,128)S(1)}, u32[]{:S(2)}, u32[]{:S(2)}) %collective-permute-start.10) | collective-permute-done | bytes 524320 | tf_op jit(solution)/shard_map/ppermute | solution.py:11
  150.8 0.1 fusion.2
  150.9 1.3 copy.6
  (12 shorter events, 0.1 us)
Async XLA Ops:
  0.0 22.0 %copy-start = (bf16[2048,512]{1,0:T(8,128)(2,1)S(1)}, bf16[2048,512]{1,0:T(8,128)(2,1)}, u32[]{:S(2)}) copy-start(bf16[2048,512]{1,0:T(8,128)(2,1)} %param.6) | copy-start | bytes 6291460
  0.0 72.3 %collective-permute-start.4 = (bf16[2048,512]{1,0:T(8,128)(2,1)}, bf16[2048,512]{1,0:T(8,128)(2,1)}, u32[]{:S(2)}, u32[]{:S(2)}) collective-permute-start(bf16[2048,512]{1,0:T(8,128)(2,1)} %param.6), channel_id=1, source_target_pairs={{0,6},{6,12},{12,18},{18,24},{24,30},{30,36},{36,42},{42,48},{48,5... | collective-permute-start | bytes 6291464 | tf_op jit(solution)/shard_map/ppermute | solution.py:11
  4.2 17.9 %collective-permute-start = (bf16[2048,128]{1,0:T(8,128)(2,1)}, bf16[2048,128]{1,0:T(8,128)(2,1)S(1)}, u32[]{:S(2)}, u32[]{:S(2)}) collective-permute-start(bf16[2048,128]{1,0:T(8,128)(2,1)} %param.5), channel_id=1, source_target_pairs={{0,762},{6,0},{12,6},{18,12},{24,18},{30,24},{36,30},{42,36},{48,4... | collective-permute-start | bytes 1572872 | tf_op jit(solution)/shard_map/ppermute | solution.py:11
  17.9 14.8 %copy-start.1 = (f32[256]{0:T(256)S(1)}, f32[256]{0:T(256)}, u32[]{:S(2)}) copy-start(f32[256]{0:T(256)} %param.7) | copy-start | bytes 3076
  17.9 28.9 %copy-start.3 = (f32[64]{0:T(128)S(1)}, f32[64]{0:T(128)}, u32[]{:S(2)}) copy-start(f32[64]{0:T(128)} %param.8) | copy-start | bytes 772
  17.9 29.2 %copy-start.2 = (f32[256]{0:T(256)S(1)}, f32[256]{0:T(256)}, u32[]{:S(2)}) copy-start(f32[256]{0:T(256)} %param.9) | copy-start | bytes 3076
  23.2 10.7 %collective-permute-start.1 = (f32[2,64,512]{2,1,0:T(8,128)}, f32[2,64,512]{2,1,0:T(8,128)S(1)}, u32[]{:S(2)}, u32[]{:S(2)}) collective-permute-start(f32[2,64,512]{2,1,0:T(8,128)} %fusion.4), channel_id=1, source_target_pairs={{0,1},{1,0},{2,3},{3,2},{4,5},{5,4},{6,7},{7,6},{8,9},{9,8},{10,11... | collective-permute-start | bytes 786440 | tf_op jit(solution)/shard_map/ppermute | solution.py:55
  34.7 27.9 %collective-permute-start.3 = (f32[2,64,512]{2,1,0:T(8,128)}, f32[2,64,512]{2,1,0:T(8,128)}, u32[]{:S(2)}, u32[]{:S(2)}) collective-permute-start(f32[2,64,512]{2,1,0:T(8,128)} %fusion.6), channel_id=1, source_target_pairs={{0,4},{1,5},{2,0},{3,1},{4,2},{5,3},{6,10},{7,11},{8,6},{9,7},{10,... | collective-permute-start | bytes 786440 | tf_op jit(solution)/shard_map/ppermute | solution.py:58
  44.8 26.4 %collective-permute-start.2 = (f32[2,64,512]{2,1,0:T(8,128)}, f32[2,64,512]{2,1,0:T(8,128)}, u32[]{:S(2)}, u32[]{:S(2)}) collective-permute-start(f32[2,64,512]{2,1,0:T(8,128)} %fusion.6), channel_id=1, source_target_pairs={{0,2},{1,3},{2,4},{3,5},{4,0},{5,1},{6,8},{7,9},{8,10},{9,11},{10,... | collective-permute-start | bytes 786440 | tf_op jit(solution)/shard_map/ppermute | solution.py:58
  74.5 3.5 %collective-permute-start.5 = (f32[1,64,512]{2,1,0:T(8,128)S(1)}, f32[1,64,512]{2,1,0:T(8,128)S(1)}, u32[]{:S(2)}, u32[]{:S(2)}) collective-permute-start(f32[1,64,512]{2,1,0:T(8,128)S(1)} %dynamic-slice_bitcast_fusion), channel_id=1, source_target_pairs={{0,1},{1,0},{2,3},{3,2},{4,5},{5,4},{6,7},{7,6},{8,9},{9,8},{10,11... | collective-permute-start | bytes 393224 | tf_op jit(solution)/shard_map/ppermute | solution.py:55
  78.0 14.5 %collective-permute-start.7 = (f32[1,64,512]{2,1,0:T(8,128)S(1)}, f32[1,64,512]{2,1,0:T(8,128)S(1)}, u32[]{:S(2)}, u32[]{:S(2)}) collective-permute-start(f32[1,64,512]{2,1,0:T(8,128)S(1)} %bitcast_add_fusion.2), channel_id=1, source_target_pairs={{0,4},{1,5},{2,0},{3,1},{4,2},{5,3},{6,10},{7,11},{8,6},{9,7},{10,... | collective-permute-start | bytes 393224 | tf_op jit(solution)/shard_map/ppermute | solution.py:58
  83.9 18.2 %collective-permute-start.6 = (f32[1,64,512]{2,1,0:T(8,128)S(1)}, f32[1,64,512]{2,1,0:T(8,128)S(1)}, u32[]{:S(2)}, u32[]{:S(2)}) collective-permute-start(f32[1,64,512]{2,1,0:T(8,128)S(1)} %bitcast_add_fusion.2), channel_id=1, source_target_pairs={{0,2},{1,3},{2,4},{3,5},{4,0},{5,1},{6,8},{7,9},{8,10},{9,11},{10,... | collective-permute-start | bytes 393224 | tf_op jit(solution)/shard_map/ppermute | solution.py:58
  102.3 6.7 %collective-permute-start.8 = (bf16[3,64,512]{2,1,0:T(8,128)(2,1)S(1)}, bf16[3,64,512]{2,1,0:T(8,128)(2,1)S(1)}, u32[]{:S(2)}, u32[]{:S(2)}) collective-permute-start(bf16[3,64,512]{2,1,0:T(8,128)(2,1)S(1)} %pad_maximum_fusion), channel_id=1, source_target_pairs={{0,1},{1,0},{2,3},{3,2},{4,5},{5,4},{6,7},{7,6},{8,9},{9,8},{10,11... | collective-permute-start | bytes 589832 | tf_op jit(solution)/shard_map/ppermute | solution.py:77
  107.1 32.5 %collective-permute-start.9 = (f32[2048,64]{0,1:T(8,128)S(1)}, f32[2048,64]{0,1:T(8,128)S(1)}, u32[]{:S(2)}, u32[]{:S(2)}) collective-permute-start(f32[2048,64]{0,1:T(8,128)S(1)} %fusion), channel_id=1, source_target_pairs={{0,6},{6,12},{12,18},{18,24},{24,30},{30,36},{36,42},{42,48},{48,5... | collective-permute-start | bytes 1572872 | tf_op jit(solution)/shard_map/ppermute | solution.py:11
  112.1 38.7 %collective-permute-start.10 = (f32[2048,64]{0,1:T(8,128)S(1)}, f32[2048,64]{0,1:T(8,128)S(1)}, u32[]{:S(2)}, u32[]{:S(2)}) collective-permute-start(f32[2048,64]{0,1:T(8,128)S(1)} %fusion.1), channel_id=1, source_target_pairs={{0,6},{6,12},{12,18},{18,24},{24,30},{30,36},{36,42},{42,48},{48,5... | collective-permute-start | bytes 1572872 | tf_op jit(solution)/shard_map/ppermute | solution.py:11
